TPU v7x, 512 devices: a whole 4x4x16 slice. The times are simulated.
512 devices in a mesh: dp: 4 (over z_lo), ctx: 128 (over x, z_hi, y, core).
Axes of the slice: x: 4, y: 4, z: 16 (z_hi: 4, z_lo: 4; z = z_hi * 4 + z_lo), core: 2. Of those that a mesh axis runs over, the one named last changes fastest.
Arguments:
- query_proj: bfloat16 [2048, 65536], P(None, ('dp', 'ctx')), may hold values from -6 to 6
- key_proj: bfloat16 [2048, 65536], P(None, ('dp', 'ctx')), may hold values from -6 to 6
- value_proj: bfloat16 [2048, 65536], P(None, ('dp', 'ctx')), may hold values from -6 to 6
- grad_out: bfloat16 [2048, 65536], P(None, ('dp', 'ctx')), may hold values from -6 to 6
- filters: bfloat16 [128, 16384], P('ctx'), may hold values from -0.046875 to 0.046875
- short_taps: float32 [3, 2048], replicated, may hold values from -3 to 3
Outputs:
- grad_query: bfloat16 [2048, 65536], P(None, ('dp', 'ctx'))
- grad_key: bfloat16 [2048, 65536], P(None, ('dp', 'ctx'))
- grad_value: bfloat16 [2048, 65536], P(None, ('dp', 'ctx'))
- grad_filters: float32 [128, 16384], P('ctx', 'dp')
All inputs are finite; a program needn't handle non-finite values.
Results may differ from a plain program's by a relative error of at most 0.0076.
Values may be sent and summed in bfloat16 or wider, within the bound.
No kernel may reach another device: no remote copies, remote signals or barrier semaphores. Data moves between devices by JAX's collectives and lax.ppermute only.
A program may use at most 64 MiB of HBM per device.

v0:
```python
import math

import jax
import jax.numpy as jnp
from jax import lax
from jax.sharding import PartitionSpec as P

highest = lax.Precision.HIGH
triple = lax.Precision.HIGH


def shifted(array, axis, by):
    size = lax.axis_size(axis)
    pairs = [(i, i + by) for i in range(size) if 0 <= i + by < size]
    return lax.ppermute(array, axis, pairs)


def ring_scatter_sum(terms, axis):
    count = lax.axis_size(axis)
    width = terms.shape[1] // count
    me = lax.axis_index(axis)
    total = lax.dynamic_slice_in_dim(terms, me * width, width, axis=1)
    for step in range(1, count):
        target = (me + step) % count
        piece = lax.dynamic_slice_in_dim(terms, target * width, width, axis=1)
        pairs = [(i, (i + step) % count) for i in range(count)]
        total = total + lax.ppermute(piece, axis, pairs)
    return total


def angle_table(first_count, second_count, modulus):
    first_index = jnp.arange(first_count, dtype=jnp.int32)
    second_index = jnp.arange(second_count, dtype=jnp.int32)
    product = first_index[:, None] * second_index[None, :] % modulus
    angle = product.astype(jnp.float32) * (2.0 * math.pi / modulus)
    return (jnp.cos(angle), jnp.sin(angle))


def rotation_table(cos_part, sin_part):
    upper = jnp.concatenate([cos_part, -sin_part], axis=1)
    lower = jnp.concatenate([sin_part, cos_part], axis=1)
    return jnp.concatenate([upper, lower], axis=0)


def fourier_tables(length):
    inner = min(128, length)
    outer = 2 * length // inner
    outer_cos, outer_sin = angle_table(outer // 2, outer, outer)
    twist_cos, twist_sin = angle_table(outer, inner, 2 * length)
    inner_cos, inner_sin = angle_table(inner, inner, inner)
    fwd_outer = rotation_table(outer_cos, outer_sin)
    fwd_inner = rotation_table(inner_cos, inner_sin)
    inv_inner = rotation_table(inner_cos, -inner_sin)
    inv_outer = rotation_table(outer_cos.T, -outer_sin.T)
    return (fwd_outer, fwd_inner, inv_inner, inv_outer, twist_cos, twist_sin)


def forward_spectrum(real_rows, imag_rows, tables):
    fwd_outer, fwd_inner, inv_inner, inv_outer, twist_cos, twist_sin = tables
    row_count = real_rows.shape[0]
    outer = twist_cos.shape[0]
    inner = twist_cos.shape[1]
    half_outer = outer // 2
    real_blocks = real_rows.reshape(row_count, half_outer, inner)
    if imag_rows is None:
        blocks = real_blocks
        table = fwd_outer[:half_outer]
    else:
        blocks = jnp.concatenate(
            [real_blocks, imag_rows.reshape(row_count, half_outer, inner)], axis=1
        )
        table = fwd_outer
    first = jnp.einsum("man,ak->mkn", blocks, table, precision=triple)
    first_real = first[:, :outer]
    first_imag = first[:, outer:]
    turned = jnp.concatenate(
        [
            first_real * twist_cos + first_imag * twist_sin,
            first_imag * twist_cos - first_real * twist_sin,
        ],
        axis=2,
    )
    return jnp.einsum("mkn,nj->mkj", turned, fwd_inner, precision=highest)


def inverse_spectrum(spectrum, tables, both_parts):
    fwd_outer, fwd_inner, inv_inner, inv_outer, twist_cos, twist_sin = tables
    row_count = spectrum.shape[0]
    outer = twist_cos.shape[0]
    inner = twist_cos.shape[1]
    half_outer = outer // 2
    length = half_outer * inner
    first = jnp.einsum("mkj,jn->mkn", spectrum, inv_inner, precision=highest)
    first_real = first[..., :inner]
    first_imag = first[..., inner:]
    turned = jnp.concatenate(
        [
            first_real * twist_cos - first_imag * twist_sin,
            first_imag * twist_cos + first_real * twist_sin,
        ],
        axis=1,
    )
    table = inv_outer if both_parts else inv_outer[:, :half_outer]
    values = jnp.einsum("mkn,ka->man", turned, table, precision=highest) * (1.0 / (2.0 * length))
    if both_parts:
        return (
            values[:, :half_outer].reshape(row_count, length),
            values[:, half_outer:].reshape(row_count, length),
        )
    return values.reshape(row_count, length)


def taps_forward(current, earlier, short_taps):
    columns = current.shape[1]
    joined = jnp.concatenate([earlier, current], axis=1)
    return (
        short_taps[0][:, None] * current
        + short_taps[1][:, None] * joined[:, 1 : columns + 1]
        + short_taps[2][:, None] * joined[:, 0:columns]
    )


def taps_backward(current, following, short_taps):
    columns = current.shape[1]
    joined = jnp.concatenate([current, following], axis=1)
    return (
        short_taps[0][:, None] * current
        + short_taps[1][:, None] * joined[:, 1 : columns + 1]
        + short_taps[2][:, None] * joined[:, 2 : columns + 2]
    )


def per_device(query_proj, key_proj, value_proj, grad_out, filters, short_taps):
    all_chans, tok_cols = query_proj.shape
    ctx_count = lax.axis_size("ctx")
    seq_len = tok_cols * ctx_count
    seq_count = ctx_count * tok_cols // seq_len
    groups_dev = filters.shape[0]
    chan_dev = all_chans // ctx_count
    group_size = chan_dev // groups_dev
    group_rows = group_size * seq_count
    pair_rows = group_rows // 2
    position = lax.axis_index("ctx") * tok_cols
    keep_prev = jnp.where(position % seq_len == 0, 0.0, 1.0).astype(jnp.float32)
    keep_next = jnp.where((position + tok_cols) % seq_len == 0, 0.0, 1.0).astype(jnp.float32)
    tables = fourier_tables(seq_len)
    inner = tables[4].shape[1]
    tails = jnp.concatenate([query_proj[:, -2:], key_proj[:, -2:], value_proj[:, -2:]], axis=1)
    tails = shifted(tails, "ctx", 1)
    earlier = (tails[:, 0:2], tails[:, 2:4], tails[:, 4:6])
    query_conv = taps_forward(
        query_proj.astype(jnp.float32), earlier[0].astype(jnp.float32) * keep_prev, short_taps
    ).astype(jnp.bfloat16)
    key_conv = taps_forward(
        key_proj.astype(jnp.float32), earlier[1].astype(jnp.float32) * keep_prev, short_taps
    ).astype(jnp.bfloat16)
    value_conv = taps_forward(
        value_proj.astype(jnp.float32), earlier[2].astype(jnp.float32) * keep_prev, short_taps
    ).astype(jnp.bfloat16)
    query_conv, key_conv, value_conv = lax.optimization_barrier((query_conv, key_conv, value_conv))
    gated_tok = (key_conv.astype(jnp.float32) * value_conv.astype(jnp.float32)).astype(jnp.bfloat16)
    filter_spec = forward_spectrum(filters.astype(jnp.float32), None, tables)
    filter_real = filter_spec[:, None, :, :inner]
    filter_imag = filter_spec[:, None, :, inner:]

    def to_rows(source):
        return source.reshape(groups_dev, group_rows, seq_len)

    def to_chan(source):
        return source.reshape(chan_dev, ctx_count * tok_cols)

    def spectrum_of(rows_three):
        paired = rows_three.reshape(groups_dev, 2, pair_rows, seq_len).astype(jnp.float32)
        spec = forward_spectrum(
            paired[:, 0].reshape(-1, seq_len), paired[:, 1].reshape(-1, seq_len), tables
        )
        spec = spec.reshape((groups_dev, pair_rows) + spec.shape[1:])
        return (spec[..., :inner], spec[..., inner:])

    def back_to_rows(spec_real, spec_imag):
        joined = jnp.concatenate([spec_real, spec_imag], axis=-1)
        joined = joined.reshape((-1,) + joined.shape[2:])
        first_rows, second_rows = inverse_spectrum(joined, tables, True)
        first_rows = first_rows.reshape(groups_dev, pair_rows, seq_len)
        second_rows = second_rows.reshape(groups_dev, pair_rows, seq_len)
        return jnp.concatenate([first_rows, second_rows], axis=1)

    cotangent = grad_out.astype(jnp.float32)
    grad_mixed_tok = (cotangent * query_conv.astype(jnp.float32)).astype(jnp.bfloat16)
    outgoing = jnp.concatenate(
        [
            gated_tok.reshape(ctx_count, chan_dev, tok_cols),
            grad_mixed_tok.reshape(ctx_count, chan_dev, tok_cols),
        ],
        axis=1,
    ).reshape(2 * all_chans, tok_cols)
    incoming = lax.all_to_all(outgoing, "ctx", split_axis=0, concat_axis=1, tiled=True)
    gated_rows = to_rows(incoming[:chan_dev])
    grad_mixed = to_rows(incoming[chan_dev:])
    gated_spec = spectrum_of(gated_rows)
    prod_real = gated_spec[0] * filter_real - gated_spec[1] * filter_imag
    prod_imag = gated_spec[0] * filter_imag + gated_spec[1] * filter_real
    mixed_rows = back_to_rows(prod_real, prod_imag).astype(jnp.bfloat16)
    grad_spec = spectrum_of(grad_mixed)
    prod_real = grad_spec[0] * filter_real + grad_spec[1] * filter_imag
    prod_imag = grad_spec[1] * filter_real - grad_spec[0] * filter_imag
    grad_gated = back_to_rows(prod_real, prod_imag).astype(jnp.bfloat16)
    returning = jnp.concatenate([to_chan(mixed_rows), to_chan(grad_gated)], axis=0)
    returned = lax.all_to_all(returning, "ctx", split_axis=1, concat_axis=0, tiled=True)
    returned = returned.reshape(ctx_count, 2 * chan_dev, tok_cols)
    mixed_tok = returned[:, :chan_dev].reshape(all_chans, tok_cols)
    grad_gated_tok = returned[:, chan_dev:].reshape(all_chans, tok_cols)
    grad_qconv = (cotangent * mixed_tok.astype(jnp.float32)).astype(jnp.bfloat16)
    cross_real = jnp.sum(grad_spec[0] * gated_spec[0] + grad_spec[1] * gated_spec[1], axis=1)
    cross_imag = jnp.sum(grad_spec[1] * gated_spec[0] - grad_spec[0] * gated_spec[1], axis=1)
    filter_terms = inverse_spectrum(
        jnp.concatenate([cross_real, cross_imag], axis=-1), tables, False
    )
    scale = 1.0 / math.sqrt(float(lax.axis_size("dp") * seq_count * group_size * seq_len))
    grad_filters = ring_scatter_sum(filter_terms, "dp") * scale
    grad_kconv = (grad_gated_tok.astype(jnp.float32) * value_conv.astype(jnp.float32)).astype(
        jnp.bfloat16
    )
    grad_vconv = (grad_gated_tok.astype(jnp.float32) * key_conv.astype(jnp.float32)).astype(
        jnp.bfloat16
    )
    grad_qconv, grad_kconv, grad_vconv = lax.optimization_barrier(
        (grad_qconv, grad_kconv, grad_vconv)
    )
    heads = jnp.concatenate([grad_qconv[:, :2], grad_kconv[:, :2], grad_vconv[:, :2]], axis=1)
    heads = shifted(heads, "ctx", -1)
    following = (heads[:, 0:2], heads[:, 2:4], heads[:, 4:6])
    grad_query = taps_backward(
        grad_qconv.astype(jnp.float32), following[0].astype(jnp.float32) * keep_next, short_taps
    ).astype(jnp.bfloat16)
    grad_key = taps_backward(
        grad_kconv.astype(jnp.float32), following[1].astype(jnp.float32) * keep_next, short_taps
    ).astype(jnp.bfloat16)
    grad_value = taps_backward(
        grad_vconv.astype(jnp.float32), following[2].astype(jnp.float32) * keep_next, short_taps
    ).astype(jnp.bfloat16)
    return (grad_query, grad_key, grad_value, grad_filters)


def solution(mesh):
    in_specs = (
        P(None, ("dp", "ctx")),
        P(None, ("dp", "ctx")),
        P(None, ("dp", "ctx")),
        P(None, ("dp", "ctx")),
        P("ctx", None),
        P(),
    )
    out_specs = (
        P(None, ("dp", "ctx")),
        P(None, ("dp", "ctx")),
        P(None, ("dp", "ctx")),
        P("ctx", "dp"),
    )
    return jax.shard_map(
        per_device, mesh=mesh, in_specs=in_specs, out_specs=out_specs, check_vma=False
    )
```

profile of v0, /device:TPU:25, one launch (start us, length us, event | category | flops | bytes accessed | tf_op | source)
XLA Modules:
  0.0 235.0 jit_solution(12373815206659188854)
XLA Ops:
  0.7 1.3 slice.197
  2.2 1.3 slice.198
  4.2 1.1 copy.81
  5.2 9.0 %collective-permute-start = (bf16[2048,6]{1,0:T(8,128)(2,1)}, bf16[2048,6]{1,0:T(8,128)(2,1)S(1)}, u32[]{:S(2)}, u32[]{:S(2)}) collective-permute-start(bf16[2048,6]{1,0:T(8,128)(2,1)} %copy.81), channel_id=1, source_target_pairs={{0,1},{1,2},{2,3},{3,4},{4,5},{5,6},{6,7},{7,8},{8,9},{9,10},{10,1... | collective-permute-start | bytes 73736 | tf_op jit(solution)/shard_map/ppermute | solution.py:15
  14.4 1.1 convert_element_type.239
  15.5 2.1 convert_element_type.242
  17.6 4.8 %collective-permute-done = bf16[2048,6]{1,0:T(8,128)(2,1)S(1)} collective-permute-done((bf16[2048,6]{1,0:T(8,128)(2,1)}, bf16[2048,6]{1,0:T(8,128)(2,1)S(1)}, u32[]{:S(2)}, u32[]{:S(2)}) %collective-permute-start) | collective-permute-done | bytes 24608 | tf_op jit(solution)/shard_map/ppermute | solution.py:15
  22.8 3.5 %fusion.70 = (bf16[2048,128]{1,0:T(8,128)(2,1)S(1)}, bf16[2048,128]{1,0:T(8,128)(2,1)S(1)}, bf16[2048,128]{1,0:T(8,128)(2,1)S(1)}) fusion(f32[2048,2]{1,0:T(8,128)S(1)} %get-tuple-element.51, f32[2048,128]{1,0:T(8,128)S(1)} %copy-done.2, f32[2048]{0:T(1024)S(1)} %bitcast.135, f32[2048]{0:T(1024)S(1)} %bitcast.137, f32[2048]{0:T(1024)S(1)} %bitcast.133, ...), kind=kLoop, calls=%fused_computation.77 | loop fusion | flops 6291456 | bytes 4792320 | tf_op jit(solution)/shard_map/convert_element_type | solution.py:159
  26.7 1.1 pad_maximum_fusion.6
  27.8 35.8 %all-to-all-start = ((bf16[128,32,128]{2,1,0:T(8,128)(2,1)}), bf16[128,32,128]{2,1,0:T(8,128)(2,1)S(1)}, u32[]{:S(2)}, u32[]{:S(2)}) async-start(bf16[128,32,128]{2,1,0:T(8,128)(2,1)} %pad_maximum_fusion.6), calls=%async_computation | async-start | bytes 2097152 | tf_op jit(solution)/shard_map/all_to_all | solution.py:197
  64.8 1.2 fusion.143
  68.8 1.1 fusion.150
  69.9 1.2 fusion.145
  71.2 1.2 fusion.147
  72.4 40.3 %all-to-all-done = bf16[128,32,128]{2,1,0:T(8,128)(2,1)S(1)} async-done(((bf16[128,32,128]{2,1,0:T(8,128)(2,1)}), bf16[128,32,128]{2,1,0:T(8,128)(2,1)S(1)}, u32[]{:S(2)}, u32[]{:S(2)}) %all-to-all-start) | async-done | bytes 1048608 | tf_op jit(solution)/shard_map/all_to_all | solution.py:197
  112.9 1.3 copy.93
  114.2 1.4 reshape.232
  118.7 1.3 copy.82
  120.1 1.4 reshape.231
  123.5 1.2 copy.130
  129.7 1.3 fusion.22
  135.0 1.1 fusion.43
  136.1 1.1 fusion.40
  137.4 1.7 copy.102
  139.0 11.4 %all-to-all-start.1 = ((bf16[32,128,128]{2,0,1:T(8,128)(2,1)}), bf16[32,128,128]{2,0,1:T(8,128)(2,1)S(1)}, u32[]{:S(2)}, u32[]{:S(2)}) async-start(bf16[32,128,128]{2,0,1:T(8,128)(2,1)} %copy.102), calls=%async_computation.1 | async-start | bytes 2097152 | tf_op jit(solution)/shard_map/all_to_all | solution.py:209
  151.8 1.9 collective-permute-start.2
  153.7 3.0 %collective-permute-start.3 = (f32[1,4096]{1,0:T(1,128)S(1)}, f32[1,4096]{1,0:T(1,128)S(1)}, u32[]{:S(2)}, u32[]{:S(2)}) collective-permute-start(f32[1,4096]{1,0:T(1,128)S(1)} %get-tuple-element.66), channel_id=1, source_target_pairs={{0,256},{128,384},{256,0},{384,128},{1,257},{129,385},{257,1},{385... | collective-permute-start | bytes 49160 | tf_op jit(solution)/shard_map/ppermute | solution.py:27
  156.7 4.0 %collective-permute-start.4 = (f32[1,4096]{1,0:T(1,128)S(1)}, f32[1,4096]{1,0:T(1,128)S(1)}, u32[]{:S(2)}, u32[]{:S(2)}) collective-permute-start(f32[1,4096]{1,0:T(1,128)S(1)} %get-tuple-element.65), channel_id=1, source_target_pairs={{0,384},{128,0},{256,128},{384,256},{1,385},{129,1},{257,129},{385... | collective-permute-start | bytes 49160 | tf_op jit(solution)/shard_map/ppermute | solution.py:27
  160.8 42.4 %all-to-all-done.1 = bf16[32,128,128]{2,0,1:T(8,128)(2,1)S(1)} async-done(((bf16[32,128,128]{2,0,1:T(8,128)(2,1)}), bf16[32,128,128]{2,0,1:T(8,128)(2,1)S(1)}, u32[]{:S(2)}, u32[]{:S(2)}) %all-to-all-start.1) | async-done | bytes 1048608 | tf_op jit(solution)/shard_map/all_to_all | solution.py:209
  204.9 2.6 %collective-permute-start.1 = (bf16[2048,6]{1,0:T(8,128)(2,1)S(1)}, bf16[2048,6]{1,0:T(8,128)(2,1)S(1)}, u32[]{:S(2)}, u32[]{:S(2)}) collective-permute-start(bf16[2048,6]{1,0:T(8,128)(2,1)S(1)} %pad_maximum_fusion.10), channel_id=1, source_target_pairs={{1,0},{2,1},{3,2},{4,3},{5,4},{6,5},{7,6},{8,7},{9,8},{10,9},{11,1... | collective-permute-start | bytes 73736 | tf_op jit(solution)/shard_map/ppermute | solution.py:15
  208.4 21.1 %collective-permute-done.1 = bf16[2048,6]{1,0:T(8,128)(2,1)S(1)} collective-permute-done((bf16[2048,6]{1,0:T(8,128)(2,1)S(1)}, bf16[2048,6]{1,0:T(8,128)(2,1)S(1)}, u32[]{:S(2)}, u32[]{:S(2)}) %collective-permute-start.1) | collective-permute-done | bytes 24608 | tf_op jit(solution)/shard_map/ppermute | solution.py:15
  229.9 5.1 %fusion.55 = (bf16[2048,128]{1,0:T(8,128)(2,1)}, bf16[2048,128]{1,0:T(8,128)(2,1)}, bf16[2048,128]{1,0:T(8,128)(2,1)}) fusion(f32[2048,128]{1,0:T(8,128)S(1)} %convert_element_type.270, f32[2048,2]{1,0:T(8,128)S(1)} %get-tuple-element.42, f32[2048]{0:T(1024)S(1)} %bitcast.136, f32[2048]{0:T(1024)S(1)} %bitcast.138, f32[2048]{0:T(1024)S(1)} %bitcast.134, ...), kind=kLoop, calls=%fused_computation.62 | loop fusion | flops 6291456 | bytes 4792320 | tf_op jit(solution)/shard_map/convert_element_type | solution.py:241
  (105 shorter events, 24.0 us)
Async XLA Ops:
  0.6 63.0 %copy-start = (bf16[1,16384]{1,0:T(2,128)(2,1)S(1)}, bf16[1,16384]{1,0:T(2,128)(2,1)}, u32[]{:S(2)}) copy-start(bf16[1,16384]{1,0:T(2,128)(2,1)} %param.10) | copy-start | bytes 98308
  0.6 3.0 %copy-start.6 = (bf16[2048,128]{1,0:T(8,128)(2,1)S(1)}, bf16[2048,128]{1,0:T(8,128)(2,1)}, u32[]{:S(2)}) copy-start(bf16[2048,128]{1,0:T(8,128)(2,1)} %param.8) | copy-start | bytes 1572868
  2.0 12.3 %copy-start.22 = (f32[3,2048]{1,0:T(4,128)S(1)}, f32[3,2048]{1,0:T(4,128)}, u32[]{:S(2)}) copy-start(f32[3,2048]{1,0:T(4,128)} %param.11) | copy-start | bytes 73732
  2.0 12.3 %copy-start.5 = (bf16[2048,128]{1,0:T(8,128)(2,1)S(1)}, bf16[2048,128]{1,0:T(8,128)(2,1)}, u32[]{:S(2)}) copy-start(bf16[2048,128]{1,0:T(8,128)(2,1)} %param.6) | copy-start | bytes 1572868
  5.2 17.2 %collective-permute-start = (bf16[2048,6]{1,0:T(8,128)(2,1)}, bf16[2048,6]{1,0:T(8,128)(2,1)S(1)}, u32[]{:S(2)}, u32[]{:S(2)}) collective-permute-start(bf16[2048,6]{1,0:T(8,128)(2,1)} %copy.81), channel_id=1, source_target_pairs={{0,1},{1,2},{2,3},{3,4},{4,5},{5,6},{6,7},{7,8},{8,9},{9,10},{10,1... | collective-permute-start | bytes 73736 | tf_op jit(solution)/shard_map/ppermute | solution.py:15
  17.6 5.2 %copy-start.2 = (f32[2048,128]{1,0:T(8,128)S(1)}, f32[2048,128]{1,0:T(8,128)}, u32[]{:S(2)}) copy-start(f32[2048,128]{1,0:T(8,128)} %convert_element_type.242) | copy-start | bytes 3145732
  22.8 3.6 %copy-start.7 = (bf16[2048,128]{1,0:T(8,128)(2,1)S(1)}, bf16[2048,128]{1,0:T(8,128)(2,1)}, u32[]{:S(2)}) copy-start(bf16[2048,128]{1,0:T(8,128)(2,1)} %param.9) | copy-start | bytes 1572868
  27.8 85.0 %all-to-all-start = ((bf16[128,32,128]{2,1,0:T(8,128)(2,1)}), bf16[128,32,128]{2,1,0:T(8,128)(2,1)S(1)}, u32[]{:S(2)}, u32[]{:S(2)}) async-start(bf16[128,32,128]{2,1,0:T(8,128)(2,1)} %pad_maximum_fusion.6), calls=%async_computation | async-start | bytes 2097152 | tf_op jit(solution)/shard_map/all_to_all | solution.py:197
  66.0 46.7 %copy-start.3 = (f32[128,256]{1,0:T(8,128)}, f32[128,256]{1,0:T(8,128)S(1)}, u32[]{:S(2)}) copy-start(f32[128,256]{1,0:T(8,128)S(1)} %get-tuple-element.79) | copy-start | bytes 393220
  116.5 1.1 copy-start.13
  122.4 3.3 %copy-start.9 = (f32[8,128,128]{1,2,0:T(8,128)S(1)}, f32[8,128,128]{1,2,0:T(8,128)}, u32[]{:S(2)}) copy-start(f32[8,128,128]{1,2,0:T(8,128)} %copy.94) | copy-start | bytes 1572868
  122.4 3.3 %copy-start.10 = (f32[8,128,128]{1,2,0:T(8,128)S(1)}, f32[8,128,128]{1,2,0:T(8,128)}, u32[]{:S(2)}) copy-start(f32[8,128,128]{1,2,0:T(8,128)} %copy.95) | copy-start | bytes 1572868
  123.5 2.3 copy-start.4
  123.5 2.3 copy-start.16
  125.7 1.0 copy-start.11
  125.7 1.2 copy-start.12
  127.0 1.0 copy-start.14
  127.0 1.0 copy-start.15
  129.7 1.3 copy-start.17
  129.7 1.3 copy-start.18
  133.9 0.9 copy-start.19
  134.0 1.0 copy-start.20
  134.0 1.0 copy-start.21
  139.0 64.1 %all-to-all-start.1 = ((bf16[32,128,128]{2,0,1:T(8,128)(2,1)}), bf16[32,128,128]{2,0,1:T(8,128)(2,1)S(1)}, u32[]{:S(2)}, u32[]{:S(2)}) async-start(bf16[32,128,128]{2,0,1:T(8,128)(2,1)} %copy.102), calls=%async_computation.1 | async-start | bytes 2097152 | tf_op jit(solution)/shard_map/all_to_all | solution.py:209
  151.8 55.7 %collective-permute-start.2 = (f32[1,4096]{1,0:T(1,128)S(1)}, f32[1,4096]{1,0:T(1,128)S(1)}, u32[]{:S(2)}, u32[]{:S(2)}) collective-permute-start(f32[1,4096]{1,0:T(1,128)S(1)} %get-tuple-element.64), channel_id=1, source_target_pairs={{0,128},{128,256},{256,384},{384,0},{1,129},{129,257},{257,385},{3... | collective-permute-start | bytes 49160 | tf_op jit(solution)/shard_map/ppermute | solution.py:27
  153.7 53.8 %collective-permute-start.3 = (f32[1,4096]{1,0:T(1,128)S(1)}, f32[1,4096]{1,0:T(1,128)S(1)}, u32[]{:S(2)}, u32[]{:S(2)}) collective-permute-start(f32[1,4096]{1,0:T(1,128)S(1)} %get-tuple-element.66), channel_id=1, source_target_pairs={{0,256},{128,384},{256,0},{384,128},{1,257},{129,385},{257,1},{385... | collective-permute-start | bytes 49160 | tf_op jit(solution)/shard_map/ppermute | solution.py:27
  156.7 50.8 %collective-permute-start.4 = (f32[1,4096]{1,0:T(1,128)S(1)}, f32[1,4096]{1,0:T(1,128)S(1)}, u32[]{:S(2)}, u32[]{:S(2)}) collective-permute-start(f32[1,4096]{1,0:T(1,128)S(1)} %get-tuple-element.65), channel_id=1, source_target_pairs={{0,384},{128,0},{256,128},{384,256},{1,385},{129,1},{257,129},{385... | collective-permute-start | bytes 49160 | tf_op jit(solution)/shard_map/ppermute | solution.py:27
  203.2 1.0 copy-start.8
  204.9 24.6 %collective-permute-start.1 = (bf16[2048,6]{1,0:T(8,128)(2,1)S(1)}, bf16[2048,6]{1,0:T(8,128)(2,1)S(1)}, u32[]{:S(2)}, u32[]{:S(2)}) collective-permute-start(bf16[2048,6]{1,0:T(8,128)(2,1)S(1)} %pad_maximum_fusion.10), channel_id=1, source_target_pairs={{1,0},{2,1},{3,2},{4,3},{5,4},{6,5},{7,6},{8,7},{9,8},{10,9},{11,1... | collective-permute-start | bytes 73736 | tf_op jit(solution)/shard_map/ppermute | solution.py:15
  229.9 5.2 %copy-start.1 = (bf16[1,16384]{1,0:T(2,128)(2,1)S(1)}, bf16[1,16384]{1,0:T(2,128)(2,1)}, u32[]{:S(2)}) copy-start(bf16[1,16384]{1,0:T(2,128)(2,1)} %param.10) | copy-start | bytes 98308
where the time goes:
time: 236 us; the launch traced here: 235 us
  waiting for transfers between devices  109 us (46%)
  starting transfers between devices  67.9 us (29%)
  other arithmetic  25.7 us (11%)
  local copies, waits for them, and re-layouts  21.9 us (9%)
  matrix products  9.67 us (4%)
    all_to_all x1, waiting for transfers between devices, per_device(): lax.all_to_all(returning, 'ctx', split_axis=1, concat_axis=0, tiled=True)  42.4 us
    all_to_all x1, waiting for transfers between devices, per_device(): lax.all_to_all(outgoing, 'ctx', split_axis=0, concat_axis=1, tiled=True)  40.3 us
    all_to_all x1, starting transfers between devices, per_device(): lax.all_to_all(outgoing, 'ctx', split_axis=0, concat_axis=1, tiled=True)  35.8 us
    ppermute x2, waiting for transfers between devices, shifted(): return lax.ppermute(array, axis, pairs)  25.9 us
    ppermute x2, starting transfers between devices, shifted(): return lax.ppermute(array, axis, pairs)  11.6 us
    all_to_all x1, starting transfers between devices, per_device(): lax.all_to_all(returning, 'ctx', split_axis=1, concat_axis=0, tiled=True)  11.4 us
    ppermute x3, starting transfers between devices, ring_scatter_sum(): total = total + lax.ppermute(piece, axis, pairs)  9 us
    convert_element_type x4, local copies, waits for them, and re-layouts, spectrum_of(): rows_three.reshape(groups_dev, 2, pair_rows, seq_len).astype(jnp.float32)  5.49 us
  transfers between devices with their start and end apart: 7, of which 4 were waited for; matrix products, arithmetic and copies ran while one was open for 6% of the time, Pallas kernels for 0%

commit v1 on v0

--- a/solution.py
+++ b/solution.py
@@ -1,8 +1,11 @@
+import functools
 import math
 
 import jax
 import jax.numpy as jnp
 from jax import lax
+from jax.experimental import pallas as pl
+from jax.experimental.pallas import tpu as pltpu
 from jax.sharding import PartitionSpec as P
 
 highest = lax.Precision.HIGH
@@ -110,6 +113,57 @@
     return values.reshape(row_count, length)
 
 
+BLOCK_ROWS = 256
+
+
+def front_kernel(chan_dev, q_ref, k_ref, v_ref, g_ref, halo_ref, taps_ref, qc_ref, kc_ref, vc_ref, out_ref):
+    rows, cols = q_ref.shape
+    lane = lax.broadcasted_iota(jnp.int32, (rows, cols), 1)
+    halo = halo_ref[...].astype(jnp.float32)
+    taps = taps_ref[...]
+    first, second, third = taps[:, 0:1], taps[:, 1:2], taps[:, 2:3]
+
+    def conv(x_ref, slot):
+        x = x_ref[...].astype(jnp.float32)
+        older = halo[:, 2 * slot : 2 * slot + 1]
+        newer = halo[:, 2 * slot + 1 : 2 * slot + 2]
+        back_one = jnp.where(lane == 0, newer, pltpu.roll(x, 1, 1))
+        rolled = pltpu.roll(x, 2, 1)
+        back_two = jnp.where(lane == 0, older, jnp.where(lane == 1, newer, rolled))
+        return (first * x + second * back_one + third * back_two).astype(jnp.bfloat16)
+
+    qc = conv(q_ref, 0)
+    kc = conv(k_ref, 1)
+    vc = conv(v_ref, 2)
+    qc_ref[...] = qc
+    kc_ref[...] = kc
+    vc_ref[...] = vc
+    gated = (kc.astype(jnp.float32) * vc.astype(jnp.float32)).astype(jnp.bfloat16)
+    grad_mixed = (g_ref[...].astype(jnp.float32) * qc.astype(jnp.float32)).astype(jnp.bfloat16)
+    for j in range(rows // chan_dev):
+        out_ref[2 * j * chan_dev : (2 * j + 1) * chan_dev, :] = gated[j * chan_dev : (j + 1) * chan_dev]
+        out_ref[(2 * j + 1) * chan_dev : (2 * j + 2) * chan_dev, :] = grad_mixed[
+            j * chan_dev : (j + 1) * chan_dev
+        ]
+
+
+def front(query_proj, key_proj, value_proj, grad_out, halo, taps_cols, chan_dev):
+    all_chans, tok_cols = query_proj.shape
+    block = min(BLOCK_ROWS, all_chans)
+    tile = pl.BlockSpec((block, tok_cols), lambda i: (i, 0))
+    return pl.pallas_call(
+        functools.partial(front_kernel, chan_dev),
+        grid=(all_chans // block,),
+        in_specs=[tile, tile, tile, tile, pl.BlockSpec((block, 6), lambda i: (i, 0)),
+                  pl.BlockSpec((block, 3), lambda i: (i, 0))],
+        out_specs=[tile, tile, tile, pl.BlockSpec((2 * block, tok_cols), lambda i: (i, 0))],
+        out_shape=[jax.ShapeDtypeStruct((all_chans, tok_cols), jnp.bfloat16)] * 3
+        + [jax.ShapeDtypeStruct((2 * all_chans, tok_cols), jnp.bfloat16)],
+        cost_estimate=pl.CostEstimate(flops=30 * all_chans * tok_cols, transcendentals=0,
+                                      bytes_accessed=18 * all_chans * tok_cols),
+    )(query_proj, key_proj, value_proj, grad_out, halo, taps_cols)
+
+
 def taps_forward(current, earlier, short_taps):
     columns = current.shape[1]
     joined = jnp.concatenate([earlier, current], axis=1)
@@ -147,18 +201,10 @@
     inner = tables[4].shape[1]
     tails = jnp.concatenate([query_proj[:, -2:], key_proj[:, -2:], value_proj[:, -2:]], axis=1)
     tails = shifted(tails, "ctx", 1)
-    earlier = (tails[:, 0:2], tails[:, 2:4], tails[:, 4:6])
-    query_conv = taps_forward(
-        query_proj.astype(jnp.float32), earlier[0].astype(jnp.float32) * keep_prev, short_taps
-    ).astype(jnp.bfloat16)
-    key_conv = taps_forward(
-        key_proj.astype(jnp.float32), earlier[1].astype(jnp.float32) * keep_prev, short_taps
-    ).astype(jnp.bfloat16)
-    value_conv = taps_forward(
-        value_proj.astype(jnp.float32), earlier[2].astype(jnp.float32) * keep_prev, short_taps
-    ).astype(jnp.bfloat16)
-    query_conv, key_conv, value_conv = lax.optimization_barrier((query_conv, key_conv, value_conv))
-    gated_tok = (key_conv.astype(jnp.float32) * value_conv.astype(jnp.float32)).astype(jnp.bfloat16)
+    halo = jnp.where(keep_prev > 0, tails, jnp.zeros_like(tails))
+    query_conv, key_conv, value_conv, outgoing = front(
+        query_proj, key_proj, value_proj, grad_out, halo, short_taps.T, chan_dev
+    )
     filter_spec = forward_spectrum(filters.astype(jnp.float32), None, tables)
     filter_real = filter_spec[:, None, :, :inner]
     filter_imag = filter_spec[:, None, :, inner:]
@@ -186,14 +232,6 @@
         return jnp.concatenate([first_rows, second_rows], axis=1)
 
     cotangent = grad_out.astype(jnp.float32)
-    grad_mixed_tok = (cotangent * query_conv.astype(jnp.float32)).astype(jnp.bfloat16)
-    outgoing = jnp.concatenate(
-        [
-            gated_tok.reshape(ctx_count, chan_dev, tok_cols),
-            grad_mixed_tok.reshape(ctx_count, chan_dev, tok_cols),
-        ],
-        axis=1,
-    ).reshape(2 * all_chans, tok_cols)
     incoming = lax.all_to_all(outgoing, "ctx", split_axis=0, concat_axis=1, tiled=True)
     gated_rows = to_rows(incoming[:chan_dev])
     grad_mixed = to_rows(incoming[chan_dev:])

time: 236 us -> 229 us (0.970)
  other arithmetic: 25.7 us -> 17.9 us
  local copies, waits for them, and re-layouts: 21.9 us -> 14.3 us
  Pallas kernels: 0 us -> 7.55 us
    pallas_call x0 -> x1, Pallas kernels: none -> 7.55 us  [front(): pl.pallas_call(functools.partial(front_kernel, chan_dev), grid=(all_chans...]
    convert_element_type x5 -> x0, other arithmetic: 7.12 us -> none  [the longest x1 3.55 us: per_device(): value_conv = taps_forward(value_proj.astype(jnp.float32), earlier[2].asty...]
    convert_element_type x4, local copies, waits for them, and re-layouts: 5.49 us -> 1.06 us  [spectrum_of(): rows_three.reshape(groups_dev, 2, pair_rows, seq_len).astype(jnp.float32)]
    unnamed x55 -> x54, local copies, waits for them, and re-layouts: 5.03 us -> 3.22 us
where the time goes in v1:
time: 229 us; the launch traced here: 228 us
  waiting for transfers between devices  110 us (48%)
  starting transfers between devices  68.1 us (30%)
  other arithmetic  17.9 us (8%)
  local copies, waits for them, and re-layouts  14.3 us (6%)
  matrix products  9.67 us (4%)
  Pallas kernels  7.55 us (3%)
    all_to_all x1, waiting for transfers between devices, per_device(): lax.all_to_all(returning, 'ctx', split_axis=1, concat_axis=0, tiled=True)  41.7 us
    all_to_all x1, waiting for transfers between devices, per_device(): lax.all_to_all(outgoing, 'ctx', split_axis=0, concat_axis=1, tiled=True)  40.3 us
    all_to_all x1, starting transfers between devices, per_device(): lax.all_to_all(outgoing, 'ctx', split_axis=0, concat_axis=1, tiled=True)  35.9 us
    ppermute x2, waiting for transfers between devices, shifted(): return lax.ppermute(array, axis, pairs)  27.6 us
    ppermute x2, starting transfers between devices, shifted(): return lax.ppermute(array, axis, pairs)  11.6 us
    all_to_all x1, starting transfers between devices, per_device(): lax.all_to_all(returning, 'ctx', split_axis=1, concat_axis=0, tiled=True)  11.6 us
    ppermute x3, starting transfers between devices, ring_scatter_sum(): total = total + lax.ppermute(piece, axis, pairs)  9 us
    pallas_call x1, Pallas kernels, front(): pl.pallas_call(functools.partial(front_kernel, chan_dev), grid=(all_chans...  7.55 us
  transfers between devices with their start and end apart: 7, of which 4 were waited for; matrix products, arithmetic and copies ran while one was open for 6% of the time, Pallas kernels for 0%

profile of v1, /device:TPU:25, one launch (start us, length us, event | category | flops | bytes accessed | tf_op | source)
XLA Modules:
  0.0 228.5 jit_solution(5201815768639974583)
XLA Ops:
  0.7 1.3 slice.160
  2.2 1.3 slice.161
  4.5 9.0 %collective-permute-start = (bf16[2048,6]{1,0:T(8,128)(2,1)S(1)}, bf16[2048,6]{1,0:T(8,128)(2,1)S(1)}, u32[]{:S(2)}, u32[]{:S(2)}) collective-permute-start(bf16[2048,6]{1,0:T(8,128)(2,1)S(1)} %copy.85), channel_id=1, source_target_pairs={{0,1},{1,2},{2,3},{3,4},{4,5},{5,6},{6,7},{7,8},{8,9},{9,10},{10,1... | collective-permute-start | bytes 73736 | tf_op jit(solution)/shard_map/ppermute | solution.py:18
  13.6 1.4 copy.86
  14.9 6.5 %collective-permute-done = bf16[2048,6]{1,0:T(8,128)(2,1)S(1)} collective-permute-done((bf16[2048,6]{1,0:T(8,128)(2,1)S(1)}, bf16[2048,6]{1,0:T(8,128)(2,1)S(1)}, u32[]{:S(2)}, u32[]{:S(2)}) %collective-permute-start) | collective-permute-done | bytes 24608 | tf_op jit(solution)/shard_map/ppermute | solution.py:18
  21.4 0.8 broadcast_select_fusion.halo_ref
  22.2 7.5 %shard_map.93 = (bf16[2048,128]{1,0:T(8,128)(2,1)}, bf16[2048,128]{1,0:T(8,128)(2,1)}, bf16[2048,128]{1,0:T(8,128)(2,1)}, bf16[4096,128]{1,0:T(8,128)(2,1)}) custom-call(bf16[2048,128]{1,0:T(8,128)(2,1)} %q_ref.1, bf16[2048,128]{1,0:T(8,128)(2,1)} %k_ref.1, bf16[2048,128]{1,0:T(8,128)(2,1)} %v_ref.1, bf16[2048,128]{1,0:T(8,128)(2,1)} %g_ref.1, ...), custom_call_target="tpu_custom_call" | custom-call | flops 7864320 | bytes 4718592 | tf_op jit(solution)/shard_map/pallas_call | solution.py:154
  29.8 35.9 %all-to-all-start = ((bf16[128,32,128]{2,1,0:T(8,128)(2,1)}), bf16[128,32,128]{2,1,0:T(8,128)(2,1)S(1)}, u32[]{:S(2)}, u32[]{:S(2)}) async-start(bf16[128,32,128]{2,1,0:T(8,128)(2,1)} %bitcast.120), calls=%async_computation | async-start | bytes 2097152 | tf_op jit(solution)/shard_map/all_to_all | solution.py:235
  66.9 1.2 fusion.123
  70.9 1.2 fusion.130
  72.1 1.3 fusion.125
  73.3 1.2 fusion.127
  74.6 40.3 %all-to-all-done = bf16[128,32,128]{2,1,0:T(8,128)(2,1)S(1)} async-done(((bf16[128,32,128]{2,1,0:T(8,128)(2,1)}), bf16[128,32,128]{2,1,0:T(8,128)(2,1)S(1)}, u32[]{:S(2)}, u32[]{:S(2)}) %all-to-all-start) | async-done | bytes 1048608 | tf_op jit(solution)/shard_map/all_to_all | solution.py:235
  115.8 1.0 copy.100
  116.8 1.0 copy.99
  119.8 1.0 fusion.69
  120.8 1.0 fusion.70
  122.5 1.0 fusion.25
  123.6 1.3 fusion.22
  125.7 1.0 fusion.15
  126.7 1.0 fusion.4
  128.8 1.1 fusion.43
  129.9 1.1 fusion.40
  131.2 1.7 copy.107
  132.9 11.6 %all-to-all-start.1 = ((bf16[32,128,128]{2,0,1:T(8,128)(2,1)}), bf16[32,128,128]{2,0,1:T(8,128)(2,1)S(1)}, u32[]{:S(2)}, u32[]{:S(2)}) async-start(bf16[32,128,128]{2,0,1:T(8,128)(2,1)} %copy.107), calls=%async_computation.1 | async-start | bytes 2097152 | tf_op jit(solution)/shard_map/all_to_all | solution.py:247
  146.4 1.9 collective-permute-start.2
  148.4 3.0 %collective-permute-start.3 = (f32[1,4096]{1,0:T(1,128)S(1)}, f32[1,4096]{1,0:T(1,128)S(1)}, u32[]{:S(2)}, u32[]{:S(2)}) collective-permute-start(f32[1,4096]{1,0:T(1,128)S(1)} %get-tuple-element.63), channel_id=1, source_target_pairs={{0,256},{128,384},{256,0},{384,128},{1,257},{129,385},{257,1},{385... | collective-permute-start | bytes 49160 | tf_op jit(solution)/shard_map/ppermute | solution.py:30
  151.4 4.0 %collective-permute-start.4 = (f32[1,4096]{1,0:T(1,128)S(1)}, f32[1,4096]{1,0:T(1,128)S(1)}, u32[]{:S(2)}, u32[]{:S(2)}) collective-permute-start(f32[1,4096]{1,0:T(1,128)S(1)} %get-tuple-element.62), channel_id=1, source_target_pairs={{0,384},{128,0},{256,128},{384,256},{1,385},{129,1},{257,129},{385... | collective-permute-start | bytes 49160 | tf_op jit(solution)/shard_map/ppermute | solution.py:30
  155.4 41.7 %all-to-all-done.1 = bf16[32,128,128]{2,0,1:T(8,128)(2,1)S(1)} async-done(((bf16[32,128,128]{2,0,1:T(8,128)(2,1)}), bf16[32,128,128]{2,0,1:T(8,128)(2,1)S(1)}, u32[]{:S(2)}, u32[]{:S(2)}) %all-to-all-start.1) | async-done | bytes 1048608 | tf_op jit(solution)/shard_map/all_to_all | solution.py:247
  198.3 2.6 %collective-permute-start.1 = (bf16[2048,6]{1,0:T(8,128)(2,1)S(1)}, bf16[2048,6]{1,0:T(8,128)(2,1)S(1)}, u32[]{:S(2)}, u32[]{:S(2)}) collective-permute-start(bf16[2048,6]{1,0:T(8,128)(2,1)S(1)} %pad_maximum_fusion.6), channel_id=1, source_target_pairs={{1,0},{2,1},{3,2},{4,3},{5,4},{6,5},{7,6},{8,7},{9,8},{10,9},{11,1... | collective-permute-start | bytes 73736 | tf_op jit(solution)/shard_map/ppermute | solution.py:18
  201.8 21.1 %collective-permute-done.1 = bf16[2048,6]{1,0:T(8,128)(2,1)S(1)} collective-permute-done((bf16[2048,6]{1,0:T(8,128)(2,1)S(1)}, bf16[2048,6]{1,0:T(8,128)(2,1)S(1)}, u32[]{:S(2)}, u32[]{:S(2)}) %collective-permute-start.1) | collective-permute-done | bytes 24608 | tf_op jit(solution)/shard_map/ppermute | solution.py:18
  223.3 5.1 %fusion.52 = (bf16[2048,128]{1,0:T(8,128)(2,1)}, bf16[2048,128]{1,0:T(8,128)(2,1)}, bf16[2048,128]{1,0:T(8,128)(2,1)}) fusion(f32[2048,128]{1,0:T(8,128)S(1)} %convert_element_type.220, f32[2048,2]{1,0:T(8,128)S(1)} %get-tuple-element.42, f32[2048]{0:T(1024)S(1)} %bitcast.126, f32[2048]{0:T(1024)S(1)} %bitcast.127, f32[2048]{0:T(1024)S(1)} %bitcast.125, ...), kind=kLoop, calls=%fused_computation.50 | loop fusion | flops 6291456 | bytes 4792320 | tf_op jit(solution)/shard_map/convert_element_type | solution.py:279
  (101 shorter events, 15.0 us)
Async XLA Ops:
  0.6 65.1 %copy-start = (bf16[1,16384]{1,0:T(2,128)(2,1)S(1)}, bf16[1,16384]{1,0:T(2,128)(2,1)}, u32[]{:S(2)}) copy-start(bf16[1,16384]{1,0:T(2,128)(2,1)} %param.10) | copy-start | bytes 98308
  0.6 3.0 %copy-start.5 = (bf16[2048,128]{1,0:T(8,128)(2,1)S(1)}, bf16[2048,128]{1,0:T(8,128)(2,1)}, u32[]{:S(2)}) copy-start(bf16[2048,128]{1,0:T(8,128)(2,1)} %v_ref.1) | copy-start | bytes 1572868
  2.0 11.6 %copy-start.21 = (f32[3,2048]{1,0:T(4,128)S(1)}, f32[3,2048]{1,0:T(4,128)}, u32[]{:S(2)}) copy-start(f32[3,2048]{1,0:T(4,128)} %param.11) | copy-start | bytes 73732
  4.5 16.9 %collective-permute-start = (bf16[2048,6]{1,0:T(8,128)(2,1)S(1)}, bf16[2048,6]{1,0:T(8,128)(2,1)S(1)}, u32[]{:S(2)}, u32[]{:S(2)}) collective-permute-start(bf16[2048,6]{1,0:T(8,128)(2,1)S(1)} %copy.85), channel_id=1, source_target_pairs={{0,1},{1,2},{2,3},{3,4},{4,5},{5,6},{6,7},{7,8},{8,9},{9,10},{10,1... | collective-permute-start | bytes 73736 | tf_op jit(solution)/shard_map/ppermute | solution.py:18
  29.8 85.1 %all-to-all-start = ((bf16[128,32,128]{2,1,0:T(8,128)(2,1)}), bf16[128,32,128]{2,1,0:T(8,128)(2,1)S(1)}, u32[]{:S(2)}, u32[]{:S(2)}) async-start(bf16[128,32,128]{2,1,0:T(8,128)(2,1)} %bitcast.120), calls=%async_computation | async-start | bytes 2097152 | tf_op jit(solution)/shard_map/all_to_all | solution.py:235
  68.1 46.7 %copy-start.2 = (f32[128,256]{1,0:T(8,128)}, f32[128,256]{1,0:T(8,128)S(1)}, u32[]{:S(2)}) copy-start(f32[128,256]{1,0:T(8,128)S(1)} %get-tuple-element.73) | copy-start | bytes 393220
  118.4 1.0 copy-start.6
  118.5 1.2 copy-start.7
  118.7 1.0 copy-start.3
  118.7 1.1 copy-start.10
  120.8 1.0 copy-start.8
  120.8 1.0 copy-start.9
  123.5 1.3 copy-start.11
  123.6 1.3 copy-start.12
  127.8 0.9 copy-start.15
  127.8 1.0 copy-start.17
  127.8 1.0 copy-start.19
  131.2 13.3 %copy-start.16 = (f32[256,128]{0,1:T(8,128)S(1)}, f32[256,128]{0,1:T(8,128)}, u32[]{:S(2)}) copy-start(f32[256,128]{0,1:T(8,128)} %fusion.130) | copy-start | bytes 393220
  131.2 13.3 %copy-start.18 = (f32[256,128]{0,1:T(8,128)S(1)}, f32[256,128]{0,1:T(8,128)}, u32[]{:S(2)}) copy-start(f32[256,128]{0,1:T(8,128)} %get-tuple-element.80) | copy-start | bytes 393220
  131.2 13.3 %copy-start.20 = (f32[256,128]{0,1:T(8,128)S(1)}, f32[256,128]{0,1:T(8,128)}, u32[]{:S(2)}) copy-start(f32[256,128]{0,1:T(8,128)} %get-tuple-element.81) | copy-start | bytes 393220
  132.9 11.7 %copy-start.22 = (f32[3,2048]{1,0:T(4,128)S(1)}, f32[3,2048]{1,0:T(4,128)}, u32[]{:S(2)}) copy-start(f32[3,2048]{1,0:T(4,128)} %param.11) | copy-start | bytes 73732
  132.9 64.3 %all-to-all-start.1 = ((bf16[32,128,128]{2,0,1:T(8,128)(2,1)}), bf16[32,128,128]{2,0,1:T(8,128)(2,1)S(1)}, u32[]{:S(2)}, u32[]{:S(2)}) async-start(bf16[32,128,128]{2,0,1:T(8,128)(2,1)} %copy.107), calls=%async_computation.1 | async-start | bytes 2097152 | tf_op jit(solution)/shard_map/all_to_all | solution.py:247
  144.6 52.7 %copy-start.4 = (bf16[2048,128]{1,0:T(8,128)(2,1)S(1)}, bf16[2048,128]{1,0:T(8,128)(2,1)}, u32[]{:S(2)}) copy-start(bf16[2048,128]{1,0:T(8,128)(2,1)} %g_ref.1) | copy-start | bytes 1572868
  146.1 51.4 %copy-start.13 = (bf16[2048,128]{1,0:T(8,128)(2,1)S(1)}, bf16[2048,128]{1,0:T(8,128)(2,1)}, u32[]{:S(2)}) copy-start(bf16[2048,128]{1,0:T(8,128)(2,1)} %get-tuple-element.12) | copy-start | bytes 1572868
  146.1 51.4 %copy-start.14 = (bf16[2048,128]{1,0:T(8,128)(2,1)S(1)}, bf16[2048,128]{1,0:T(8,128)(2,1)}, u32[]{:S(2)}) copy-start(bf16[2048,128]{1,0:T(8,128)(2,1)} %get-tuple-element.11) | copy-start | bytes 1572868
  146.4 54.5 %collective-permute-start.2 = (f32[1,4096]{1,0:T(1,128)S(1)}, f32[1,4096]{1,0:T(1,128)S(1)}, u32[]{:S(2)}, u32[]{:S(2)}) collective-permute-start(f32[1,4096]{1,0:T(1,128)S(1)} %get-tuple-element.61), channel_id=1, source_target_pairs={{0,128},{128,256},{256,384},{384,0},{1,129},{129,257},{257,385},{3... | collective-permute-start | bytes 49160 | tf_op jit(solution)/shard_map/ppermute | solution.py:30
  148.4 52.6 %collective-permute-start.3 = (f32[1,4096]{1,0:T(1,128)S(1)}, f32[1,4096]{1,0:T(1,128)S(1)}, u32[]{:S(2)}, u32[]{:S(2)}) collective-permute-start(f32[1,4096]{1,0:T(1,128)S(1)} %get-tuple-element.63), channel_id=1, source_target_pairs={{0,256},{128,384},{256,0},{384,128},{1,257},{129,385},{257,1},{385... | collective-permute-start | bytes 49160 | tf_op jit(solution)/shard_map/ppermute | solution.py:30
  151.4 49.5 %collective-permute-start.4 = (f32[1,4096]{1,0:T(1,128)S(1)}, f32[1,4096]{1,0:T(1,128)S(1)}, u32[]{:S(2)}, u32[]{:S(2)}) collective-permute-start(f32[1,4096]{1,0:T(1,128)S(1)} %get-tuple-element.62), channel_id=1, source_target_pairs={{0,384},{128,0},{256,128},{384,256},{1,385},{129,1},{257,129},{385... | collective-permute-start | bytes 49160 | tf_op jit(solution)/shard_map/ppermute | solution.py:30
  198.3 24.6 %collective-permute-start.1 = (bf16[2048,6]{1,0:T(8,128)(2,1)S(1)}, bf16[2048,6]{1,0:T(8,128)(2,1)S(1)}, u32[]{:S(2)}, u32[]{:S(2)}) collective-permute-start(bf16[2048,6]{1,0:T(8,128)(2,1)S(1)} %pad_maximum_fusion.6), channel_id=1, source_target_pairs={{1,0},{2,1},{3,2},{4,3},{5,4},{6,5},{7,6},{8,7},{9,8},{10,9},{11,1... | collective-permute-start | bytes 73736 | tf_op jit(solution)/shard_map/ppermute | solution.py:18
  201.8 21.5 %copy-start.23 = (f32[1,2048]{1,0:T(1,128)S(1)}, f32[1,2048]{1,0:T(1,128)}, u32[]{:S(2)}) copy-start(f32[1,2048]{1,0:T(1,128)} %get-tuple-element.66) | copy-start | bytes 24580
  223.3 5.2 %copy-start.1 = (bf16[1,16384]{1,0:T(2,128)(2,1)S(1)}, bf16[1,16384]{1,0:T(2,128)(2,1)}, u32[]{:S(2)}) copy-start(bf16[1,16384]{1,0:T(2,128)(2,1)} %param.10) | copy-start | bytes 98308

commit v2 on v1

--- a/solution.py
+++ b/solution.py
@@ -20,14 +20,17 @@
 
 def ring_scatter_sum(terms, axis):
     count = lax.axis_size(axis)
-    width = terms.shape[1] // count
     me = lax.axis_index(axis)
-    total = lax.dynamic_slice_in_dim(terms, me * width, width, axis=1)
-    for step in range(1, count):
-        target = (me + step) % count
-        piece = lax.dynamic_slice_in_dim(terms, target * width, width, axis=1)
-        pairs = [(i, (i + step) % count) for i in range(count)]
-        total = total + lax.ppermute(piece, axis, pairs)
+    total = terms
+    span = count
+    while span > 1:
+        span //= 2
+        width = total.shape[1] // 2
+        upper = (me // span) % 2
+        keep = lax.dynamic_slice_in_dim(total, upper * width, width, axis=1)
+        give = lax.dynamic_slice_in_dim(total, (1 - upper) * width, width, axis=1)
+        pairs = [(i, i ^ span) for i in range(count)]
+        total = keep + lax.ppermute(give, axis, pairs)
     return total
 
 
@@ -113,7 +116,7 @@
     return values.reshape(row_count, length)
 
 
-BLOCK_ROWS = 256
+BLOCK_ROWS = 1024
 
 
 def front_kernel(chan_dev, q_ref, k_ref, v_ref, g_ref, halo_ref, taps_ref, qc_ref, kc_ref, vc_ref, out_ref):

time: 229 us -> 231 us (level)
  waiting for transfers between devices: 110 us -> 118 us
  starting transfers between devices: 68.1 us -> 64.4 us
    ppermute x3 -> x2, waiting for transfers between devices: 0.01 us -> 39.8 us  [ring_scatter_sum(): total = keep + lax.ppermute(give, axis, pairs)]
    all_to_all x1, waiting for transfers between devices: 41.7 us -> 6.31 us  [per_device(): lax.all_to_all(returning, 'ctx', split_axis=1, concat_axis=0, tiled=True)]
    ppermute x2, waiting for transfers between devices: 27.6 us -> 31.8 us  [shifted(): return lax.ppermute(array, axis, pairs)]
    ppermute x3 -> x2, starting transfers between devices: 9 us -> 5.43 us  [ring_scatter_sum(): total = keep + lax.ppermute(give, axis, pairs)]
  transfers between devices with their start and end apart: 7 -> 6, of which waited for: 4 -> 5; matrix products, arithmetic and copies ran while one was open for 6% -> 6% of each run, Pallas kernels for 0% -> 0%
where the time goes in v2:
time: 231 us
  waiting for transfers between devices  118 us (51%)
  starting transfers between devices  64.4 us (28%)
  other arithmetic  17.9 us (8%)
  local copies, waits for them, and re-layouts  13.7 us (6%)
  matrix products  9.67 us (4%)
  Pallas kernels  5.78 us (3%)
    all_to_all x1, waiting for transfers between devices, per_device(): lax.all_to_all(outgoing, 'ctx', split_axis=0, concat_axis=1, tiled=True)  40.3 us
    ppermute x2, waiting for transfers between devices, ring_scatter_sum(): total = keep + lax.ppermute(give, axis, pairs)  39.8 us
    all_to_all x1, starting transfers between devices, per_device(): lax.all_to_all(outgoing, 'ctx', split_axis=0, concat_axis=1, tiled=True)  35.9 us
    ppermute x2, waiting for transfers between devices, shifted(): return lax.ppermute(array, axis, pairs)  31.8 us
    all_to_all x1, starting transfers between devices, per_device(): lax.all_to_all(returning, 'ctx', split_axis=1, concat_axis=0, tiled=True)  11.6 us
    ppermute x2, starting transfers between devices, shifted(): return lax.ppermute(array, axis, pairs)  11.5 us
    all_to_all x1, waiting for transfers between devices, per_device(): lax.all_to_all(returning, 'ctx', split_axis=1, concat_axis=0, tiled=True)  6.31 us
    pallas_call x1, Pallas kernels, front(): pl.pallas_call(functools.partial(front_kernel, chan_dev), grid=(all_chans...  5.78 us
  transfers between devices with their start and end apart: 6, of which 5 were waited for; matrix products, arithmetic and copies ran while one was open for 6% of the time, Pallas kernels for 0%

profile of v2, /device:TPU:25, one launch (start us, length us, event | category | flops | bytes accessed | tf_op | source)
XLA Modules:
  0.0 231.0 jit_solution(1665075972717788575)
XLA Ops:
  0.7 1.3 slice.160
  2.2 1.3 slice.161
  4.5 9.0 %collective-permute-start = (bf16[2048,6]{1,0:T(8,128)(2,1)S(1)}, bf16[2048,6]{1,0:T(8,128)(2,1)S(1)}, u32[]{:S(2)}, u32[]{:S(2)}) collective-permute-start(bf16[2048,6]{1,0:T(8,128)(2,1)S(1)} %copy.85), channel_id=1, source_target_pairs={{0,1},{1,2},{2,3},{3,4},{4,5},{5,6},{6,7},{7,8},{8,9},{9,10},{10,1... | collective-permute-start | bytes 73736 | tf_op jit(solution)/shard_map/ppermute | solution.py:18
  13.6 1.4 copy.86
  14.9 6.5 %collective-permute-done = bf16[2048,6]{1,0:T(8,128)(2,1)S(1)} collective-permute-done((bf16[2048,6]{1,0:T(8,128)(2,1)S(1)}, bf16[2048,6]{1,0:T(8,128)(2,1)S(1)}, u32[]{:S(2)}, u32[]{:S(2)}) %collective-permute-start) | collective-permute-done | bytes 24608 | tf_op jit(solution)/shard_map/ppermute | solution.py:18
  21.4 0.8 broadcast_select_fusion.halo_ref
  22.2 5.8 %shard_map.93 = (bf16[2048,128]{1,0:T(8,128)(2,1)}, bf16[2048,128]{1,0:T(8,128)(2,1)}, bf16[2048,128]{1,0:T(8,128)(2,1)}, bf16[4096,128]{1,0:T(8,128)(2,1)}) custom-call(bf16[2048,128]{1,0:T(8,128)(2,1)} %q_ref.1, bf16[2048,128]{1,0:T(8,128)(2,1)} %k_ref.1, bf16[2048,128]{1,0:T(8,128)(2,1)} %v_ref.1, bf16[2048,128]{1,0:T(8,128)(2,1)} %g_ref.1, ...), custom_call_target="tpu_custom_call" | custom-call | flops 7864320 | bytes 4718592 | tf_op jit(solution)/shard_map/pallas_call | solution.py:157
  28.0 35.9 %all-to-all-start = ((bf16[128,32,128]{2,1,0:T(8,128)(2,1)}), bf16[128,32,128]{2,1,0:T(8,128)(2,1)S(1)}, u32[]{:S(2)}, u32[]{:S(2)}) async-start(bf16[128,32,128]{2,1,0:T(8,128)(2,1)} %bitcast.120), calls=%async_computation | async-start | bytes 2097152 | tf_op jit(solution)/shard_map/all_to_all | solution.py:238
  65.2 1.2 fusion.123
  69.2 1.1 fusion.130
  70.3 1.2 fusion.125
  71.5 1.2 fusion.127
  72.8 40.3 %all-to-all-done = bf16[128,32,128]{2,1,0:T(8,128)(2,1)S(1)} async-done(((bf16[128,32,128]{2,1,0:T(8,128)(2,1)}), bf16[128,32,128]{2,1,0:T(8,128)(2,1)S(1)}, u32[]{:S(2)}, u32[]{:S(2)}) %all-to-all-start) | async-done | bytes 1048608 | tf_op jit(solution)/shard_map/all_to_all | solution.py:238
  114.1 1.0 copy.100
  115.1 1.0 copy.99
  118.0 1.0 fusion.69
  119.1 1.0 fusion.70
  120.7 1.0 fusion.25
  121.8 1.3 fusion.22
  123.9 1.0 fusion.15
  125.0 1.0 fusion.4
  127.0 1.1 fusion.43
  128.2 1.1 fusion.40
  129.5 1.7 copy.107
  131.1 11.6 %all-to-all-start.1 = ((bf16[32,128,128]{2,0,1:T(8,128)(2,1)}), bf16[32,128,128]{2,0,1:T(8,128)(2,1)S(1)}, u32[]{:S(2)}, u32[]{:S(2)}) async-start(bf16[32,128,128]{2,0,1:T(8,128)(2,1)} %copy.107), calls=%async_computation.1 | async-start | bytes 2097152 | tf_op jit(solution)/shard_map/all_to_all | solution.py:250
  144.0 2.1 collective-permute-start.2
  146.1 39.8 %collective-permute-done.2 = f32[1,8192]{1,0:T(1,128)S(1)} collective-permute-done((f32[1,8192]{1,0:T(1,128)S(1)}, f32[1,8192]{1,0:T(1,128)S(1)}, u32[]{:S(2)}, u32[]{:S(2)}) %collective-permute-start.2) | collective-permute-done | bytes 32800 | tf_op jit(solution)/shard_map/ppermute | solution.py:33
  186.0 3.4 %collective-permute-start.3 = (f32[1,4096]{1,0:T(1,128)S(1)}, f32[1,4096]{1,0:T(1,128)S(1)}, u32[]{:S(2)}, u32[]{:S(2)}) collective-permute-start(f32[1,4096]{1,0:T(1,128)S(1)} %constant_dynamic-slice_fusion), channel_id=1, source_target_pairs={{0,128},{128,0},{256,384},{384,256},{1,129},{129,1},{257,385},{385... | collective-permute-start | bytes 49160 | tf_op jit(solution)/shard_map/ppermute | solution.py:33
  189.4 6.3 %all-to-all-done.1 = bf16[32,128,128]{2,0,1:T(8,128)(2,1)S(1)} async-done(((bf16[32,128,128]{2,0,1:T(8,128)(2,1)}), bf16[32,128,128]{2,0,1:T(8,128)(2,1)S(1)}, u32[]{:S(2)}, u32[]{:S(2)}) %all-to-all-start.1) | async-done | bytes 1048608 | tf_op jit(solution)/shard_map/all_to_all | solution.py:250
  196.8 2.4 %collective-permute-start.1 = (bf16[2048,6]{1,0:T(8,128)(2,1)S(1)}, bf16[2048,6]{1,0:T(8,128)(2,1)S(1)}, u32[]{:S(2)}, u32[]{:S(2)}) collective-permute-start(bf16[2048,6]{1,0:T(8,128)(2,1)S(1)} %pad_maximum_fusion.6), channel_id=1, source_target_pairs={{1,0},{2,1},{3,2},{4,3},{5,4},{6,5},{7,6},{8,7},{9,8},{10,9},{11,1... | collective-permute-start | bytes 73736 | tf_op jit(solution)/shard_map/ppermute | solution.py:18
  200.2 25.3 %collective-permute-done.1 = bf16[2048,6]{1,0:T(8,128)(2,1)S(1)} collective-permute-done((bf16[2048,6]{1,0:T(8,128)(2,1)S(1)}, bf16[2048,6]{1,0:T(8,128)(2,1)S(1)}, u32[]{:S(2)}, u32[]{:S(2)}) %collective-permute-start.1) | collective-permute-done | bytes 24608 | tf_op jit(solution)/shard_map/ppermute | solution.py:18
  225.8 5.1 %fusion.52 = (bf16[2048,128]{1,0:T(8,128)(2,1)}, bf16[2048,128]{1,0:T(8,128)(2,1)}, bf16[2048,128]{1,0:T(8,128)(2,1)}) fusion(f32[2048,128]{1,0:T(8,128)S(1)} %convert_element_type.220, f32[2048,2]{1,0:T(8,128)S(1)} %get-tuple-element.42, f32[2048]{0:T(1024)S(1)} %bitcast.126, f32[2048]{0:T(1024)S(1)} %bitcast.127, f32[2048]{0:T(1024)S(1)} %bitcast.125, ...), kind=kLoop, calls=%fused_computation.50 | loop fusion | flops 6291456 | bytes 4792320 | tf_op jit(solution)/shard_map/convert_element_type | solution.py:282
  (99 shorter events, 14.4 us)
Async XLA Ops:
  0.6 63.3 %copy-start = (bf16[1,16384]{1,0:T(2,128)(2,1)S(1)}, bf16[1,16384]{1,0:T(2,128)(2,1)}, u32[]{:S(2)}) copy-start(bf16[1,16384]{1,0:T(2,128)(2,1)} %param.10) | copy-start | bytes 98308
  0.6 3.0 %copy-start.5 = (bf16[2048,128]{1,0:T(8,128)(2,1)S(1)}, bf16[2048,128]{1,0:T(8,128)(2,1)}, u32[]{:S(2)}) copy-start(bf16[2048,128]{1,0:T(8,128)(2,1)} %v_ref.1) | copy-start | bytes 1572868
  2.0 11.6 %copy-start.21 = (f32[3,2048]{1,0:T(4,128)S(1)}, f32[3,2048]{1,0:T(4,128)}, u32[]{:S(2)}) copy-start(f32[3,2048]{1,0:T(4,128)} %param.11) | copy-start | bytes 73732
  4.5 16.9 %collective-permute-start = (bf16[2048,6]{1,0:T(8,128)(2,1)S(1)}, bf16[2048,6]{1,0:T(8,128)(2,1)S(1)}, u32[]{:S(2)}, u32[]{:S(2)}) collective-permute-start(bf16[2048,6]{1,0:T(8,128)(2,1)S(1)} %copy.85), channel_id=1, source_target_pairs={{0,1},{1,2},{2,3},{3,4},{4,5},{5,6},{6,7},{7,8},{8,9},{9,10},{10,1... | collective-permute-start | bytes 73736 | tf_op jit(solution)/shard_map/ppermute | solution.py:18
  28.0 85.1 %all-to-all-start = ((bf16[128,32,128]{2,1,0:T(8,128)(2,1)}), bf16[128,32,128]{2,1,0:T(8,128)(2,1)S(1)}, u32[]{:S(2)}, u32[]{:S(2)}) async-start(bf16[128,32,128]{2,1,0:T(8,128)(2,1)} %bitcast.120), calls=%async_computation | async-start | bytes 2097152 | tf_op jit(solution)/shard_map/all_to_all | solution.py:238
  66.4 46.7 %copy-start.2 = (f32[128,256]{1,0:T(8,128)}, f32[128,256]{1,0:T(8,128)S(1)}, u32[]{:S(2)}) copy-start(f32[128,256]{1,0:T(8,128)S(1)} %get-tuple-element.70) | copy-start | bytes 393220
  116.7 1.0 copy-start.6
  116.7 1.2 copy-start.7
  116.9 1.0 copy-start.3
  116.9 1.1 copy-start.10
  119.1 1.0 copy-start.8
  119.1 1.0 copy-start.9
  121.8 1.3 copy-start.11
  121.8 1.3 copy-start.12
  126.0 0.9 copy-start.15
  126.0 1.0 copy-start.17
  126.0 1.0 copy-start.19
  129.4 13.3 %copy-start.16 = (f32[256,128]{0,1:T(8,128)S(1)}, f32[256,128]{0,1:T(8,128)}, u32[]{:S(2)}) copy-start(f32[256,128]{0,1:T(8,128)} %fusion.130) | copy-start | bytes 393220
  129.4 13.3 %copy-start.18 = (f32[256,128]{0,1:T(8,128)S(1)}, f32[256,128]{0,1:T(8,128)}, u32[]{:S(2)}) copy-start(f32[256,128]{0,1:T(8,128)} %get-tuple-element.77) | copy-start | bytes 393220
  129.4 13.3 %copy-start.20 = (f32[256,128]{0,1:T(8,128)S(1)}, f32[256,128]{0,1:T(8,128)}, u32[]{:S(2)}) copy-start(f32[256,128]{0,1:T(8,128)} %get-tuple-element.78) | copy-start | bytes 393220
  131.1 14.9 %copy-start.22 = (f32[3,2048]{1,0:T(4,128)S(1)}, f32[3,2048]{1,0:T(4,128)}, u32[]{:S(2)}) copy-start(f32[3,2048]{1,0:T(4,128)} %param.11) | copy-start | bytes 73732
  131.1 64.5 %all-to-all-start.1 = ((bf16[32,128,128]{2,0,1:T(8,128)(2,1)}), bf16[32,128,128]{2,0,1:T(8,128)(2,1)S(1)}, u32[]{:S(2)}, u32[]{:S(2)}) async-start(bf16[32,128,128]{2,0,1:T(8,128)(2,1)} %copy.107), calls=%async_computation.1 | async-start | bytes 2097152 | tf_op jit(solution)/shard_map/all_to_all | solution.py:250
  142.8 53.1 %copy-start.4 = (bf16[2048,128]{1,0:T(8,128)(2,1)S(1)}, bf16[2048,128]{1,0:T(8,128)(2,1)}, u32[]{:S(2)}) copy-start(bf16[2048,128]{1,0:T(8,128)(2,1)} %g_ref.1) | copy-start | bytes 1572868
  143.9 52.1 %copy-start.13 = (bf16[2048,128]{1,0:T(8,128)(2,1)S(1)}, bf16[2048,128]{1,0:T(8,128)(2,1)}, u32[]{:S(2)}) copy-start(bf16[2048,128]{1,0:T(8,128)(2,1)} %get-tuple-element.12) | copy-start | bytes 1572868
  143.9 52.1 %copy-start.14 = (bf16[2048,128]{1,0:T(8,128)(2,1)S(1)}, bf16[2048,128]{1,0:T(8,128)(2,1)}, u32[]{:S(2)}) copy-start(bf16[2048,128]{1,0:T(8,128)(2,1)} %get-tuple-element.11) | copy-start | bytes 1572868
  144.0 42.0 %collective-permute-start.2 = (f32[1,8192]{1,0:T(1,128)S(1)}, f32[1,8192]{1,0:T(1,128)S(1)}, u32[]{:S(2)}, u32[]{:S(2)}) collective-permute-start(f32[1,8192]{1,0:T(1,128)S(1)} %constant_dynamic-slice_fusion.1), channel_id=1, source_target_pairs={{0,256},{128,384},{256,0},{384,128},{1,257},{129,385},{257,1},{385... | collective-permute-start | bytes 98312 | tf_op jit(solution)/shard_map/ppermute | solution.py:33
  186.0 13.3 %collective-permute-start.3 = (f32[1,4096]{1,0:T(1,128)S(1)}, f32[1,4096]{1,0:T(1,128)S(1)}, u32[]{:S(2)}, u32[]{:S(2)}) collective-permute-start(f32[1,4096]{1,0:T(1,128)S(1)} %constant_dynamic-slice_fusion), channel_id=1, source_target_pairs={{0,128},{128,0},{256,384},{384,256},{1,129},{129,1},{257,385},{385... | collective-permute-start | bytes 49160 | tf_op jit(solution)/shard_map/ppermute | solution.py:33
  196.8 28.6 %collective-permute-start.1 = (bf16[2048,6]{1,0:T(8,128)(2,1)S(1)}, bf16[2048,6]{1,0:T(8,128)(2,1)S(1)}, u32[]{:S(2)}, u32[]{:S(2)}) collective-permute-start(bf16[2048,6]{1,0:T(8,128)(2,1)S(1)} %pad_maximum_fusion.6), channel_id=1, source_target_pairs={{1,0},{2,1},{3,2},{4,3},{5,4},{6,5},{7,6},{8,7},{9,8},{10,9},{11,1... | collective-permute-start | bytes 73736 | tf_op jit(solution)/shard_map/ppermute | solution.py:18
  225.8 5.2 %copy-start.1 = (bf16[1,16384]{1,0:T(2,128)(2,1)S(1)}, bf16[1,16384]{1,0:T(2,128)(2,1)}, u32[]{:S(2)}) copy-start(bf16[1,16384]{1,0:T(2,128)(2,1)} %param.10) | copy-start | bytes 98308

commit v3 on v1

--- a/solution.py
+++ b/solution.py
@@ -113,38 +113,45 @@
     return values.reshape(row_count, length)
 
 
-BLOCK_ROWS = 256
+BLOCK_ROWS = 1024
+SUB_ROWS = 128
 
 
 def front_kernel(chan_dev, q_ref, k_ref, v_ref, g_ref, halo_ref, taps_ref, qc_ref, kc_ref, vc_ref, out_ref):
     rows, cols = q_ref.shape
-    lane = lax.broadcasted_iota(jnp.int32, (rows, cols), 1)
-    halo = halo_ref[...].astype(jnp.float32)
-    taps = taps_ref[...]
-    first, second, third = taps[:, 0:1], taps[:, 1:2], taps[:, 2:3]
-
-    def conv(x_ref, slot):
-        x = x_ref[...].astype(jnp.float32)
-        older = halo[:, 2 * slot : 2 * slot + 1]
-        newer = halo[:, 2 * slot + 1 : 2 * slot + 2]
-        back_one = jnp.where(lane == 0, newer, pltpu.roll(x, 1, 1))
-        rolled = pltpu.roll(x, 2, 1)
-        back_two = jnp.where(lane == 0, older, jnp.where(lane == 1, newer, rolled))
-        return (first * x + second * back_one + third * back_two).astype(jnp.bfloat16)
-
-    qc = conv(q_ref, 0)
-    kc = conv(k_ref, 1)
-    vc = conv(v_ref, 2)
-    qc_ref[...] = qc
-    kc_ref[...] = kc
-    vc_ref[...] = vc
-    gated = (kc.astype(jnp.float32) * vc.astype(jnp.float32)).astype(jnp.bfloat16)
-    grad_mixed = (g_ref[...].astype(jnp.float32) * qc.astype(jnp.float32)).astype(jnp.bfloat16)
-    for j in range(rows // chan_dev):
-        out_ref[2 * j * chan_dev : (2 * j + 1) * chan_dev, :] = gated[j * chan_dev : (j + 1) * chan_dev]
-        out_ref[(2 * j + 1) * chan_dev : (2 * j + 2) * chan_dev, :] = grad_mixed[
-            j * chan_dev : (j + 1) * chan_dev
-        ]
+    chunk = min(SUB_ROWS, rows)
+    per_chunk = chunk // chan_dev
+    lane = lax.broadcasted_iota(jnp.int32, (chunk, cols), 1)
+
+    def body(step, carry):
+        span = pl.ds(pl.multiple_of(step * chunk, chunk), chunk)
+        halo = halo_ref[span, :].astype(jnp.float32)
+        taps = taps_ref[span, :]
+        first, second, third = taps[:, 0:1], taps[:, 1:2], taps[:, 2:3]
+
+        def conv(x_ref, slot):
+            x = x_ref[span, :].astype(jnp.float32)
+            older = halo[:, 2 * slot : 2 * slot + 1]
+            newer = halo[:, 2 * slot + 1 : 2 * slot + 2]
+            back_one = jnp.where(lane == 0, newer, pltpu.roll(x, 1, 1))
+            rolled = pltpu.roll(x, 2, 1)
+            back_two = jnp.where(lane == 0, older, jnp.where(lane == 1, newer, rolled))
+            return (first * x + second * back_one + third * back_two).astype(jnp.bfloat16)
+
+        qc = conv(q_ref, 0)
+        kc = conv(k_ref, 1)
+        vc = conv(v_ref, 2)
+        qc_ref[span, :] = qc
+        kc_ref[span, :] = kc
+        vc_ref[span, :] = vc
+        gated = (kc.astype(jnp.float32) * vc.astype(jnp.float32)).astype(jnp.bfloat16)
+        grad_mixed = (g_ref[span, :].astype(jnp.float32) * qc.astype(jnp.float32)).astype(jnp.bfloat16)
+        dest = pl.ds(pl.multiple_of(step * per_chunk, per_chunk), per_chunk)
+        out_ref[dest, :chan_dev, :] = gated.reshape(per_chunk, chan_dev, cols)
+        out_ref[dest, chan_dev:, :] = grad_mixed.reshape(per_chunk, chan_dev, cols)
+        return carry
+
+    lax.fori_loop(0, rows // chunk, body, 0)
 
 
 def front(query_proj, key_proj, value_proj, grad_out, halo, taps_cols, chan_dev):
@@ -156,9 +163,10 @@
         grid=(all_chans // block,),
         in_specs=[tile, tile, tile, tile, pl.BlockSpec((block, 6), lambda i: (i, 0)),
                   pl.BlockSpec((block, 3), lambda i: (i, 0))],
-        out_specs=[tile, tile, tile, pl.BlockSpec((2 * block, tok_cols), lambda i: (i, 0))],
+        out_specs=[tile, tile, tile,
+                   pl.BlockSpec((block // chan_dev, 2 * chan_dev, tok_cols), lambda i: (i, 0, 0))],
         out_shape=[jax.ShapeDtypeStruct((all_chans, tok_cols), jnp.bfloat16)] * 3
-        + [jax.ShapeDtypeStruct((2 * all_chans, tok_cols), jnp.bfloat16)],
+        + [jax.ShapeDtypeStruct((all_chans // chan_dev, 2 * chan_dev, tok_cols), jnp.bfloat16)],
         cost_estimate=pl.CostEstimate(flops=30 * all_chans * tok_cols, transcendentals=0,
                                       bytes_accessed=18 * all_chans * tok_cols),
     )(query_proj, key_proj, value_proj, grad_out, halo, taps_cols)
@@ -205,6 +213,7 @@
     query_conv, key_conv, value_conv, outgoing = front(
         query_proj, key_proj, value_proj, grad_out, halo, short_taps.T, chan_dev
     )
+    outgoing = outgoing.reshape(2 * all_chans, tok_cols)
     filter_spec = forward_spectrum(filters.astype(jnp.float32), None, tables)
     filter_real = filter_spec[:, None, :, :inner]
     filter_imag = filter_spec[:, None, :, inner:]
@@ -265,18 +274,25 @@
     grad_qconv, grad_kconv, grad_vconv = lax.optimization_barrier(
         (grad_qconv, grad_kconv, grad_vconv)
     )
+    zero_tail = jnp.zeros((all_chans, 2), jnp.float32)
+    interior = lax.optimization_barrier(
+        tuple(
+            taps_backward(part.astype(jnp.float32), zero_tail, short_taps).astype(jnp.bfloat16)
+            for part in (grad_qconv, grad_kconv, grad_vconv)
+        )
+    )
     heads = jnp.concatenate([grad_qconv[:, :2], grad_kconv[:, :2], grad_vconv[:, :2]], axis=1)
-    heads = shifted(heads, "ctx", -1)
-    following = (heads[:, 0:2], heads[:, 2:4], heads[:, 4:6])
-    grad_query = taps_backward(
-        grad_qconv.astype(jnp.float32), following[0].astype(jnp.float32) * keep_next, short_taps
-    ).astype(jnp.bfloat16)
-    grad_key = taps_backward(
-        grad_kconv.astype(jnp.float32), following[1].astype(jnp.float32) * keep_next, short_taps
-    ).astype(jnp.bfloat16)
-    grad_value = taps_backward(
-        grad_vconv.astype(jnp.float32), following[2].astype(jnp.float32) * keep_next, short_taps
-    ).astype(jnp.bfloat16)
+    heads = shifted(heads, "ctx", -1).astype(jnp.float32) * keep_next
+
+    def patched(whole, part, slot):
+        edge = taps_backward(
+            part[:, -2:].astype(jnp.float32), heads[:, 2 * slot : 2 * slot + 2], short_taps
+        ).astype(jnp.bfloat16)
+        return lax.dynamic_update_slice(whole, edge, (0, tok_cols - 2))
+
+    grad_query = patched(interior[0], grad_qconv, 0)
+    grad_key = patched(interior[1], grad_kconv, 1)
+    grad_value = patched(interior[2], grad_vconv, 2)
     return (grad_query, grad_key, grad_value, grad_filters)
 
 

time: 229 us -> 242 us (1.057)
  local copies, waits for them, and re-layouts: 14.3 us -> 29.2 us
    all_to_all x1, waiting for transfers between devices: 41.7 us -> 7.75 us  [per_device(): lax.all_to_all(returning, 'ctx', split_axis=1, concat_axis=0, tiled=True)]
    ppermute x3, waiting for transfers between devices: 0.01 us -> 33.8 us  [ring_scatter_sum(): total = total + lax.ppermute(piece, axis, pairs)]
    dynamic_update_slice x0 -> x3, local copies, waits for them, and re-layouts: none -> 10.9 us  [patched(): return lax.dynamic_update_slice(whole, edge, (0, tok_cols - 2))]
    unnamed x54 -> x67, local copies, waits for them, and re-layouts: 3.22 us -> 5.02 us
    convert_element_type x4 -> x8, other arithmetic: 5.35 us -> 3.89 us  [the longest x1 3.55 us: per_device(): taps_backward(part.astype(jnp.float32), zero_tail, short_taps)]
  transfers between devices with their start and end apart: 7 -> 7, of which waited for: 4 -> 5; matrix products, arithmetic and copies ran while one was open for 6% -> 7% of each run, Pallas kernels for 0% -> 0%
where the time goes in v3:
time: 242 us; the launch traced here: 241 us
  waiting for transfers between devices  109 us (45%)
  starting transfers between devices  68.5 us (28%)
  local copies, waits for them, and re-layouts  29.2 us (12%)
  other arithmetic  16.1 us (7%)
  matrix products  9.66 us (4%)
  Pallas kernels  6.7 us (3%)
    all_to_all x1, waiting for transfers between devices, per_device(): lax.all_to_all(outgoing, 'ctx', split_axis=0, concat_axis=1, tiled=True)  40.3 us
    all_to_all x1, starting transfers between devices, per_device(): lax.all_to_all(outgoing, 'ctx', split_axis=0, concat_axis=1, tiled=True)  35.9 us
    ppermute x3, waiting for transfers between devices, ring_scatter_sum(): total = total + lax.ppermute(piece, axis, pairs)  33.8 us
    ppermute x2, waiting for transfers between devices, shifted(): return lax.ppermute(array, axis, pairs)  27.1 us
    ppermute x2, starting transfers between devices, shifted(): return lax.ppermute(array, axis, pairs)  11.9 us
    all_to_all x1, starting transfers between devices, per_device(): lax.all_to_all(returning, 'ctx', split_axis=1, concat_axis=0, tiled=True)  11.6 us
    dynamic_update_slice x3, local copies, waits for them, and re-layouts, patched(): return lax.dynamic_update_slice(whole, edge, (0, tok_cols - 2))  10.9 us
    ppermute x3, starting transfers between devices, ring_scatter_sum(): total = total + lax.ppermute(piece, axis, pairs)  9.13 us
  transfers between devices with their start and end apart: 7, of which 5 were waited for; matrix products, arithmetic and copies ran while one was open for 7% of the time, Pallas kernels for 0%

profile of v3, /device:TPU:25, one launch (start us, length us, event | category | flops | bytes accessed | tf_op | source)
XLA Modules:
  0.0 240.6 jit_solution(10066397897490216100)
XLA Ops:
  0.7 1.3 slice.187
  2.2 1.3 slice.188
  4.5 9.0 %collective-permute-start = (bf16[2048,6]{1,0:T(8,128)(2,1)S(1)}, bf16[2048,6]{1,0:T(8,128)(2,1)S(1)}, u32[]{:S(2)}, u32[]{:S(2)}) collective-permute-start(bf16[2048,6]{1,0:T(8,128)(2,1)S(1)} %copy.149), channel_id=1, source_target_pairs={{0,1},{1,2},{2,3},{3,4},{4,5},{5,6},{6,7},{7,8},{8,9},{9,10},{10,1... | collective-permute-start | bytes 73736 | tf_op jit(solution)/shard_map/ppermute | solution.py:18
  13.6 1.3 copy.150
  14.9 6.5 %collective-permute-done = bf16[2048,6]{1,0:T(8,128)(2,1)S(1)} collective-permute-done((bf16[2048,6]{1,0:T(8,128)(2,1)S(1)}, bf16[2048,6]{1,0:T(8,128)(2,1)S(1)}, u32[]{:S(2)}, u32[]{:S(2)}) %collective-permute-start) | collective-permute-done | bytes 24608 | tf_op jit(solution)/shard_map/ppermute | solution.py:18
  22.2 6.7 %shard_map.93 = (bf16[2048,128]{1,0:T(8,128)(2,1)}, bf16[2048,128]{1,0:T(8,128)(2,1)}, bf16[2048,128]{1,0:T(8,128)(2,1)}, bf16[128,32,128]{2,1,0:T(8,128)(2,1)}) custom-call(bf16[2048,128]{1,0:T(8,128)(2,1)} %q_ref.1, bf16[2048,128]{1,0:T(8,128)(2,1)} %k_ref.1, bf16[2048,128]{1,0:T(8,128)(2,1)} %v_ref.1, bf16[2048,128]{1,0:T(8,128)(2,1)} %g_ref.1, ...), custom_call_target="tpu_custom_call" | custom-call | flops 7864320 | bytes 4718592 | tf_op jit(solution)/shard_map/pallas_call | solution.py:161
  28.9 35.9 %all-to-all-start = ((bf16[128,32,128]{2,1,0:T(8,128)(2,1)}), bf16[128,32,128]{2,1,0:T(8,128)(2,1)S(1)}, u32[]{:S(2)}, u32[]{:S(2)}) async-start(bf16[128,32,128]{2,1,0:T(8,128)(2,1)} %get-tuple-element.13), calls=%async_computation | async-start | bytes 2097152 | tf_op jit(solution)/shard_map/all_to_all | solution.py:244
  66.1 1.2 fusion.120
  70.0 1.1 fusion.127
  71.2 1.2 fusion.122
  72.4 1.2 fusion.124
  73.7 40.3 %all-to-all-done = bf16[128,32,128]{2,1,0:T(8,128)(2,1)S(1)} async-done(((bf16[128,32,128]{2,1,0:T(8,128)(2,1)}), bf16[128,32,128]{2,1,0:T(8,128)(2,1)S(1)}, u32[]{:S(2)}, u32[]{:S(2)}) %all-to-all-start) | async-done | bytes 1048608 | tf_op jit(solution)/shard_map/all_to_all | solution.py:244
  115.0 1.0 copy.163
  121.7 1.0 fusion.25
  122.7 1.3 fusion.22
  124.8 1.0 fusion.15
  125.9 1.0 fusion.4
  128.0 1.1 fusion.43
  129.1 1.1 fusion.40
  130.4 1.7 copy.171
  132.1 11.6 %all-to-all-start.1 = ((bf16[32,128,128]{2,0,1:T(8,128)(2,1)}), bf16[32,128,128]{2,0,1:T(8,128)(2,1)S(1)}, u32[]{:S(2)}, u32[]{:S(2)}) async-start(bf16[32,128,128]{2,0,1:T(8,128)(2,1)} %copy.171), calls=%async_computation.1 | async-start | bytes 2097152 | tf_op jit(solution)/shard_map/all_to_all | solution.py:256
  144.9 2.1 collective-permute-start.2
  147.0 3.0 %collective-permute-start.3 = (f32[1,4096]{1,0:T(1,128)S(1)}, f32[1,4096]{1,0:T(1,128)S(1)}, u32[]{:S(2)}, u32[]{:S(2)}) collective-permute-start(f32[1,4096]{1,0:T(1,128)S(1)} %get-tuple-element.75), channel_id=1, source_target_pairs={{0,256},{128,384},{256,0},{384,128},{1,257},{129,385},{257,1},{385... | collective-permute-start | bytes 49160 | tf_op jit(solution)/shard_map/ppermute | solution.py:30
  150.1 4.0 %collective-permute-start.4 = (f32[1,4096]{1,0:T(1,128)S(1)}, f32[1,4096]{1,0:T(1,128)S(1)}, u32[]{:S(2)}, u32[]{:S(2)}) collective-permute-start(f32[1,4096]{1,0:T(1,128)S(1)} %get-tuple-element.74), channel_id=1, source_target_pairs={{0,384},{128,0},{256,128},{384,256},{1,385},{129,1},{257,129},{385... | collective-permute-start | bytes 49160 | tf_op jit(solution)/shard_map/ppermute | solution.py:30
  154.2 33.8 %collective-permute-done.2 = f32[1,4096]{1,0:T(1,128)S(1)} collective-permute-done((f32[1,4096]{1,0:T(1,128)S(1)}, f32[1,4096]{1,0:T(1,128)S(1)}, u32[]{:S(2)}, u32[]{:S(2)}) %collective-permute-start.2) | collective-permute-done | bytes 16416 | tf_op jit(solution)/shard_map/ppermute | solution.py:30
  188.6 7.7 %all-to-all-done.1 = bf16[32,128,128]{2,0,1:T(8,128)(2,1)S(1)} async-done(((bf16[32,128,128]{2,0,1:T(8,128)(2,1)}), bf16[32,128,128]{2,0,1:T(8,128)(2,1)S(1)}, u32[]{:S(2)}, u32[]{:S(2)}) %all-to-all-start.1) | async-done | bytes 1048608 | tf_op jit(solution)/shard_map/all_to_all | solution.py:256
  198.4 2.8 %collective-permute-start.1 = (bf16[2048,6]{1,0:T(8,128)(2,1)S(1)}, bf16[2048,6]{1,0:T(8,128)(2,1)S(1)}, u32[]{:S(2)}, u32[]{:S(2)}) collective-permute-start(bf16[2048,6]{1,0:T(8,128)(2,1)S(1)} %pad_maximum_fusion.3), channel_id=1, source_target_pairs={{1,0},{2,1},{3,2},{4,3},{5,4},{6,5},{7,6},{8,7},{9,8},{10,9},{11,1... | collective-permute-start | bytes 73736 | tf_op jit(solution)/shard_map/ppermute | solution.py:18
  201.2 3.5 %fusion.61 = (bf16[2048,128]{1,0:T(8,128)(2,1)}, bf16[2048,128]{1,0:T(8,128)(2,1)}, bf16[2048,128]{1,0:T(8,128)(2,1)}) fusion(f32[2048,128]{1,0:T(8,128)S(1)} %convert_element_type.230, f32[2048]{0:T(1024)S(1)} %bitcast.119, f32[2048]{0:T(1024)S(1)} %bitcast.121, f32[2048]{0:T(1024)S(1)} %bitcast.117, f32[2048,128]{1,0:T(8,128)S(1)} %convert_element_type.228, ...), kind=kLoop, calls=%fused_computation.59 | loop fusion | flops 4718592 | bytes 4743168 | tf_op jit(solution)/shard_map/convert_element_type | solution.py:280
  205.5 20.6 %collective-permute-done.1 = bf16[2048,6]{1,0:T(8,128)(2,1)S(1)} collective-permute-done((bf16[2048,6]{1,0:T(8,128)(2,1)S(1)}, bf16[2048,6]{1,0:T(8,128)(2,1)S(1)}, u32[]{:S(2)}, u32[]{:S(2)}) %collective-permute-start.1) | collective-permute-done | bytes 24608 | tf_op jit(solution)/shard_map/ppermute | solution.py:18
  228.9 3.6 %dynamic_update_slice.11 = bf16[2048,128]{1,0:T(8,128)(2,1)S(1)} dynamic-update-slice(bf16[2048,128]{1,0:T(8,128)(2,1)S(1)} %copy-done.19, bf16[2048,2]{1,0:T(8,128)(2,1)S(1)} %copy.180, s32[]{:T(128)} %constant.90.clone.1, s32[]{:T(128)} %constant.107.clone.1) | dynamic-update-slice | bytes 16388 | tf_op jit(solution)/shard_map/dynamic_update_slice | solution.py:291
  232.5 3.6 %dynamic_update_slice.10 = bf16[2048,128]{1,0:T(8,128)(2,1)S(1)} dynamic-update-slice(bf16[2048,128]{1,0:T(8,128)(2,1)S(1)} %copy-done.17, bf16[2048,2]{1,0:T(8,128)(2,1)S(1)} %copy.177, s32[]{:T(128)} %constant.90.clone.1, s32[]{:T(128)} %constant.107.clone.1) | dynamic-update-slice | bytes 16388 | tf_op jit(solution)/shard_map/dynamic_update_slice | solution.py:291
  236.2 3.6 %dynamic_update_slice.9 = bf16[2048,128]{1,0:T(8,128)(2,1)S(1)} dynamic-update-slice(bf16[2048,128]{1,0:T(8,128)(2,1)S(1)} %copy-done.15, bf16[2048,2]{1,0:T(8,128)(2,1)S(1)} %copy.174, s32[]{:T(128)} %constant.90.clone.1, s32[]{:T(128)} %constant.107.clone.1) | dynamic-update-slice | bytes 16388 | tf_op jit(solution)/shard_map/dynamic_update_slice | solution.py:291
  (131 shorter events, 22.7 us)
Async XLA Ops:
  0.6 64.2 %copy-start = (bf16[1,16384]{1,0:T(2,128)(2,1)S(1)}, bf16[1,16384]{1,0:T(2,128)(2,1)}, u32[]{:S(2)}) copy-start(bf16[1,16384]{1,0:T(2,128)(2,1)} %param.10) | copy-start | bytes 98308
  0.6 3.0 %copy-start.5 = (bf16[2048,128]{1,0:T(8,128)(2,1)S(1)}, bf16[2048,128]{1,0:T(8,128)(2,1)}, u32[]{:S(2)}) copy-start(bf16[2048,128]{1,0:T(8,128)(2,1)} %v_ref.1) | copy-start | bytes 1572868
  2.0 11.6 %copy-start.27 = (f32[3,2048]{1,0:T(4,128)S(1)}, f32[3,2048]{1,0:T(4,128)}, u32[]{:S(2)}) copy-start(f32[3,2048]{1,0:T(4,128)} %param.11) | copy-start | bytes 73732
  4.5 16.9 %collective-permute-start = (bf16[2048,6]{1,0:T(8,128)(2,1)S(1)}, bf16[2048,6]{1,0:T(8,128)(2,1)S(1)}, u32[]{:S(2)}, u32[]{:S(2)}) collective-permute-start(bf16[2048,6]{1,0:T(8,128)(2,1)S(1)} %copy.149), channel_id=1, source_target_pairs={{0,1},{1,2},{2,3},{3,4},{4,5},{5,6},{6,7},{7,8},{8,9},{9,10},{10,1... | collective-permute-start | bytes 73736 | tf_op jit(solution)/shard_map/ppermute | solution.py:18
  28.9 85.1 %all-to-all-start = ((bf16[128,32,128]{2,1,0:T(8,128)(2,1)}), bf16[128,32,128]{2,1,0:T(8,128)(2,1)S(1)}, u32[]{:S(2)}, u32[]{:S(2)}) async-start(bf16[128,32,128]{2,1,0:T(8,128)(2,1)} %get-tuple-element.13), calls=%async_computation | async-start | bytes 2097152 | tf_op jit(solution)/shard_map/all_to_all | solution.py:244
  67.3 46.7 %copy-start.2 = (f32[128,256]{1,0:T(8,128)}, f32[128,256]{1,0:T(8,128)S(1)}, u32[]{:S(2)}) copy-start(f32[128,256]{1,0:T(8,128)S(1)} %get-tuple-element.88) | copy-start | bytes 393220
  117.6 1.0 copy-start.6
  117.6 1.2 copy-start.7
  117.8 1.0 copy-start.3
  117.8 1.1 copy-start.10
  120.0 1.0 copy-start.8
  120.0 1.0 copy-start.9
  122.7 1.3 copy-start.11
  122.7 1.3 copy-start.12
  130.3 13.4 %copy-start.22 = (f32[256,128]{0,1:T(8,128)S(1)}, f32[256,128]{0,1:T(8,128)}, u32[]{:S(2)}) copy-start(f32[256,128]{0,1:T(8,128)} %fusion.127) | copy-start | bytes 393220
  130.3 13.4 %copy-start.24 = (f32[256,128]{0,1:T(8,128)S(1)}, f32[256,128]{0,1:T(8,128)}, u32[]{:S(2)}) copy-start(f32[256,128]{0,1:T(8,128)} %get-tuple-element.95) | copy-start | bytes 393220
  130.3 13.4 %copy-start.26 = (f32[256,128]{0,1:T(8,128)S(1)}, f32[256,128]{0,1:T(8,128)}, u32[]{:S(2)}) copy-start(f32[256,128]{0,1:T(8,128)} %get-tuple-element.96) | copy-start | bytes 393220
  132.1 22.1 %copy-start.28 = (f32[3,2048]{1,0:T(4,128)S(1)}, f32[3,2048]{1,0:T(4,128)}, u32[]{:S(2)}) copy-start(f32[3,2048]{1,0:T(4,128)} %param.11) | copy-start | bytes 73732
  132.1 64.3 %all-to-all-start.1 = ((bf16[32,128,128]{2,0,1:T(8,128)(2,1)}), bf16[32,128,128]{2,0,1:T(8,128)(2,1)S(1)}, u32[]{:S(2)}, u32[]{:S(2)}) async-start(bf16[32,128,128]{2,0,1:T(8,128)(2,1)} %copy.171), calls=%async_computation.1 | async-start | bytes 2097152 | tf_op jit(solution)/shard_map/all_to_all | solution.py:256
  143.8 52.7 %copy-start.4 = (bf16[2048,128]{1,0:T(8,128)(2,1)S(1)}, bf16[2048,128]{1,0:T(8,128)(2,1)}, u32[]{:S(2)}) copy-start(bf16[2048,128]{1,0:T(8,128)(2,1)} %g_ref.1) | copy-start | bytes 1572868
  144.9 51.8 %copy-start.13 = (bf16[2048,128]{1,0:T(8,128)(2,1)S(1)}, bf16[2048,128]{1,0:T(8,128)(2,1)}, u32[]{:S(2)}) copy-start(bf16[2048,128]{1,0:T(8,128)(2,1)} %get-tuple-element.15) | copy-start | bytes 1572868
  144.9 51.8 %copy-start.14 = (bf16[2048,128]{1,0:T(8,128)(2,1)S(1)}, bf16[2048,128]{1,0:T(8,128)(2,1)}, u32[]{:S(2)}) copy-start(bf16[2048,128]{1,0:T(8,128)(2,1)} %get-tuple-element.14) | copy-start | bytes 1572868
  144.9 43.0 %collective-permute-start.2 = (f32[1,4096]{1,0:T(1,128)S(1)}, f32[1,4096]{1,0:T(1,128)S(1)}, u32[]{:S(2)}, u32[]{:S(2)}) collective-permute-start(f32[1,4096]{1,0:T(1,128)S(1)} %get-tuple-element.73), channel_id=1, source_target_pairs={{0,128},{128,256},{256,384},{384,0},{1,129},{129,257},{257,385},{3... | collective-permute-start | bytes 49160 | tf_op jit(solution)/shard_map/ppermute | solution.py:30
  147.0 40.9 %collective-permute-start.3 = (f32[1,4096]{1,0:T(1,128)S(1)}, f32[1,4096]{1,0:T(1,128)S(1)}, u32[]{:S(2)}, u32[]{:S(2)}) collective-permute-start(f32[1,4096]{1,0:T(1,128)S(1)} %get-tuple-element.75), channel_id=1, source_target_pairs={{0,256},{128,384},{256,0},{384,128},{1,257},{129,385},{257,1},{385... | collective-permute-start | bytes 49160 | tf_op jit(solution)/shard_map/ppermute | solution.py:30
  150.1 37.9 %collective-permute-start.4 = (f32[1,4096]{1,0:T(1,128)S(1)}, f32[1,4096]{1,0:T(1,128)S(1)}, u32[]{:S(2)}, u32[]{:S(2)}) collective-permute-start(f32[1,4096]{1,0:T(1,128)S(1)} %get-tuple-element.74), channel_id=1, source_target_pairs={{0,384},{128,0},{256,128},{384,256},{1,385},{129,1},{257,129},{385... | collective-permute-start | bytes 49160 | tf_op jit(solution)/shard_map/ppermute | solution.py:30
  198.4 27.7 %collective-permute-start.1 = (bf16[2048,6]{1,0:T(8,128)(2,1)S(1)}, bf16[2048,6]{1,0:T(8,128)(2,1)S(1)}, u32[]{:S(2)}, u32[]{:S(2)}) collective-permute-start(bf16[2048,6]{1,0:T(8,128)(2,1)S(1)} %pad_maximum_fusion.3), channel_id=1, source_target_pairs={{1,0},{2,1},{3,2},{4,3},{5,4},{6,5},{7,6},{8,7},{9,8},{10,9},{11,1... | collective-permute-start | bytes 73736 | tf_op jit(solution)/shard_map/ppermute | solution.py:18
  227.1 1.8 copy-start.19
  227.5 5.1 %copy-start.17 = (bf16[2048,128]{1,0:T(8,128)(2,1)S(1)}, bf16[2048,128]{1,0:T(8,128)(2,1)}, u32[]{:S(2)}) copy-start(bf16[2048,128]{1,0:T(8,128)(2,1)} %get-tuple-element.20) | copy-start | bytes 1572868
  227.8 8.4 %copy-start.15 = (bf16[2048,128]{1,0:T(8,128)(2,1)S(1)}, bf16[2048,128]{1,0:T(8,128)(2,1)}, u32[]{:S(2)}) copy-start(bf16[2048,128]{1,0:T(8,128)(2,1)} %get-tuple-element.19) | copy-start | bytes 1572868
  228.2 12.4 %copy-start.1 = (bf16[1,16384]{1,0:T(2,128)(2,1)S(1)}, bf16[1,16384]{1,0:T(2,128)(2,1)}, u32[]{:S(2)}) copy-start(bf16[1,16384]{1,0:T(2,128)(2,1)} %param.10) | copy-start | bytes 98308
  232.5 7.3 %copy-start.20 = (bf16[2048,128]{1,0:T(8,128)(2,1)}, bf16[2048,128]{1,0:T(8,128)(2,1)S(1)}, u32[]{:S(2)}) copy-start(bf16[2048,128]{1,0:T(8,128)(2,1)S(1)} %dynamic_update_slice.11) | copy-start | bytes 1572868
  236.2 3.6 %copy-start.18 = (bf16[2048,128]{1,0:T(8,128)(2,1)}, bf16[2048,128]{1,0:T(8,128)(2,1)S(1)}, u32[]{:S(2)}) copy-start(bf16[2048,128]{1,0:T(8,128)(2,1)S(1)} %dynamic_update_slice.10) | copy-start | bytes 1572868
  (4 other events, 3.7 us)

commit v4 on v3

--- a/solution.py
+++ b/solution.py
@@ -284,11 +284,14 @@
     heads = jnp.concatenate([grad_qconv[:, :2], grad_kconv[:, :2], grad_vconv[:, :2]], axis=1)
     heads = shifted(heads, "ctx", -1).astype(jnp.float32) * keep_next
 
+    lane = lax.broadcasted_iota(jnp.int32, (all_chans, tok_cols), 1)
+
     def patched(whole, part, slot):
         edge = taps_backward(
             part[:, -2:].astype(jnp.float32), heads[:, 2 * slot : 2 * slot + 2], short_taps
         ).astype(jnp.bfloat16)
-        return lax.dynamic_update_slice(whole, edge, (0, tok_cols - 2))
+        edge = jnp.pad(edge, ((0, 0), (tok_cols - 2, 0)))
+        return jnp.where(lane >= tok_cols - 2, edge, whole)
 
     grad_query = patched(interior[0], grad_qconv, 0)
     grad_key = patched(interior[1], grad_kconv, 1)

time: 242 us -> 234 us (0.967)
  local copies, waits for them, and re-layouts: 29.2 us -> 18.2 us
  other arithmetic: 16.1 us -> 19 us
    dynamic_update_slice x3 -> x0, local copies, waits for them, and re-layouts: 10.9 us -> none  [patched(): return lax.dynamic_update_slice(whole, edge, (0, tok_cols - 2))]
    select_n x0 -> x1, other arithmetic: none -> 2.93 us  [patched(): return jnp.where(lane >= tok_cols - 2, edge, whole)]
    unnamed x67 -> x61, local copies, waits for them, and re-layouts: 5.02 us -> 4.21 us
where the time goes in v4:
time: 234 us; the launch traced here: 232 us
  waiting for transfers between devices  109 us (47%)
  starting transfers between devices  68.3 us (29%)
  other arithmetic  19 us (8%)
  local copies, waits for them, and re-layouts  18.2 us (8%)
  matrix products  9.67 us (4%)
  Pallas kernels  6.7 us (3%)
    all_to_all x1, waiting for transfers between devices, per_device(): lax.all_to_all(outgoing, 'ctx', split_axis=0, concat_axis=1, tiled=True)  40.3 us
    all_to_all x1, starting transfers between devices, per_device(): lax.all_to_all(outgoing, 'ctx', split_axis=0, concat_axis=1, tiled=True)  35.9 us
    ppermute x3, waiting for transfers between devices, ring_scatter_sum(): total = total + lax.ppermute(piece, axis, pairs)  33.7 us
    ppermute x2, waiting for transfers between devices, shifted(): return lax.ppermute(array, axis, pairs)  27.2 us
    ppermute x2, starting transfers between devices, shifted(): return lax.ppermute(array, axis, pairs)  11.9 us
    all_to_all x1, starting transfers between devices, per_device(): lax.all_to_all(returning, 'ctx', split_axis=1, concat_axis=0, tiled=True)  11.4 us
    ppermute x3, starting transfers between devices, ring_scatter_sum(): total = total + lax.ppermute(piece, axis, pairs)  9.13 us
    all_to_all x1, waiting for transfers between devices, per_device(): lax.all_to_all(returning, 'ctx', split_axis=1, concat_axis=0, tiled=True)  7.77 us
  transfers between devices with their start and end apart: 7, of which 5 were waited for; matrix products, arithmetic and copies ran while one was open for 7% of the time, Pallas kernels for 0%

profile of v4, /device:TPU:25, one launch (start us, length us, event | category | flops | bytes accessed | tf_op | source)
XLA Modules:
  0.0 232.5 jit_solution(14994424436928600363)
XLA Ops:
  0.7 1.3 slice.187
  2.2 1.3 slice.188
  4.5 9.0 %collective-permute-start = (bf16[2048,6]{1,0:T(8,128)(2,1)S(1)}, bf16[2048,6]{1,0:T(8,128)(2,1)S(1)}, u32[]{:S(2)}, u32[]{:S(2)}) collective-permute-start(bf16[2048,6]{1,0:T(8,128)(2,1)S(1)} %copy.149), channel_id=1, source_target_pairs={{0,1},{1,2},{2,3},{3,4},{4,5},{5,6},{6,7},{7,8},{8,9},{9,10},{10,1... | collective-permute-start | bytes 73736 | tf_op jit(solution)/shard_map/ppermute | solution.py:18
  13.6 1.3 copy.150
  14.9 6.5 %collective-permute-done = bf16[2048,6]{1,0:T(8,128)(2,1)S(1)} collective-permute-done((bf16[2048,6]{1,0:T(8,128)(2,1)S(1)}, bf16[2048,6]{1,0:T(8,128)(2,1)S(1)}, u32[]{:S(2)}, u32[]{:S(2)}) %collective-permute-start) | collective-permute-done | bytes 24608 | tf_op jit(solution)/shard_map/ppermute | solution.py:18
  22.2 6.7 %shard_map.93 = (bf16[2048,128]{1,0:T(8,128)(2,1)}, bf16[2048,128]{1,0:T(8,128)(2,1)}, bf16[2048,128]{1,0:T(8,128)(2,1)}, bf16[128,32,128]{2,1,0:T(8,128)(2,1)}) custom-call(bf16[2048,128]{1,0:T(8,128)(2,1)} %q_ref.1, bf16[2048,128]{1,0:T(8,128)(2,1)} %k_ref.1, bf16[2048,128]{1,0:T(8,128)(2,1)} %v_ref.1, bf16[2048,128]{1,0:T(8,128)(2,1)} %g_ref.1, ...), custom_call_target="tpu_custom_call" | custom-call | flops 7864320 | bytes 4718592 | tf_op jit(solution)/shard_map/pallas_call | solution.py:161
  28.9 35.9 %all-to-all-start = ((bf16[128,32,128]{2,1,0:T(8,128)(2,1)}), bf16[128,32,128]{2,1,0:T(8,128)(2,1)S(1)}, u32[]{:S(2)}, u32[]{:S(2)}) async-start(bf16[128,32,128]{2,1,0:T(8,128)(2,1)} %get-tuple-element.13), calls=%async_computation | async-start | bytes 2097152 | tf_op jit(solution)/shard_map/all_to_all | solution.py:244
  66.1 1.2 fusion.120
  70.0 1.2 fusion.127
  71.2 1.2 fusion.122
  72.4 1.2 fusion.124
  73.7 40.3 %all-to-all-done = bf16[128,32,128]{2,1,0:T(8,128)(2,1)S(1)} async-done(((bf16[128,32,128]{2,1,0:T(8,128)(2,1)}), bf16[128,32,128]{2,1,0:T(8,128)(2,1)S(1)}, u32[]{:S(2)}, u32[]{:S(2)}) %all-to-all-start) | async-done | bytes 1048608 | tf_op jit(solution)/shard_map/all_to_all | solution.py:244
  115.0 1.0 copy.163
  116.0 1.0 copy.164
  121.7 1.0 fusion.25
  122.7 1.3 fusion.22
  124.8 1.0 fusion.15
  125.9 1.0 fusion.4
  128.0 1.1 fusion.43
  129.1 1.1 fusion.40
  130.4 1.7 copy.171
  132.1 11.4 %all-to-all-start.1 = ((bf16[32,128,128]{2,0,1:T(8,128)(2,1)}), bf16[32,128,128]{2,0,1:T(8,128)(2,1)S(1)}, u32[]{:S(2)}, u32[]{:S(2)}) async-start(bf16[32,128,128]{2,0,1:T(8,128)(2,1)} %copy.171), calls=%async_computation.1 | async-start | bytes 2097152 | tf_op jit(solution)/shard_map/all_to_all | solution.py:256
  144.8 2.1 collective-permute-start.2
  146.9 3.1 %collective-permute-start.3 = (f32[1,4096]{1,0:T(1,128)S(1)}, f32[1,4096]{1,0:T(1,128)S(1)}, u32[]{:S(2)}, u32[]{:S(2)}) collective-permute-start(f32[1,4096]{1,0:T(1,128)S(1)} %get-tuple-element.75), channel_id=1, source_target_pairs={{0,256},{128,384},{256,0},{384,128},{1,257},{129,385},{257,1},{385... | collective-permute-start | bytes 49160 | tf_op jit(solution)/shard_map/ppermute | solution.py:30
  150.0 4.0 %collective-permute-start.4 = (f32[1,4096]{1,0:T(1,128)S(1)}, f32[1,4096]{1,0:T(1,128)S(1)}, u32[]{:S(2)}, u32[]{:S(2)}) collective-permute-start(f32[1,4096]{1,0:T(1,128)S(1)} %get-tuple-element.74), channel_id=1, source_target_pairs={{0,384},{128,0},{256,128},{384,256},{1,385},{129,1},{257,129},{385... | collective-permute-start | bytes 49160 | tf_op jit(solution)/shard_map/ppermute | solution.py:30
  154.0 33.7 %collective-permute-done.2 = f32[1,4096]{1,0:T(1,128)S(1)} collective-permute-done((f32[1,4096]{1,0:T(1,128)S(1)}, f32[1,4096]{1,0:T(1,128)S(1)}, u32[]{:S(2)}, u32[]{:S(2)}) %collective-permute-start.2) | collective-permute-done | bytes 16416 | tf_op jit(solution)/shard_map/ppermute | solution.py:30
  188.4 7.8 %all-to-all-done.1 = bf16[32,128,128]{2,0,1:T(8,128)(2,1)S(1)} async-done(((bf16[32,128,128]{2,0,1:T(8,128)(2,1)}), bf16[32,128,128]{2,0,1:T(8,128)(2,1)S(1)}, u32[]{:S(2)}, u32[]{:S(2)}) %all-to-all-start.1) | async-done | bytes 1048608 | tf_op jit(solution)/shard_map/all_to_all | solution.py:256
  198.2 2.8 %collective-permute-start.1 = (bf16[2048,6]{1,0:T(8,128)(2,1)S(1)}, bf16[2048,6]{1,0:T(8,128)(2,1)S(1)}, u32[]{:S(2)}, u32[]{:S(2)}) collective-permute-start(bf16[2048,6]{1,0:T(8,128)(2,1)S(1)} %pad_maximum_fusion.3), channel_id=1, source_target_pairs={{1,0},{2,1},{3,2},{4,3},{5,4},{6,5},{7,6},{8,7},{9,8},{10,9},{11,1... | collective-permute-start | bytes 73736 | tf_op jit(solution)/shard_map/ppermute | solution.py:18
  201.1 3.5 %fusion.61 = (bf16[2048,128]{1,0:T(8,128)(2,1)}, bf16[2048,128]{1,0:T(8,128)(2,1)}, bf16[2048,128]{1,0:T(8,128)(2,1)}) fusion(f32[2048,128]{1,0:T(8,128)S(1)} %convert_element_type.237, f32[2048]{0:T(1024)S(1)} %bitcast.119, f32[2048]{0:T(1024)S(1)} %bitcast.121, f32[2048]{0:T(1024)S(1)} %bitcast.117, f32[2048,128]{1,0:T(8,128)S(1)} %convert_element_type.235, ...), kind=kLoop, calls=%fused_computation.59 | loop fusion | flops 4718592 | bytes 4743168 | tf_op jit(solution)/shard_map/convert_element_type | solution.py:280
  205.3 20.7 %collective-permute-done.1 = bf16[2048,6]{1,0:T(8,128)(2,1)S(1)} collective-permute-done((bf16[2048,6]{1,0:T(8,128)(2,1)S(1)}, bf16[2048,6]{1,0:T(8,128)(2,1)S(1)}, u32[]{:S(2)}, u32[]{:S(2)}) %collective-permute-start.1) | collective-permute-done | bytes 24608 | tf_op jit(solution)/shard_map/ppermute | solution.py:18
  228.5 1.1 copy.180
  229.5 2.9 %pad_select_fusion = (bf16[2048,128]{1,0:T(8,128)(2,1)}, bf16[2048,128]{1,0:T(8,128)(2,1)}, bf16[2048,128]{1,0:T(8,128)(2,1)}) fusion(bf16[2048,128]{1,0:T(8,128)(2,1)S(1)} %copy-done.5, bf16[2048,2]{1,0:T(8,128)(2,1)} %copy.180, pred[128]{0:T(512)(128)(4,1)S(1)} %iota_compare_fusion, bf16[2048,128]{1,0:T(8,128)(2,1)S(1)} %copy-done.6, ...), kind=kLoop, calls=%fused_computation.96 | loop fusion | flops 786432 | bytes 3170432 | tf_op jit(solution)/shard_map/jit(_where)/select_n | solution.py:294
  (124 shorter events, 20.5 us)
Async XLA Ops:
  0.6 64.2 %copy-start = (bf16[1,16384]{1,0:T(2,128)(2,1)S(1)}, bf16[1,16384]{1,0:T(2,128)(2,1)}, u32[]{:S(2)}) copy-start(bf16[1,16384]{1,0:T(2,128)(2,1)} %param.10) | copy-start | bytes 98308
  0.6 3.0 %copy-start.8 = (bf16[2048,128]{1,0:T(8,128)(2,1)S(1)}, bf16[2048,128]{1,0:T(8,128)(2,1)}, u32[]{:S(2)}) copy-start(bf16[2048,128]{1,0:T(8,128)(2,1)} %v_ref.1) | copy-start | bytes 1572868
  2.0 11.6 %copy-start.24 = (f32[3,2048]{1,0:T(4,128)S(1)}, f32[3,2048]{1,0:T(4,128)}, u32[]{:S(2)}) copy-start(f32[3,2048]{1,0:T(4,128)} %param.11) | copy-start | bytes 73732
  4.5 16.9 %collective-permute-start = (bf16[2048,6]{1,0:T(8,128)(2,1)S(1)}, bf16[2048,6]{1,0:T(8,128)(2,1)S(1)}, u32[]{:S(2)}, u32[]{:S(2)}) collective-permute-start(bf16[2048,6]{1,0:T(8,128)(2,1)S(1)} %copy.149), channel_id=1, source_target_pairs={{0,1},{1,2},{2,3},{3,4},{4,5},{5,6},{6,7},{7,8},{8,9},{9,10},{10,1... | collective-permute-start | bytes 73736 | tf_op jit(solution)/shard_map/ppermute | solution.py:18
  28.9 85.1 %all-to-all-start = ((bf16[128,32,128]{2,1,0:T(8,128)(2,1)}), bf16[128,32,128]{2,1,0:T(8,128)(2,1)S(1)}, u32[]{:S(2)}, u32[]{:S(2)}) async-start(bf16[128,32,128]{2,1,0:T(8,128)(2,1)} %get-tuple-element.13), calls=%async_computation | async-start | bytes 2097152 | tf_op jit(solution)/shard_map/all_to_all | solution.py:244
  67.3 46.7 %copy-start.2 = (f32[128,256]{1,0:T(8,128)}, f32[128,256]{1,0:T(8,128)S(1)}, u32[]{:S(2)}) copy-start(f32[128,256]{1,0:T(8,128)S(1)} %get-tuple-element.91) | copy-start | bytes 393220
  117.6 1.0 copy-start.9
  117.6 1.2 copy-start.10
  117.8 1.0 copy-start.3
  117.8 1.1 copy-start.13
  120.0 1.0 copy-start.11
  120.0 1.0 copy-start.12
  122.7 1.3 copy-start.14
  122.7 1.3 copy-start.15
  126.9 1.0 copy-start.20
  126.9 1.0 copy-start.22
  130.3 13.2 %copy-start.19 = (f32[256,128]{0,1:T(8,128)S(1)}, f32[256,128]{0,1:T(8,128)}, u32[]{:S(2)}) copy-start(f32[256,128]{0,1:T(8,128)} %fusion.127) | copy-start | bytes 393220
  130.3 13.2 %copy-start.21 = (f32[256,128]{0,1:T(8,128)S(1)}, f32[256,128]{0,1:T(8,128)}, u32[]{:S(2)}) copy-start(f32[256,128]{0,1:T(8,128)} %get-tuple-element.98) | copy-start | bytes 393220
  130.4 13.2 %copy-start.23 = (f32[256,128]{0,1:T(8,128)S(1)}, f32[256,128]{0,1:T(8,128)}, u32[]{:S(2)}) copy-start(f32[256,128]{0,1:T(8,128)} %get-tuple-element.99) | copy-start | bytes 393220
  130.4 13.3 %copy-start.25 = (f32[3,2048]{1,0:T(4,128)S(1)}, f32[3,2048]{1,0:T(4,128)}, u32[]{:S(2)}) copy-start(f32[3,2048]{1,0:T(4,128)} %param.11) | copy-start | bytes 73732
  132.1 64.1 %all-to-all-start.1 = ((bf16[32,128,128]{2,0,1:T(8,128)(2,1)}), bf16[32,128,128]{2,0,1:T(8,128)(2,1)S(1)}, u32[]{:S(2)}, u32[]{:S(2)}) async-start(bf16[32,128,128]{2,0,1:T(8,128)(2,1)} %copy.171), calls=%async_computation.1 | async-start | bytes 2097152 | tf_op jit(solution)/shard_map/all_to_all | solution.py:256
  143.7 52.7 %copy-start.4 = (bf16[2048,128]{1,0:T(8,128)(2,1)S(1)}, bf16[2048,128]{1,0:T(8,128)(2,1)}, u32[]{:S(2)}) copy-start(bf16[2048,128]{1,0:T(8,128)(2,1)} %g_ref.1) | copy-start | bytes 1572868
  144.8 51.8 %copy-start.16 = (bf16[2048,128]{1,0:T(8,128)(2,1)S(1)}, bf16[2048,128]{1,0:T(8,128)(2,1)}, u32[]{:S(2)}) copy-start(bf16[2048,128]{1,0:T(8,128)(2,1)} %get-tuple-element.15) | copy-start | bytes 1572868
  144.8 51.8 %copy-start.17 = (bf16[2048,128]{1,0:T(8,128)(2,1)S(1)}, bf16[2048,128]{1,0:T(8,128)(2,1)}, u32[]{:S(2)}) copy-start(bf16[2048,128]{1,0:T(8,128)(2,1)} %get-tuple-element.14) | copy-start | bytes 1572868
  144.8 42.9 %collective-permute-start.2 = (f32[1,4096]{1,0:T(1,128)S(1)}, f32[1,4096]{1,0:T(1,128)S(1)}, u32[]{:S(2)}, u32[]{:S(2)}) collective-permute-start(f32[1,4096]{1,0:T(1,128)S(1)} %get-tuple-element.73), channel_id=1, source_target_pairs={{0,128},{128,256},{256,384},{384,0},{1,129},{129,257},{257,385},{3... | collective-permute-start | bytes 49160 | tf_op jit(solution)/shard_map/ppermute | solution.py:30
  146.9 40.9 %collective-permute-start.3 = (f32[1,4096]{1,0:T(1,128)S(1)}, f32[1,4096]{1,0:T(1,128)S(1)}, u32[]{:S(2)}, u32[]{:S(2)}) collective-permute-start(f32[1,4096]{1,0:T(1,128)S(1)} %get-tuple-element.75), channel_id=1, source_target_pairs={{0,256},{128,384},{256,0},{384,128},{1,257},{129,385},{257,1},{385... | collective-permute-start | bytes 49160 | tf_op jit(solution)/shard_map/ppermute | solution.py:30
  150.0 37.8 %collective-permute-start.4 = (f32[1,4096]{1,0:T(1,128)S(1)}, f32[1,4096]{1,0:T(1,128)S(1)}, u32[]{:S(2)}, u32[]{:S(2)}) collective-permute-start(f32[1,4096]{1,0:T(1,128)S(1)} %get-tuple-element.74), channel_id=1, source_target_pairs={{0,384},{128,0},{256,128},{384,256},{1,385},{129,1},{257,129},{385... | collective-permute-start | bytes 49160 | tf_op jit(solution)/shard_map/ppermute | solution.py:30
  198.2 27.8 %collective-permute-start.1 = (bf16[2048,6]{1,0:T(8,128)(2,1)S(1)}, bf16[2048,6]{1,0:T(8,128)(2,1)S(1)}, u32[]{:S(2)}, u32[]{:S(2)}) collective-permute-start(bf16[2048,6]{1,0:T(8,128)(2,1)S(1)} %pad_maximum_fusion.3), channel_id=1, source_target_pairs={{1,0},{2,1},{3,2},{4,3},{5,4},{6,5},{7,6},{8,7},{9,8},{10,9},{11,1... | collective-permute-start | bytes 73736 | tf_op jit(solution)/shard_map/ppermute | solution.py:18
  227.0 2.5 %copy-start.5 = (bf16[2048,128]{1,0:T(8,128)(2,1)S(1)}, bf16[2048,128]{1,0:T(8,128)(2,1)}, u32[]{:S(2)}) copy-start(bf16[2048,128]{1,0:T(8,128)(2,1)} %get-tuple-element.21) | copy-start | bytes 1572868
  227.0 2.5 %copy-start.6 = (bf16[2048,128]{1,0:T(8,128)(2,1)S(1)}, bf16[2048,128]{1,0:T(8,128)(2,1)}, u32[]{:S(2)}) copy-start(bf16[2048,128]{1,0:T(8,128)(2,1)} %get-tuple-element.20) | copy-start | bytes 1572868
  227.4 2.2 copy-start.7
  228.5 4.0 %copy-start.1 = (bf16[1,16384]{1,0:T(2,128)(2,1)S(1)}, bf16[1,16384]{1,0:T(2,128)(2,1)}, u32[]{:S(2)}) copy-start(bf16[1,16384]{1,0:T(2,128)(2,1)} %param.10) | copy-start | bytes 98308
  (1 other events, 0.9 us)

commit v5 on v1

--- a/solution.py
+++ b/solution.py
@@ -113,7 +113,7 @@
     return values.reshape(row_count, length)
 
 
-BLOCK_ROWS = 256
+BLOCK_ROWS = 1024
 
 
 def front_kernel(chan_dev, q_ref, k_ref, v_ref, g_ref, halo_ref, taps_ref, qc_ref, kc_ref, vc_ref, out_ref):

time: 229 us -> 227 us (level)
  no operation moved by 1% of the time
where the time goes in v5:
time: 227 us
  waiting for transfers between devices  110 us (48%)
  starting transfers between devices  68.1 us (30%)
  other arithmetic  17.9 us (8%)
  local copies, waits for them, and re-layouts  14.3 us (6%)
  matrix products  9.66 us (4%)
  Pallas kernels  5.78 us (3%)
    all_to_all x1, waiting for transfers between devices, per_device(): lax.all_to_all(returning, 'ctx', split_axis=1, concat_axis=0, tiled=True)  41.7 us
    all_to_all x1, waiting for transfers between devices, per_device(): lax.all_to_all(outgoing, 'ctx', split_axis=0, concat_axis=1, tiled=True)  40.3 us
    all_to_all x1, starting transfers between devices, per_device(): lax.all_to_all(outgoing, 'ctx', split_axis=0, concat_axis=1, tiled=True)  35.9 us
    ppermute x2, waiting for transfers between devices, shifted(): return lax.ppermute(array, axis, pairs)  27.5 us
    ppermute x2, starting transfers between devices, shifted(): return lax.ppermute(array, axis, pairs)  11.6 us
    all_to_all x1, starting transfers between devices, per_device(): lax.all_to_all(returning, 'ctx', split_axis=1, concat_axis=0, tiled=True)  11.6 us
    ppermute x3, starting transfers between devices, ring_scatter_sum(): total = total + lax.ppermute(piece, axis, pairs)  9 us
    pallas_call x1, Pallas kernels, front(): pl.pallas_call(functools.partial(front_kernel, chan_dev), grid=(all_chans...  5.78 us
  transfers between devices with their start and end apart: 7, of which 4 were waited for; matrix products, arithmetic and copies ran while one was open for 6% of the time, Pallas kernels for 0%

profile of v5, /device:TPU:25, one launch (start us, length us, event | category | flops | bytes accessed | tf_op | source)
XLA Modules:
  0.0 226.7 jit_solution(11215309927668680949)
XLA Ops:
  0.7 1.3 slice.160
  2.2 1.3 slice.161
  4.5 9.0 %collective-permute-start = (bf16[2048,6]{1,0:T(8,128)(2,1)S(1)}, bf16[2048,6]{1,0:T(8,128)(2,1)S(1)}, u32[]{:S(2)}, u32[]{:S(2)}) collective-permute-start(bf16[2048,6]{1,0:T(8,128)(2,1)S(1)} %copy.85), channel_id=1, source_target_pairs={{0,1},{1,2},{2,3},{3,4},{4,5},{5,6},{6,7},{7,8},{8,9},{9,10},{10,1... | collective-permute-start | bytes 73736 | tf_op jit(solution)/shard_map/ppermute | solution.py:18
  13.6 1.4 copy.86
  14.9 6.5 %collective-permute-done = bf16[2048,6]{1,0:T(8,128)(2,1)S(1)} collective-permute-done((bf16[2048,6]{1,0:T(8,128)(2,1)S(1)}, bf16[2048,6]{1,0:T(8,128)(2,1)S(1)}, u32[]{:S(2)}, u32[]{:S(2)}) %collective-permute-start) | collective-permute-done | bytes 24608 | tf_op jit(solution)/shard_map/ppermute | solution.py:18
  21.4 0.8 broadcast_select_fusion.halo_ref
  22.2 5.8 %shard_map.93 = (bf16[2048,128]{1,0:T(8,128)(2,1)}, bf16[2048,128]{1,0:T(8,128)(2,1)}, bf16[2048,128]{1,0:T(8,128)(2,1)}, bf16[4096,128]{1,0:T(8,128)(2,1)}) custom-call(bf16[2048,128]{1,0:T(8,128)(2,1)} %q_ref.1, bf16[2048,128]{1,0:T(8,128)(2,1)} %k_ref.1, bf16[2048,128]{1,0:T(8,128)(2,1)} %v_ref.1, bf16[2048,128]{1,0:T(8,128)(2,1)} %g_ref.1, ...), custom_call_target="tpu_custom_call" | custom-call | flops 7864320 | bytes 4718592 | tf_op jit(solution)/shard_map/pallas_call | solution.py:154
  28.0 35.9 %all-to-all-start = ((bf16[128,32,128]{2,1,0:T(8,128)(2,1)}), bf16[128,32,128]{2,1,0:T(8,128)(2,1)S(1)}, u32[]{:S(2)}, u32[]{:S(2)}) async-start(bf16[128,32,128]{2,1,0:T(8,128)(2,1)} %bitcast.120), calls=%async_computation | async-start | bytes 2097152 | tf_op jit(solution)/shard_map/all_to_all | solution.py:235
  65.2 1.2 fusion.123
  69.1 1.2 fusion.130
  70.3 1.3 fusion.125
  71.5 1.2 fusion.127
  72.8 40.3 %all-to-all-done = bf16[128,32,128]{2,1,0:T(8,128)(2,1)S(1)} async-done(((bf16[128,32,128]{2,1,0:T(8,128)(2,1)}), bf16[128,32,128]{2,1,0:T(8,128)(2,1)S(1)}, u32[]{:S(2)}, u32[]{:S(2)}) %all-to-all-start) | async-done | bytes 1048608 | tf_op jit(solution)/shard_map/all_to_all | solution.py:235
  114.1 1.0 copy.100
  115.1 1.0 copy.99
  118.0 1.0 fusion.69
  119.1 1.0 fusion.70
  120.7 1.0 fusion.25
  121.8 1.3 fusion.22
  123.9 1.0 fusion.15
  125.0 1.0 fusion.4
  127.0 1.1 fusion.43
  128.1 1.1 fusion.40
  129.4 1.7 copy.107
  131.1 11.6 %all-to-all-start.1 = ((bf16[32,128,128]{2,0,1:T(8,128)(2,1)}), bf16[32,128,128]{2,0,1:T(8,128)(2,1)S(1)}, u32[]{:S(2)}, u32[]{:S(2)}) async-start(bf16[32,128,128]{2,0,1:T(8,128)(2,1)} %copy.107), calls=%async_computation.1 | async-start | bytes 2097152 | tf_op jit(solution)/shard_map/all_to_all | solution.py:247
  144.7 1.9 collective-permute-start.2
  146.6 3.0 %collective-permute-start.3 = (f32[1,4096]{1,0:T(1,128)S(1)}, f32[1,4096]{1,0:T(1,128)S(1)}, u32[]{:S(2)}, u32[]{:S(2)}) collective-permute-start(f32[1,4096]{1,0:T(1,128)S(1)} %get-tuple-element.63), channel_id=1, source_target_pairs={{0,256},{128,384},{256,0},{384,128},{1,257},{129,385},{257,1},{385... | collective-permute-start | bytes 49160 | tf_op jit(solution)/shard_map/ppermute | solution.py:30
  149.6 4.0 %collective-permute-start.4 = (f32[1,4096]{1,0:T(1,128)S(1)}, f32[1,4096]{1,0:T(1,128)S(1)}, u32[]{:S(2)}, u32[]{:S(2)}) collective-permute-start(f32[1,4096]{1,0:T(1,128)S(1)} %get-tuple-element.62), channel_id=1, source_target_pairs={{0,384},{128,0},{256,128},{384,256},{1,385},{129,1},{257,129},{385... | collective-permute-start | bytes 49160 | tf_op jit(solution)/shard_map/ppermute | solution.py:30
  153.7 41.7 %all-to-all-done.1 = bf16[32,128,128]{2,0,1:T(8,128)(2,1)S(1)} async-done(((bf16[32,128,128]{2,0,1:T(8,128)(2,1)}), bf16[32,128,128]{2,0,1:T(8,128)(2,1)S(1)}, u32[]{:S(2)}, u32[]{:S(2)}) %all-to-all-start.1) | async-done | bytes 1048608 | tf_op jit(solution)/shard_map/all_to_all | solution.py:247
  196.6 2.6 %collective-permute-start.1 = (bf16[2048,6]{1,0:T(8,128)(2,1)S(1)}, bf16[2048,6]{1,0:T(8,128)(2,1)S(1)}, u32[]{:S(2)}, u32[]{:S(2)}) collective-permute-start(bf16[2048,6]{1,0:T(8,128)(2,1)S(1)} %pad_maximum_fusion.6), channel_id=1, source_target_pairs={{1,0},{2,1},{3,2},{4,3},{5,4},{6,5},{7,6},{8,7},{9,8},{10,9},{11,1... | collective-permute-start | bytes 73736 | tf_op jit(solution)/shard_map/ppermute | solution.py:18
  200.1 21.1 %collective-permute-done.1 = bf16[2048,6]{1,0:T(8,128)(2,1)S(1)} collective-permute-done((bf16[2048,6]{1,0:T(8,128)(2,1)S(1)}, bf16[2048,6]{1,0:T(8,128)(2,1)S(1)}, u32[]{:S(2)}, u32[]{:S(2)}) %collective-permute-start.1) | collective-permute-done | bytes 24608 | tf_op jit(solution)/shard_map/ppermute | solution.py:18
  221.5 5.1 %fusion.52 = (bf16[2048,128]{1,0:T(8,128)(2,1)}, bf16[2048,128]{1,0:T(8,128)(2,1)}, bf16[2048,128]{1,0:T(8,128)(2,1)}) fusion(f32[2048,128]{1,0:T(8,128)S(1)} %convert_element_type.220, f32[2048,2]{1,0:T(8,128)S(1)} %get-tuple-element.42, f32[2048]{0:T(1024)S(1)} %bitcast.126, f32[2048]{0:T(1024)S(1)} %bitcast.127, f32[2048]{0:T(1024)S(1)} %bitcast.125, ...), kind=kLoop, calls=%fused_computation.50 | loop fusion | flops 6291456 | bytes 4792320 | tf_op jit(solution)/shard_map/convert_element_type | solution.py:279
  (101 shorter events, 15.0 us)
Async XLA Ops:
  0.6 63.3 %copy-start = (bf16[1,16384]{1,0:T(2,128)(2,1)S(1)}, bf16[1,16384]{1,0:T(2,128)(2,1)}, u32[]{:S(2)}) copy-start(bf16[1,16384]{1,0:T(2,128)(2,1)} %param.10) | copy-start | bytes 98308
  0.6 3.0 %copy-start.5 = (bf16[2048,128]{1,0:T(8,128)(2,1)S(1)}, bf16[2048,128]{1,0:T(8,128)(2,1)}, u32[]{:S(2)}) copy-start(bf16[2048,128]{1,0:T(8,128)(2,1)} %v_ref.1) | copy-start | bytes 1572868
  2.0 11.6 %copy-start.21 = (f32[3,2048]{1,0:T(4,128)S(1)}, f32[3,2048]{1,0:T(4,128)}, u32[]{:S(2)}) copy-start(f32[3,2048]{1,0:T(4,128)} %param.11) | copy-start | bytes 73732
  4.5 16.9 %collective-permute-start = (bf16[2048,6]{1,0:T(8,128)(2,1)S(1)}, bf16[2048,6]{1,0:T(8,128)(2,1)S(1)}, u32[]{:S(2)}, u32[]{:S(2)}) collective-permute-start(bf16[2048,6]{1,0:T(8,128)(2,1)S(1)} %copy.85), channel_id=1, source_target_pairs={{0,1},{1,2},{2,3},{3,4},{4,5},{5,6},{6,7},{7,8},{8,9},{9,10},{10,1... | collective-permute-start | bytes 73736 | tf_op jit(solution)/shard_map/ppermute | solution.py:18
  28.0 85.1 %all-to-all-start = ((bf16[128,32,128]{2,1,0:T(8,128)(2,1)}), bf16[128,32,128]{2,1,0:T(8,128)(2,1)S(1)}, u32[]{:S(2)}, u32[]{:S(2)}) async-start(bf16[128,32,128]{2,1,0:T(8,128)(2,1)} %bitcast.120), calls=%async_computation | async-start | bytes 2097152 | tf_op jit(solution)/shard_map/all_to_all | solution.py:235
  66.3 46.7 %copy-start.2 = (f32[128,256]{1,0:T(8,128)}, f32[128,256]{1,0:T(8,128)S(1)}, u32[]{:S(2)}) copy-start(f32[128,256]{1,0:T(8,128)S(1)} %get-tuple-element.73) | copy-start | bytes 393220
  116.7 1.0 copy-start.6
  116.7 1.2 copy-start.7
  116.9 1.0 copy-start.3
  116.9 1.1 copy-start.10
  119.1 1.0 copy-start.8
  119.1 1.0 copy-start.9
  121.8 1.3 copy-start.11
  121.8 1.3 copy-start.12
  126.0 0.9 copy-start.15
  126.0 1.0 copy-start.17
  126.0 1.0 copy-start.19
  129.4 13.4 %copy-start.16 = (f32[256,128]{0,1:T(8,128)S(1)}, f32[256,128]{0,1:T(8,128)}, u32[]{:S(2)}) copy-start(f32[256,128]{0,1:T(8,128)} %fusion.130) | copy-start | bytes 393220
  129.4 13.4 %copy-start.18 = (f32[256,128]{0,1:T(8,128)S(1)}, f32[256,128]{0,1:T(8,128)}, u32[]{:S(2)}) copy-start(f32[256,128]{0,1:T(8,128)} %get-tuple-element.80) | copy-start | bytes 393220
  129.4 13.4 %copy-start.20 = (f32[256,128]{0,1:T(8,128)S(1)}, f32[256,128]{0,1:T(8,128)}, u32[]{:S(2)}) copy-start(f32[256,128]{0,1:T(8,128)} %get-tuple-element.81) | copy-start | bytes 393220
  131.1 11.7 %copy-start.22 = (f32[3,2048]{1,0:T(4,128)S(1)}, f32[3,2048]{1,0:T(4,128)}, u32[]{:S(2)}) copy-start(f32[3,2048]{1,0:T(4,128)} %param.11) | copy-start | bytes 73732
  131.1 64.3 %all-to-all-start.1 = ((bf16[32,128,128]{2,0,1:T(8,128)(2,1)}), bf16[32,128,128]{2,0,1:T(8,128)(2,1)S(1)}, u32[]{:S(2)}, u32[]{:S(2)}) async-start(bf16[32,128,128]{2,0,1:T(8,128)(2,1)} %copy.107), calls=%async_computation.1 | async-start | bytes 2097152 | tf_op jit(solution)/shard_map/all_to_all | solution.py:247
  142.9 52.7 %copy-start.4 = (bf16[2048,128]{1,0:T(8,128)(2,1)S(1)}, bf16[2048,128]{1,0:T(8,128)(2,1)}, u32[]{:S(2)}) copy-start(bf16[2048,128]{1,0:T(8,128)(2,1)} %g_ref.1) | copy-start | bytes 1572868
  144.3 51.4 %copy-start.13 = (bf16[2048,128]{1,0:T(8,128)(2,1)S(1)}, bf16[2048,128]{1,0:T(8,128)(2,1)}, u32[]{:S(2)}) copy-start(bf16[2048,128]{1,0:T(8,128)(2,1)} %get-tuple-element.12) | copy-start | bytes 1572868
  144.3 51.4 %copy-start.14 = (bf16[2048,128]{1,0:T(8,128)(2,1)S(1)}, bf16[2048,128]{1,0:T(8,128)(2,1)}, u32[]{:S(2)}) copy-start(bf16[2048,128]{1,0:T(8,128)(2,1)} %get-tuple-element.11) | copy-start | bytes 1572868
  144.7 54.5 %collective-permute-start.2 = (f32[1,4096]{1,0:T(1,128)S(1)}, f32[1,4096]{1,0:T(1,128)S(1)}, u32[]{:S(2)}, u32[]{:S(2)}) collective-permute-start(f32[1,4096]{1,0:T(1,128)S(1)} %get-tuple-element.61), channel_id=1, source_target_pairs={{0,128},{128,256},{256,384},{384,0},{1,129},{129,257},{257,385},{3... | collective-permute-start | bytes 49160 | tf_op jit(solution)/shard_map/ppermute | solution.py:30
  146.6 52.6 %collective-permute-start.3 = (f32[1,4096]{1,0:T(1,128)S(1)}, f32[1,4096]{1,0:T(1,128)S(1)}, u32[]{:S(2)}, u32[]{:S(2)}) collective-permute-start(f32[1,4096]{1,0:T(1,128)S(1)} %get-tuple-element.63), channel_id=1, source_target_pairs={{0,256},{128,384},{256,0},{384,128},{1,257},{129,385},{257,1},{385... | collective-permute-start | bytes 49160 | tf_op jit(solution)/shard_map/ppermute | solution.py:30
  149.6 49.5 %collective-permute-start.4 = (f32[1,4096]{1,0:T(1,128)S(1)}, f32[1,4096]{1,0:T(1,128)S(1)}, u32[]{:S(2)}, u32[]{:S(2)}) collective-permute-start(f32[1,4096]{1,0:T(1,128)S(1)} %get-tuple-element.62), channel_id=1, source_target_pairs={{0,384},{128,0},{256,128},{384,256},{1,385},{129,1},{257,129},{385... | collective-permute-start | bytes 49160 | tf_op jit(solution)/shard_map/ppermute | solution.py:30
  196.6 24.6 %collective-permute-start.1 = (bf16[2048,6]{1,0:T(8,128)(2,1)S(1)}, bf16[2048,6]{1,0:T(8,128)(2,1)S(1)}, u32[]{:S(2)}, u32[]{:S(2)}) collective-permute-start(bf16[2048,6]{1,0:T(8,128)(2,1)S(1)} %pad_maximum_fusion.6), channel_id=1, source_target_pairs={{1,0},{2,1},{3,2},{4,3},{5,4},{6,5},{7,6},{8,7},{9,8},{10,9},{11,1... | collective-permute-start | bytes 73736 | tf_op jit(solution)/shard_map/ppermute | solution.py:18
  200.0 21.5 %copy-start.23 = (f32[1,2048]{1,0:T(1,128)S(1)}, f32[1,2048]{1,0:T(1,128)}, u32[]{:S(2)}) copy-start(f32[1,2048]{1,0:T(1,128)} %get-tuple-element.66) | copy-start | bytes 24580
  221.5 5.2 %copy-start.1 = (bf16[1,16384]{1,0:T(2,128)(2,1)S(1)}, bf16[1,16384]{1,0:T(2,128)(2,1)}, u32[]{:S(2)}) copy-start(bf16[1,16384]{1,0:T(2,128)(2,1)} %param.10) | copy-start | bytes 98308

commit v6 on v5

--- a/solution.py
+++ b/solution.py
@@ -200,8 +200,8 @@
     tables = fourier_tables(seq_len)
     inner = tables[4].shape[1]
     tails = jnp.concatenate([query_proj[:, -2:], key_proj[:, -2:], value_proj[:, -2:]], axis=1)
-    tails = shifted(tails, "ctx", 1)
-    halo = jnp.where(keep_prev > 0, tails, jnp.zeros_like(tails))
+    tails = jnp.where(keep_next > 0, tails, jnp.zeros_like(tails))
+    halo = shifted(tails, "ctx", 1)
     query_conv, key_conv, value_conv, outgoing = front(
         query_proj, key_proj, value_proj, grad_out, halo, short_taps.T, chan_dev
     )
@@ -266,16 +266,17 @@
         (grad_qconv, grad_kconv, grad_vconv)
     )
     heads = jnp.concatenate([grad_qconv[:, :2], grad_kconv[:, :2], grad_vconv[:, :2]], axis=1)
+    heads = jnp.where(keep_prev > 0, heads, jnp.zeros_like(heads))
     heads = shifted(heads, "ctx", -1)
     following = (heads[:, 0:2], heads[:, 2:4], heads[:, 4:6])
     grad_query = taps_backward(
-        grad_qconv.astype(jnp.float32), following[0].astype(jnp.float32) * keep_next, short_taps
+        grad_qconv.astype(jnp.float32), following[0].astype(jnp.float32), short_taps
     ).astype(jnp.bfloat16)
     grad_key = taps_backward(
-        grad_kconv.astype(jnp.float32), following[1].astype(jnp.float32) * keep_next, short_taps
+        grad_kconv.astype(jnp.float32), following[1].astype(jnp.float32), short_taps
     ).astype(jnp.bfloat16)
     grad_value = taps_backward(
-        grad_vconv.astype(jnp.float32), following[2].astype(jnp.float32) * keep_next, short_taps
+        grad_vconv.astype(jnp.float32), following[2].astype(jnp.float32), short_taps
     ).astype(jnp.bfloat16)
     return (grad_query, grad_key, grad_value, grad_filters)
 

time: 227 us -> 228 us (level)
  no operation moved by 1% of the time
where the time goes in v6:
time: 228 us; the launch traced here: 227 us
  waiting for transfers between devices  110 us (48%)
  starting transfers between devices  68.1 us (30%)
  other arithmetic  16.6 us (7%)
  local copies, waits for them, and re-layouts  16 us (7%)
  matrix products  9.65 us (4%)
  Pallas kernels  5.77 us (3%)
    all_to_all x1, waiting for transfers between devices, per_device(): lax.all_to_all(returning, 'ctx', split_axis=1, concat_axis=0, tiled=True)  41.7 us
    all_to_all x1, waiting for transfers between devices, per_device(): lax.all_to_all(outgoing, 'ctx', split_axis=0, concat_axis=1, tiled=True)  40.3 us
    all_to_all x1, starting transfers between devices, per_device(): lax.all_to_all(outgoing, 'ctx', split_axis=0, concat_axis=1, tiled=True)  35.9 us
    ppermute x2, waiting for transfers between devices, shifted(): return lax.ppermute(array, axis, pairs)  27.6 us
    ppermute x2, starting transfers between devices, shifted(): return lax.ppermute(array, axis, pairs)  11.6 us
    all_to_all x1, starting transfers between devices, per_device(): lax.all_to_all(returning, 'ctx', split_axis=1, concat_axis=0, tiled=True)  11.6 us
    ppermute x3, starting transfers between devices, ring_scatter_sum(): total = total + lax.ppermute(piece, axis, pairs)  9 us
    pallas_call x1, Pallas kernels, front(): pl.pallas_call(functools.partial(front_kernel, chan_dev), grid=(all_chans...  5.77 us
  transfers between devices with their start and end apart: 7, of which 4 were waited for; matrix products, arithmetic and copies ran while one was open for 6% of the time, Pallas kernels for 0%

profile of v6, /device:TPU:25, one launch (start us, length us, event | category | flops | bytes accessed | tf_op | source)
XLA Modules:
  0.0 227.2 jit_solution(18096077155054842476)
XLA Ops:
  0.7 1.3 slice.160
  2.2 1.3 slice.161
  4.5 9.0 %collective-permute-start = (bf16[2048,6]{1,0:T(8,128)(2,1)S(1)}, bf16[2048,6]{1,0:T(8,128)(2,1)S(1)}, u32[]{:S(2)}, u32[]{:S(2)}) collective-permute-start(bf16[2048,6]{1,0:T(8,128)(2,1)S(1)} %copy.89), channel_id=1, source_target_pairs={{0,1},{1,2},{2,3},{3,4},{4,5},{5,6},{6,7},{7,8},{8,9},{9,10},{10,1... | collective-permute-start | bytes 73736 | tf_op jit(solution)/shard_map/ppermute | solution.py:18
  13.6 1.4 copy.90
  14.9 6.5 %collective-permute-done.halo_ref = bf16[2048,6]{1,0:T(8,128)(2,1)S(1)} collective-permute-done((bf16[2048,6]{1,0:T(8,128)(2,1)S(1)}, bf16[2048,6]{1,0:T(8,128)(2,1)S(1)}, u32[]{:S(2)}, u32[]{:S(2)}) %collective-permute-start) | collective-permute-done | bytes 24608 | tf_op jit(solution)/shard_map/ppermute | solution.py:18
  22.2 5.8 %shard_map.93 = (bf16[2048,128]{1,0:T(8,128)(2,1)}, bf16[2048,128]{1,0:T(8,128)(2,1)}, bf16[2048,128]{1,0:T(8,128)(2,1)}, bf16[4096,128]{1,0:T(8,128)(2,1)}) custom-call(bf16[2048,128]{1,0:T(8,128)(2,1)} %q_ref.1, bf16[2048,128]{1,0:T(8,128)(2,1)} %k_ref.1, bf16[2048,128]{1,0:T(8,128)(2,1)} %v_ref.1, bf16[2048,128]{1,0:T(8,128)(2,1)} %g_ref.1, ...), custom_call_target="tpu_custom_call" | custom-call | flops 7864320 | bytes 4718592 | tf_op jit(solution)/shard_map/pallas_call | solution.py:154
  28.0 35.9 %all-to-all-start = ((bf16[128,32,128]{2,1,0:T(8,128)(2,1)}), bf16[128,32,128]{2,1,0:T(8,128)(2,1)S(1)}, u32[]{:S(2)}, u32[]{:S(2)}) async-start(bf16[128,32,128]{2,1,0:T(8,128)(2,1)} %bitcast.120), calls=%async_computation | async-start | bytes 2097152 | tf_op jit(solution)/shard_map/all_to_all | solution.py:235
  65.1 1.2 fusion.123
  69.1 1.1 fusion.130
  70.2 1.3 fusion.125
  71.5 1.2 fusion.127
  72.8 40.3 %all-to-all-done = bf16[128,32,128]{2,1,0:T(8,128)(2,1)S(1)} async-done(((bf16[128,32,128]{2,1,0:T(8,128)(2,1)}), bf16[128,32,128]{2,1,0:T(8,128)(2,1)S(1)}, u32[]{:S(2)}, u32[]{:S(2)}) %all-to-all-start) | async-done | bytes 1048608 | tf_op jit(solution)/shard_map/all_to_all | solution.py:235
  114.0 1.0 copy.103
  115.0 1.0 copy.104
  118.0 1.0 fusion.69
  119.1 1.0 fusion.70
  120.7 1.0 fusion.25
  121.8 1.3 fusion.22
  123.1 0.8 add_reduce_fusion
  123.9 1.0 fusion.15
  124.9 1.0 fusion.4
  127.0 1.1 fusion.43
  128.1 1.1 fusion.40
  129.4 1.7 copy.111
  131.1 11.6 %all-to-all-start.1 = ((bf16[32,128,128]{2,0,1:T(8,128)(2,1)}), bf16[32,128,128]{2,0,1:T(8,128)(2,1)S(1)}, u32[]{:S(2)}, u32[]{:S(2)}) async-start(bf16[32,128,128]{2,0,1:T(8,128)(2,1)} %copy.111), calls=%async_computation.1 | async-start | bytes 2097152 | tf_op jit(solution)/shard_map/all_to_all | solution.py:247
  144.6 1.9 collective-permute-start.2
  146.6 3.0 %collective-permute-start.3 = (f32[1,4096]{1,0:T(1,128)S(1)}, f32[1,4096]{1,0:T(1,128)S(1)}, u32[]{:S(2)}, u32[]{:S(2)}) collective-permute-start(f32[1,4096]{1,0:T(1,128)S(1)} %get-tuple-element.63), channel_id=1, source_target_pairs={{0,256},{128,384},{256,0},{384,128},{1,257},{129,385},{257,1},{385... | collective-permute-start | bytes 49160 | tf_op jit(solution)/shard_map/ppermute | solution.py:30
  149.6 4.0 %collective-permute-start.4 = (f32[1,4096]{1,0:T(1,128)S(1)}, f32[1,4096]{1,0:T(1,128)S(1)}, u32[]{:S(2)}, u32[]{:S(2)}) collective-permute-start(f32[1,4096]{1,0:T(1,128)S(1)} %get-tuple-element.62), channel_id=1, source_target_pairs={{0,384},{128,0},{256,128},{384,256},{1,385},{129,1},{257,129},{385... | collective-permute-start | bytes 49160 | tf_op jit(solution)/shard_map/ppermute | solution.py:30
  153.7 41.7 %all-to-all-done.1 = bf16[32,128,128]{2,0,1:T(8,128)(2,1)S(1)} async-done(((bf16[32,128,128]{2,0,1:T(8,128)(2,1)}), bf16[32,128,128]{2,0,1:T(8,128)(2,1)S(1)}, u32[]{:S(2)}, u32[]{:S(2)}) %all-to-all-start.1) | async-done | bytes 1048608 | tf_op jit(solution)/shard_map/all_to_all | solution.py:247
  197.1 2.6 %collective-permute-start.1 = (bf16[2048,6]{1,0:T(8,128)(2,1)S(1)}, bf16[2048,6]{1,0:T(8,128)(2,1)S(1)}, u32[]{:S(2)}, u32[]{:S(2)}) collective-permute-start(bf16[2048,6]{1,0:T(8,128)(2,1)S(1)} %copy.115), channel_id=1, source_target_pairs={{1,0},{2,1},{3,2},{4,3},{5,4},{6,5},{7,6},{8,7},{9,8},{10,9},{11,1... | collective-permute-start | bytes 73736 | tf_op jit(solution)/shard_map/ppermute | solution.py:18
  200.6 21.1 %collective-permute-done.1 = bf16[2048,6]{1,0:T(8,128)(2,1)S(1)} collective-permute-done((bf16[2048,6]{1,0:T(8,128)(2,1)S(1)}, bf16[2048,6]{1,0:T(8,128)(2,1)S(1)}, u32[]{:S(2)}, u32[]{:S(2)}) %collective-permute-start.1) | collective-permute-done | bytes 24608 | tf_op jit(solution)/shard_map/ppermute | solution.py:18
  222.1 5.1 %fusion.52 = (bf16[2048,128]{1,0:T(8,128)(2,1)}, bf16[2048,128]{1,0:T(8,128)(2,1)}, bf16[2048,128]{1,0:T(8,128)(2,1)}) fusion(f32[2048,128]{1,0:T(8,128)S(1)} %convert_element_type.220, f32[2048,2]{1,0:T(8,128)S(1)} %get-tuple-element.42, f32[2048]{0:T(1024)S(1)} %bitcast.126, f32[2048]{0:T(1024)S(1)} %bitcast.127, f32[2048]{0:T(1024)S(1)} %bitcast.125, ...), kind=kLoop, calls=%fused_computation.50 | loop fusion | flops 6291456 | bytes 4792320 | tf_op jit(solution)/shard_map/convert_element_type | solution.py:280
  (106 shorter events, 15.5 us)
Async XLA Ops:
  0.6 63.3 %copy-start = (bf16[1,16384]{1,0:T(2,128)(2,1)S(1)}, bf16[1,16384]{1,0:T(2,128)(2,1)}, u32[]{:S(2)}) copy-start(bf16[1,16384]{1,0:T(2,128)(2,1)} %param.10) | copy-start | bytes 98308
  0.6 3.1 %copy-start.5 = (bf16[2048,128]{1,0:T(8,128)(2,1)S(1)}, bf16[2048,128]{1,0:T(8,128)(2,1)}, u32[]{:S(2)}) copy-start(bf16[2048,128]{1,0:T(8,128)(2,1)} %v_ref.1) | copy-start | bytes 1572868
  2.0 11.6 %copy-start.22 = (f32[3,2048]{1,0:T(4,128)S(1)}, f32[3,2048]{1,0:T(4,128)}, u32[]{:S(2)}) copy-start(f32[3,2048]{1,0:T(4,128)} %param.11) | copy-start | bytes 73732
  4.5 16.9 %collective-permute-start = (bf16[2048,6]{1,0:T(8,128)(2,1)S(1)}, bf16[2048,6]{1,0:T(8,128)(2,1)S(1)}, u32[]{:S(2)}, u32[]{:S(2)}) collective-permute-start(bf16[2048,6]{1,0:T(8,128)(2,1)S(1)} %copy.89), channel_id=1, source_target_pairs={{0,1},{1,2},{2,3},{3,4},{4,5},{5,6},{6,7},{7,8},{8,9},{9,10},{10,1... | collective-permute-start | bytes 73736 | tf_op jit(solution)/shard_map/ppermute | solution.py:18
  21.4 0.8 copy-start.15
  28.0 85.1 %all-to-all-start = ((bf16[128,32,128]{2,1,0:T(8,128)(2,1)}), bf16[128,32,128]{2,1,0:T(8,128)(2,1)S(1)}, u32[]{:S(2)}, u32[]{:S(2)}) async-start(bf16[128,32,128]{2,1,0:T(8,128)(2,1)} %bitcast.120), calls=%async_computation | async-start | bytes 2097152 | tf_op jit(solution)/shard_map/all_to_all | solution.py:235
  66.3 46.7 %copy-start.2 = (f32[128,256]{1,0:T(8,128)}, f32[128,256]{1,0:T(8,128)S(1)}, u32[]{:S(2)}) copy-start(f32[128,256]{1,0:T(8,128)S(1)} %get-tuple-element.73) | copy-start | bytes 393220
  116.7 1.0 copy-start.6
  116.7 1.2 copy-start.7
  116.9 1.0 copy-start.3
  116.9 1.1 copy-start.10
  119.0 1.0 copy-start.8
  119.1 1.0 copy-start.9
  121.8 1.3 copy-start.11
  121.8 1.3 copy-start.12
  126.0 0.9 copy-start.16
  126.0 1.0 copy-start.18
  126.0 1.0 copy-start.20
  129.4 13.4 %copy-start.17 = (f32[256,128]{0,1:T(8,128)S(1)}, f32[256,128]{0,1:T(8,128)}, u32[]{:S(2)}) copy-start(f32[256,128]{0,1:T(8,128)} %fusion.130) | copy-start | bytes 393220
  129.4 13.4 %copy-start.19 = (f32[256,128]{0,1:T(8,128)S(1)}, f32[256,128]{0,1:T(8,128)}, u32[]{:S(2)}) copy-start(f32[256,128]{0,1:T(8,128)} %get-tuple-element.80) | copy-start | bytes 393220
  129.4 13.4 %copy-start.21 = (f32[256,128]{0,1:T(8,128)S(1)}, f32[256,128]{0,1:T(8,128)}, u32[]{:S(2)}) copy-start(f32[256,128]{0,1:T(8,128)} %get-tuple-element.81) | copy-start | bytes 393220
  131.1 11.7 %copy-start.23 = (f32[3,2048]{1,0:T(4,128)S(1)}, f32[3,2048]{1,0:T(4,128)}, u32[]{:S(2)}) copy-start(f32[3,2048]{1,0:T(4,128)} %param.11) | copy-start | bytes 73732
  131.1 64.3 %all-to-all-start.1 = ((bf16[32,128,128]{2,0,1:T(8,128)(2,1)}), bf16[32,128,128]{2,0,1:T(8,128)(2,1)S(1)}, u32[]{:S(2)}, u32[]{:S(2)}) async-start(bf16[32,128,128]{2,0,1:T(8,128)(2,1)} %copy.111), calls=%async_computation.1 | async-start | bytes 2097152 | tf_op jit(solution)/shard_map/all_to_all | solution.py:247
  142.8 52.7 %copy-start.4 = (bf16[2048,128]{1,0:T(8,128)(2,1)S(1)}, bf16[2048,128]{1,0:T(8,128)(2,1)}, u32[]{:S(2)}) copy-start(bf16[2048,128]{1,0:T(8,128)(2,1)} %g_ref.1) | copy-start | bytes 1572868
  144.3 51.4 %copy-start.13 = (bf16[2048,128]{1,0:T(8,128)(2,1)S(1)}, bf16[2048,128]{1,0:T(8,128)(2,1)}, u32[]{:S(2)}) copy-start(bf16[2048,128]{1,0:T(8,128)(2,1)} %get-tuple-element.12) | copy-start | bytes 1572868
  144.3 51.4 %copy-start.14 = (bf16[2048,128]{1,0:T(8,128)(2,1)S(1)}, bf16[2048,128]{1,0:T(8,128)(2,1)}, u32[]{:S(2)}) copy-start(bf16[2048,128]{1,0:T(8,128)(2,1)} %get-tuple-element.11) | copy-start | bytes 1572868
  144.6 55.0 %collective-permute-start.2 = (f32[1,4096]{1,0:T(1,128)S(1)}, f32[1,4096]{1,0:T(1,128)S(1)}, u32[]{:S(2)}, u32[]{:S(2)}) collective-permute-start(f32[1,4096]{1,0:T(1,128)S(1)} %get-tuple-element.61), channel_id=1, source_target_pairs={{0,128},{128,256},{256,384},{384,0},{1,129},{129,257},{257,385},{3... | collective-permute-start | bytes 49160 | tf_op jit(solution)/shard_map/ppermute | solution.py:30
  146.6 53.1 %collective-permute-start.3 = (f32[1,4096]{1,0:T(1,128)S(1)}, f32[1,4096]{1,0:T(1,128)S(1)}, u32[]{:S(2)}, u32[]{:S(2)}) collective-permute-start(f32[1,4096]{1,0:T(1,128)S(1)} %get-tuple-element.63), channel_id=1, source_target_pairs={{0,256},{128,384},{256,0},{384,128},{1,257},{129,385},{257,1},{385... | collective-permute-start | bytes 49160 | tf_op jit(solution)/shard_map/ppermute | solution.py:30
  149.6 50.1 %collective-permute-start.4 = (f32[1,4096]{1,0:T(1,128)S(1)}, f32[1,4096]{1,0:T(1,128)S(1)}, u32[]{:S(2)}, u32[]{:S(2)}) collective-permute-start(f32[1,4096]{1,0:T(1,128)S(1)} %get-tuple-element.62), channel_id=1, source_target_pairs={{0,384},{128,0},{256,128},{384,256},{1,385},{129,1},{257,129},{385... | collective-permute-start | bytes 49160 | tf_op jit(solution)/shard_map/ppermute | solution.py:30
  197.1 24.6 %collective-permute-start.1 = (bf16[2048,6]{1,0:T(8,128)(2,1)S(1)}, bf16[2048,6]{1,0:T(8,128)(2,1)S(1)}, u32[]{:S(2)}, u32[]{:S(2)}) collective-permute-start(bf16[2048,6]{1,0:T(8,128)(2,1)S(1)} %copy.115), channel_id=1, source_target_pairs={{1,0},{2,1},{3,2},{4,3},{5,4},{6,5},{7,6},{8,7},{9,8},{10,9},{11,1... | collective-permute-start | bytes 73736 | tf_op jit(solution)/shard_map/ppermute | solution.py:18
  200.6 21.5 %copy-start.24 = (f32[1,2048]{1,0:T(1,128)S(1)}, f32[1,2048]{1,0:T(1,128)}, u32[]{:S(2)}) copy-start(f32[1,2048]{1,0:T(1,128)} %get-tuple-element.66) | copy-start | bytes 24580
  222.0 5.2 %copy-start.1 = (bf16[1,16384]{1,0:T(2,128)(2,1)S(1)}, bf16[1,16384]{1,0:T(2,128)(2,1)}, u32[]{:S(2)}) copy-start(bf16[1,16384]{1,0:T(2,128)(2,1)} %param.10) | copy-start | bytes 98308

commit v7 on v6

--- a/solution.py
+++ b/solution.py
@@ -164,6 +164,29 @@
     )(query_proj, key_proj, value_proj, grad_out, halo, taps_cols)
 
 
+def tails_kernel(keep_ref, q_ref, k_ref, v_ref, out_ref):
+    cols = q_ref.shape[1]
+    keep = keep_ref[0, 0]
+    for slot, ref in enumerate((q_ref, k_ref, v_ref)):
+        part = ref[:, cols - 2 : cols].astype(jnp.float32) * keep
+        out_ref[:, 2 * slot : 2 * slot + 2] = part.astype(out_ref.dtype)
+
+
+def tails_of(query_proj, key_proj, value_proj, keep):
+    all_chans, tok_cols = query_proj.shape
+    block = min(BLOCK_ROWS, all_chans)
+    tile = pl.BlockSpec((block, tok_cols), lambda i: (i, 0))
+    return pl.pallas_call(
+        tails_kernel,
+        grid=(all_chans // block,),
+        in_specs=[pl.BlockSpec(memory_space=pltpu.SMEM), tile, tile, tile],
+        out_specs=pl.BlockSpec((block, 6), lambda i: (i, 0)),
+        out_shape=jax.ShapeDtypeStruct((all_chans, 6), query_proj.dtype),
+        cost_estimate=pl.CostEstimate(flops=6 * all_chans, transcendentals=0,
+                                      bytes_accessed=6 * all_chans * tok_cols),
+    )(keep.reshape(1, 1), query_proj, key_proj, value_proj)
+
+
 def taps_forward(current, earlier, short_taps):
     columns = current.shape[1]
     joined = jnp.concatenate([earlier, current], axis=1)
@@ -199,8 +222,7 @@
     keep_next = jnp.where((position + tok_cols) % seq_len == 0, 0.0, 1.0).astype(jnp.float32)
     tables = fourier_tables(seq_len)
     inner = tables[4].shape[1]
-    tails = jnp.concatenate([query_proj[:, -2:], key_proj[:, -2:], value_proj[:, -2:]], axis=1)
-    tails = jnp.where(keep_next > 0, tails, jnp.zeros_like(tails))
+    tails = tails_of(query_proj, key_proj, value_proj, keep_next)
     halo = shifted(tails, "ctx", 1)
     query_conv, key_conv, value_conv, outgoing = front(
         query_proj, key_proj, value_proj, grad_out, halo, short_taps.T, chan_dev

time: 228 us -> 227 us (level)
  local copies, waits for them, and re-layouts: 16 us -> 12.3 us
  Pallas kernels: 5.77 us -> 8.57 us
    pallas_call x0 -> x1, Pallas kernels: none -> 2.79 us  [tails_of(): pl.pallas_call(tails_kernel, grid=(all_chans // block,), in_specs=[pl.Blo...]
    slice x3 -> x0, local copies, waits for them, and re-layouts: 2.78 us -> none  [the longest x1 1.31 us: per_device(): query_proj[:, -2:]]
where the time goes in v7:
time: 227 us; the launch traced here: 226 us
  waiting for transfers between devices  110 us (48%)
  starting transfers between devices  68 us (30%)
  other arithmetic  16.6 us (7%)
  local copies, waits for them, and re-layouts  12.3 us (5%)
  matrix products  9.67 us (4%)
  Pallas kernels  8.57 us (4%)
    all_to_all x1, waiting for transfers between devices, per_device(): lax.all_to_all(returning, 'ctx', split_axis=1, concat_axis=0, tiled=True)  41.7 us
    all_to_all x1, waiting for transfers between devices, per_device(): lax.all_to_all(outgoing, 'ctx', split_axis=0, concat_axis=1, tiled=True)  40.3 us
    all_to_all x1, starting transfers between devices, per_device(): lax.all_to_all(outgoing, 'ctx', split_axis=0, concat_axis=1, tiled=True)  35.8 us
    ppermute x2, waiting for transfers between devices, shifted(): return lax.ppermute(array, axis, pairs)  27.9 us
    ppermute x2, starting transfers between devices, shifted(): return lax.ppermute(array, axis, pairs)  11.6 us
    all_to_all x1, starting transfers between devices, per_device(): lax.all_to_all(returning, 'ctx', split_axis=1, concat_axis=0, tiled=True)  11.6 us
    ppermute x3, starting transfers between devices, ring_scatter_sum(): total = total + lax.ppermute(piece, axis, pairs)  9 us
    pallas_call x1, Pallas kernels, front(): pl.pallas_call(functools.partial(front_kernel, chan_dev), grid=(all_chans...  5.78 us
  transfers between devices with their start and end apart: 7, of which 4 were waited for; matrix products, arithmetic and copies ran while one was open for 6% of the time, Pallas kernels for 0%

profile of v7, /device:TPU:25, one launch (start us, length us, event | category | flops | bytes accessed | tf_op | source)
XLA Modules:
  0.0 226.4 jit_solution(13724568916331831938)
XLA Ops:
  0.7 2.8 %shard_map.93 = bf16[2048,6]{1,0:T(8,128)(2,1)} custom-call(f32[1,1]{1,0:T(1,128)} %bitcast.2.keep_ref, bf16[2048,128]{1,0:T(8,128)(2,1)} %q_ref.3, bf16[2048,128]{1,0:T(8,128)(2,1)} %k_ref.3, bf16[2048,128]{1,0:T(8,128)(2,1)} %v_ref.3), custom_call_target="tpu_custom_call" | custom-call | flops 12288 | bytes 1572864 | tf_op jit(solution)/shard_map/pallas_call | solution.py:179
  3.5 9.0 %collective-permute-start = (bf16[2048,6]{1,0:T(8,128)(2,1)}, bf16[2048,6]{1,0:T(8,128)(2,1)S(1)}, u32[]{:S(2)}, u32[]{:S(2)}) collective-permute-start(bf16[2048,6]{1,0:T(8,128)(2,1)} %shard_map.93), channel_id=1, source_target_pairs={{0,1},{1,2},{2,3},{3,4},{4,5},{5,6},{6,7},{7,8},{8,9},{9,10},{10,1... | collective-permute-start | bytes 73736 | tf_op jit(solution)/shard_map/ppermute | solution.py:18
  12.5 1.4 copy.80
  13.9 6.8 %collective-permute-done.halo_ref = bf16[2048,6]{1,0:T(8,128)(2,1)S(1)} collective-permute-done((bf16[2048,6]{1,0:T(8,128)(2,1)}, bf16[2048,6]{1,0:T(8,128)(2,1)S(1)}, u32[]{:S(2)}, u32[]{:S(2)}) %collective-permute-start) | collective-permute-done | bytes 24608 | tf_op jit(solution)/shard_map/ppermute | solution.py:18
  20.7 0.8 copy-done.14
  21.5 5.8 %shard_map.94 = (bf16[2048,128]{1,0:T(8,128)(2,1)}, bf16[2048,128]{1,0:T(8,128)(2,1)}, bf16[2048,128]{1,0:T(8,128)(2,1)}, bf16[4096,128]{1,0:T(8,128)(2,1)}) custom-call(bf16[2048,128]{1,0:T(8,128)(2,1)} %q_ref.3, bf16[2048,128]{1,0:T(8,128)(2,1)} %k_ref.3, bf16[2048,128]{1,0:T(8,128)(2,1)} %v_ref.3, bf16[2048,128]{1,0:T(8,128)(2,1)} %g_ref.1, ...), custom_call_target="tpu_custom_call" | custom-call | flops 7864320 | bytes 4718592 | tf_op jit(solution)/shard_map/pallas_call | solution.py:154
  27.3 35.8 %all-to-all-start = ((bf16[128,32,128]{2,1,0:T(8,128)(2,1)}), bf16[128,32,128]{2,1,0:T(8,128)(2,1)S(1)}, u32[]{:S(2)}, u32[]{:S(2)}) async-start(bf16[128,32,128]{2,1,0:T(8,128)(2,1)} %bitcast.121), calls=%async_computation | async-start | bytes 2097152 | tf_op jit(solution)/shard_map/all_to_all | solution.py:257
  64.3 1.2 fusion.123
  68.3 1.2 fusion.130
  69.4 1.3 fusion.125
  70.7 1.2 fusion.127
  71.9 40.3 %all-to-all-done = bf16[128,32,128]{2,1,0:T(8,128)(2,1)S(1)} async-done(((bf16[128,32,128]{2,1,0:T(8,128)(2,1)}), bf16[128,32,128]{2,1,0:T(8,128)(2,1)S(1)}, u32[]{:S(2)}, u32[]{:S(2)}) %all-to-all-start) | async-done | bytes 1048608 | tf_op jit(solution)/shard_map/all_to_all | solution.py:257
  113.2 1.0 copy.93
  114.2 1.0 copy.94
  117.1 1.0 fusion.69
  118.2 1.0 fusion.70
  119.9 1.0 fusion.25
  121.0 1.3 fusion.22
  122.2 0.8 add_reduce_fusion
  123.1 1.0 fusion.15
  124.1 1.0 fusion.4
  126.2 1.1 fusion.43
  127.3 1.1 fusion.40
  128.6 1.7 copy.101
  130.3 11.6 %all-to-all-start.1 = ((bf16[32,128,128]{2,0,1:T(8,128)(2,1)}), bf16[32,128,128]{2,0,1:T(8,128)(2,1)S(1)}, u32[]{:S(2)}, u32[]{:S(2)}) async-start(bf16[32,128,128]{2,0,1:T(8,128)(2,1)} %copy.101), calls=%async_computation.1 | async-start | bytes 2097152 | tf_op jit(solution)/shard_map/all_to_all | solution.py:269
  143.8 1.9 collective-permute-start.2
  145.7 3.0 %collective-permute-start.3 = (f32[1,4096]{1,0:T(1,128)S(1)}, f32[1,4096]{1,0:T(1,128)S(1)}, u32[]{:S(2)}, u32[]{:S(2)}) collective-permute-start(f32[1,4096]{1,0:T(1,128)S(1)} %get-tuple-element.63), channel_id=1, source_target_pairs={{0,256},{128,384},{256,0},{384,128},{1,257},{129,385},{257,1},{385... | collective-permute-start | bytes 49160 | tf_op jit(solution)/shard_map/ppermute | solution.py:30
  148.8 4.0 %collective-permute-start.4 = (f32[1,4096]{1,0:T(1,128)S(1)}, f32[1,4096]{1,0:T(1,128)S(1)}, u32[]{:S(2)}, u32[]{:S(2)}) collective-permute-start(f32[1,4096]{1,0:T(1,128)S(1)} %get-tuple-element.62), channel_id=1, source_target_pairs={{0,384},{128,0},{256,128},{384,256},{1,385},{129,1},{257,129},{385... | collective-permute-start | bytes 49160 | tf_op jit(solution)/shard_map/ppermute | solution.py:30
  152.8 41.7 %all-to-all-done.1 = bf16[32,128,128]{2,0,1:T(8,128)(2,1)S(1)} async-done(((bf16[32,128,128]{2,0,1:T(8,128)(2,1)}), bf16[32,128,128]{2,0,1:T(8,128)(2,1)S(1)}, u32[]{:S(2)}, u32[]{:S(2)}) %all-to-all-start.1) | async-done | bytes 1048608 | tf_op jit(solution)/shard_map/all_to_all | solution.py:269
  196.3 2.6 %collective-permute-start.1 = (bf16[2048,6]{1,0:T(8,128)(2,1)S(1)}, bf16[2048,6]{1,0:T(8,128)(2,1)S(1)}, u32[]{:S(2)}, u32[]{:S(2)}) collective-permute-start(bf16[2048,6]{1,0:T(8,128)(2,1)S(1)} %copy.105), channel_id=1, source_target_pairs={{1,0},{2,1},{3,2},{4,3},{5,4},{6,5},{7,6},{8,7},{9,8},{10,9},{11,1... | collective-permute-start | bytes 73736 | tf_op jit(solution)/shard_map/ppermute | solution.py:18
  199.8 21.1 %collective-permute-done.1 = bf16[2048,6]{1,0:T(8,128)(2,1)S(1)} collective-permute-done((bf16[2048,6]{1,0:T(8,128)(2,1)S(1)}, bf16[2048,6]{1,0:T(8,128)(2,1)S(1)}, u32[]{:S(2)}, u32[]{:S(2)}) %collective-permute-start.1) | collective-permute-done | bytes 24608 | tf_op jit(solution)/shard_map/ppermute | solution.py:18
  221.3 5.1 %fusion.52 = (bf16[2048,128]{1,0:T(8,128)(2,1)}, bf16[2048,128]{1,0:T(8,128)(2,1)}, bf16[2048,128]{1,0:T(8,128)(2,1)}) fusion(f32[2048,128]{1,0:T(8,128)S(1)} %convert_element_type.220, f32[2048,2]{1,0:T(8,128)S(1)} %get-tuple-element.42, f32[2048]{0:T(1024)S(1)} %bitcast.127, f32[2048]{0:T(1024)S(1)} %bitcast.128, f32[2048]{0:T(1024)S(1)} %bitcast.126, ...), kind=kLoop, calls=%fused_computation.50 | loop fusion | flops 6291456 | bytes 4792320 | tf_op jit(solution)/shard_map/convert_element_type | solution.py:302
  (97 shorter events, 13.5 us)
Async XLA Ops:
  0.6 62.4 %copy-start = (bf16[1,16384]{1,0:T(2,128)(2,1)S(1)}, bf16[1,16384]{1,0:T(2,128)(2,1)}, u32[]{:S(2)}) copy-start(bf16[1,16384]{1,0:T(2,128)(2,1)} %param.10) | copy-start | bytes 98308
  0.6 11.9 %copy-start.21 = (f32[3,2048]{1,0:T(4,128)S(1)}, f32[3,2048]{1,0:T(4,128)}, u32[]{:S(2)}) copy-start(f32[3,2048]{1,0:T(4,128)} %param.11) | copy-start | bytes 73732
  3.5 17.2 %collective-permute-start = (bf16[2048,6]{1,0:T(8,128)(2,1)}, bf16[2048,6]{1,0:T(8,128)(2,1)S(1)}, u32[]{:S(2)}, u32[]{:S(2)}) collective-permute-start(bf16[2048,6]{1,0:T(8,128)(2,1)} %shard_map.93), channel_id=1, source_target_pairs={{0,1},{1,2},{2,3},{3,4},{4,5},{5,6},{6,7},{7,8},{8,9},{9,10},{10,1... | collective-permute-start | bytes 73736 | tf_op jit(solution)/shard_map/ppermute | solution.py:18
  20.7 0.8 copy-start.14
  27.3 85.0 %all-to-all-start = ((bf16[128,32,128]{2,1,0:T(8,128)(2,1)}), bf16[128,32,128]{2,1,0:T(8,128)(2,1)S(1)}, u32[]{:S(2)}, u32[]{:S(2)}) async-start(bf16[128,32,128]{2,1,0:T(8,128)(2,1)} %bitcast.121), calls=%async_computation | async-start | bytes 2097152 | tf_op jit(solution)/shard_map/all_to_all | solution.py:257
  65.5 46.7 %copy-start.2 = (f32[128,256]{1,0:T(8,128)}, f32[128,256]{1,0:T(8,128)S(1)}, u32[]{:S(2)}) copy-start(f32[128,256]{1,0:T(8,128)S(1)} %get-tuple-element.73) | copy-start | bytes 393220
  115.8 1.0 copy-start.5
  115.8 1.2 copy-start.6
  116.1 1.0 copy-start.3
  116.1 1.1 copy-start.9
  118.2 1.0 copy-start.7
  118.2 1.0 copy-start.8
  120.9 1.3 copy-start.10
  120.9 1.3 copy-start.11
  125.2 0.9 copy-start.15
  125.2 1.0 copy-start.17
  125.2 1.0 copy-start.19
  128.6 13.4 %copy-start.16 = (f32[256,128]{0,1:T(8,128)S(1)}, f32[256,128]{0,1:T(8,128)}, u32[]{:S(2)}) copy-start(f32[256,128]{0,1:T(8,128)} %fusion.130) | copy-start | bytes 393220
  128.6 13.4 %copy-start.18 = (f32[256,128]{0,1:T(8,128)S(1)}, f32[256,128]{0,1:T(8,128)}, u32[]{:S(2)}) copy-start(f32[256,128]{0,1:T(8,128)} %get-tuple-element.80) | copy-start | bytes 393220
  128.6 13.4 %copy-start.20 = (f32[256,128]{0,1:T(8,128)S(1)}, f32[256,128]{0,1:T(8,128)}, u32[]{:S(2)}) copy-start(f32[256,128]{0,1:T(8,128)} %get-tuple-element.81) | copy-start | bytes 393220
  130.3 11.7 %copy-start.22 = (f32[3,2048]{1,0:T(4,128)S(1)}, f32[3,2048]{1,0:T(4,128)}, u32[]{:S(2)}) copy-start(f32[3,2048]{1,0:T(4,128)} %param.11) | copy-start | bytes 73732
  130.3 64.3 %all-to-all-start.1 = ((bf16[32,128,128]{2,0,1:T(8,128)(2,1)}), bf16[32,128,128]{2,0,1:T(8,128)(2,1)S(1)}, u32[]{:S(2)}, u32[]{:S(2)}) async-start(bf16[32,128,128]{2,0,1:T(8,128)(2,1)} %copy.101), calls=%async_computation.1 | async-start | bytes 2097152 | tf_op jit(solution)/shard_map/all_to_all | solution.py:269
  142.0 52.7 %copy-start.4 = (bf16[2048,128]{1,0:T(8,128)(2,1)S(1)}, bf16[2048,128]{1,0:T(8,128)(2,1)}, u32[]{:S(2)}) copy-start(bf16[2048,128]{1,0:T(8,128)(2,1)} %g_ref.1) | copy-start | bytes 1572868
  143.5 51.4 %copy-start.12 = (bf16[2048,128]{1,0:T(8,128)(2,1)S(1)}, bf16[2048,128]{1,0:T(8,128)(2,1)}, u32[]{:S(2)}) copy-start(bf16[2048,128]{1,0:T(8,128)(2,1)} %get-tuple-element.12) | copy-start | bytes 1572868
  143.5 51.4 %copy-start.13 = (bf16[2048,128]{1,0:T(8,128)(2,1)S(1)}, bf16[2048,128]{1,0:T(8,128)(2,1)}, u32[]{:S(2)}) copy-start(bf16[2048,128]{1,0:T(8,128)(2,1)} %get-tuple-element.11) | copy-start | bytes 1572868
  143.8 55.0 %collective-permute-start.2 = (f32[1,4096]{1,0:T(1,128)S(1)}, f32[1,4096]{1,0:T(1,128)S(1)}, u32[]{:S(2)}, u32[]{:S(2)}) collective-permute-start(f32[1,4096]{1,0:T(1,128)S(1)} %get-tuple-element.61), channel_id=1, source_target_pairs={{0,128},{128,256},{256,384},{384,0},{1,129},{129,257},{257,385},{3... | collective-permute-start | bytes 49160 | tf_op jit(solution)/shard_map/ppermute | solution.py:30
  145.7 53.1 %collective-permute-start.3 = (f32[1,4096]{1,0:T(1,128)S(1)}, f32[1,4096]{1,0:T(1,128)S(1)}, u32[]{:S(2)}, u32[]{:S(2)}) collective-permute-start(f32[1,4096]{1,0:T(1,128)S(1)} %get-tuple-element.63), channel_id=1, source_target_pairs={{0,256},{128,384},{256,0},{384,128},{1,257},{129,385},{257,1},{385... | collective-permute-start | bytes 49160 | tf_op jit(solution)/shard_map/ppermute | solution.py:30
  148.8 50.1 %collective-permute-start.4 = (f32[1,4096]{1,0:T(1,128)S(1)}, f32[1,4096]{1,0:T(1,128)S(1)}, u32[]{:S(2)}, u32[]{:S(2)}) collective-permute-start(f32[1,4096]{1,0:T(1,128)S(1)} %get-tuple-element.62), channel_id=1, source_target_pairs={{0,384},{128,0},{256,128},{384,256},{1,385},{129,1},{257,129},{385... | collective-permute-start | bytes 49160 | tf_op jit(solution)/shard_map/ppermute | solution.py:30
  196.3 24.6 %collective-permute-start.1 = (bf16[2048,6]{1,0:T(8,128)(2,1)S(1)}, bf16[2048,6]{1,0:T(8,128)(2,1)S(1)}, u32[]{:S(2)}, u32[]{:S(2)}) collective-permute-start(bf16[2048,6]{1,0:T(8,128)(2,1)S(1)} %copy.105), channel_id=1, source_target_pairs={{1,0},{2,1},{3,2},{4,3},{5,4},{6,5},{7,6},{8,7},{9,8},{10,9},{11,1... | collective-permute-start | bytes 73736 | tf_op jit(solution)/shard_map/ppermute | solution.py:18
  199.7 21.5 %copy-start.23 = (f32[1,2048]{1,0:T(1,128)S(1)}, f32[1,2048]{1,0:T(1,128)}, u32[]{:S(2)}) copy-start(f32[1,2048]{1,0:T(1,128)} %get-tuple-element.66) | copy-start | bytes 24580
  221.2 5.2 %copy-start.1 = (bf16[1,16384]{1,0:T(2,128)(2,1)S(1)}, bf16[1,16384]{1,0:T(2,128)(2,1)}, u32[]{:S(2)}) copy-start(bf16[1,16384]{1,0:T(2,128)(2,1)} %param.10) | copy-start | bytes 98308

commit v8 on v5

--- a/solution.py
+++ b/solution.py
@@ -73,7 +73,14 @@
             [real_blocks, imag_rows.reshape(row_count, half_outer, inner)], axis=1
         )
         table = fwd_outer
-    first = jnp.einsum("man,ak->mkn", blocks, table, precision=triple)
+    if blocks.dtype == jnp.bfloat16:
+        table_hi = table.astype(jnp.bfloat16)
+        table_lo = (table - table_hi.astype(jnp.float32)).astype(jnp.bfloat16)
+        first = jnp.einsum(
+            "man,ak->mkn", blocks, table_hi, preferred_element_type=jnp.float32
+        ) + jnp.einsum("man,ak->mkn", blocks, table_lo, preferred_element_type=jnp.float32)
+    else:
+        first = jnp.einsum("man,ak->mkn", blocks, table, precision=triple)
     first_real = first[:, :outer]
     first_imag = first[:, outer:]
     turned = jnp.concatenate(
@@ -205,7 +212,7 @@
     query_conv, key_conv, value_conv, outgoing = front(
         query_proj, key_proj, value_proj, grad_out, halo, short_taps.T, chan_dev
     )
-    filter_spec = forward_spectrum(filters.astype(jnp.float32), None, tables)
+    filter_spec = forward_spectrum(filters, None, tables)
     filter_real = filter_spec[:, None, :, :inner]
     filter_imag = filter_spec[:, None, :, inner:]
 
@@ -216,7 +223,7 @@
         return source.reshape(chan_dev, ctx_count * tok_cols)
 
     def spectrum_of(rows_three):
-        paired = rows_three.reshape(groups_dev, 2, pair_rows, seq_len).astype(jnp.float32)
+        paired = rows_three.reshape(groups_dev, 2, pair_rows, seq_len)
         spec = forward_spectrum(
             paired[:, 0].reshape(-1, seq_len), paired[:, 1].reshape(-1, seq_len), tables
         )

time: 227 us -> 231 us (1.018)
  transfers between devices with their start and end apart: 7 -> 7, of which waited for: 4 -> 4; matrix products, arithmetic and copies ran while one was open for 6% -> 5% of each run, Pallas kernels for 0% -> 0%
where the time goes in v8:
time: 231 us; the launch traced here: 230 us
  waiting for transfers between devices  111 us (48%)
  starting transfers between devices  68 us (29%)
  other arithmetic  18.5 us (8%)
  local copies, waits for them, and re-layouts  14.5 us (6%)
  matrix products  10.7 us (5%)
  Pallas kernels  5.76 us (2%)
    all_to_all x1, waiting for transfers between devices, per_device(): lax.all_to_all(returning, 'ctx', split_axis=1, concat_axis=0, tiled=True)  42.3 us
    all_to_all x1, waiting for transfers between devices, per_device(): lax.all_to_all(outgoing, 'ctx', split_axis=0, concat_axis=1, tiled=True)  41.5 us
    all_to_all x1, starting transfers between devices, per_device(): lax.all_to_all(outgoing, 'ctx', split_axis=0, concat_axis=1, tiled=True)  35.9 us
    ppermute x2, waiting for transfers between devices, shifted(): return lax.ppermute(array, axis, pairs)  27.6 us
    ppermute x2, starting transfers between devices, shifted(): return lax.ppermute(array, axis, pairs)  11.6 us
    all_to_all x1, starting transfers between devices, per_device(): lax.all_to_all(returning, 'ctx', split_axis=1, concat_axis=0, tiled=True)  11.4 us
    ppermute x3, starting transfers between devices, ring_scatter_sum(): total = total + lax.ppermute(piece, axis, pairs)  9 us
    pallas_call x1, Pallas kernels, front(): pl.pallas_call(functools.partial(front_kernel, chan_dev), grid=(all_chans...  5.76 us
  transfers between devices with their start and end apart: 7, of which 4 were waited for; matrix products, arithmetic and copies ran while one was open for 5% of the time, Pallas kernels for 0%

profile of v8, /device:TPU:25, one launch (start us, length us, event | category | flops | bytes accessed | tf_op | source)
XLA Modules:
  0.0 230.2 jit_solution(7701238342873646368)
XLA Ops:
  0.7 1.3 slice.160
  2.2 1.3 slice.161
  4.5 9.0 %collective-permute-start = (bf16[2048,6]{1,0:T(8,128)(2,1)S(1)}, bf16[2048,6]{1,0:T(8,128)(2,1)S(1)}, u32[]{:S(2)}, u32[]{:S(2)}) collective-permute-start(bf16[2048,6]{1,0:T(8,128)(2,1)S(1)} %copy.85), channel_id=1, source_target_pairs={{0,1},{1,2},{2,3},{3,4},{4,5},{5,6},{6,7},{7,8},{8,9},{9,10},{10,1... | collective-permute-start | bytes 73736 | tf_op jit(solution)/shard_map/ppermute | solution.py:18
  13.6 1.3 copy.86
  14.9 6.5 %collective-permute-done = bf16[2048,6]{1,0:T(8,128)(2,1)S(1)} collective-permute-done((bf16[2048,6]{1,0:T(8,128)(2,1)S(1)}, bf16[2048,6]{1,0:T(8,128)(2,1)S(1)}, u32[]{:S(2)}, u32[]{:S(2)}) %collective-permute-start) | collective-permute-done | bytes 24608 | tf_op jit(solution)/shard_map/ppermute | solution.py:18
  22.2 5.8 %shard_map.93 = (bf16[2048,128]{1,0:T(8,128)(2,1)}, bf16[2048,128]{1,0:T(8,128)(2,1)}, bf16[2048,128]{1,0:T(8,128)(2,1)}, bf16[4096,128]{1,0:T(8,128)(2,1)}) custom-call(bf16[2048,128]{1,0:T(8,128)(2,1)} %q_ref.1, bf16[2048,128]{1,0:T(8,128)(2,1)} %k_ref.1, bf16[2048,128]{1,0:T(8,128)(2,1)} %v_ref.1, bf16[2048,128]{1,0:T(8,128)(2,1)} %g_ref.1, ...), custom_call_target="tpu_custom_call" | custom-call | flops 7864320 | bytes 4718592 | tf_op jit(solution)/shard_map/pallas_call | solution.py:161
  28.0 35.9 %all-to-all-start = ((bf16[128,32,128]{2,1,0:T(8,128)(2,1)}), bf16[128,32,128]{2,1,0:T(8,128)(2,1)S(1)}, u32[]{:S(2)}, u32[]{:S(2)}) async-start(bf16[128,32,128]{2,1,0:T(8,128)(2,1)} %bitcast.134), calls=%async_computation | async-start | bytes 2097152 | tf_op jit(solution)/shard_map/all_to_all | solution.py:242
  68.6 1.1 fusion.130
  70.3 1.2 fusion.127
  71.5 41.5 %all-to-all-done = bf16[128,32,128]{2,1,0:T(8,128)(2,1)S(1)} async-done(((bf16[128,32,128]{2,1,0:T(8,128)(2,1)}), bf16[128,32,128]{2,1,0:T(8,128)(2,1)S(1)}, u32[]{:S(2)}, u32[]{:S(2)}) %all-to-all-start) | async-done | bytes 1048608 | tf_op jit(solution)/shard_map/all_to_all | solution.py:242
  114.6 1.8 fusion.150
  116.4 0.9 copy.87
  117.4 1.3 reshape_reshape.4
  118.8 0.9 copy.88
  119.8 1.0 pad_maximum_fusion.4
  121.7 1.1 copy-done.2
  124.5 1.0 fusion.25
  125.5 1.0 fusion.22
  126.6 1.0 add_reduce_fusion
  127.6 1.0 fusion.15
  128.7 1.0 fusion.4
  130.7 1.1 fusion.43
  131.9 1.1 fusion.40
  133.1 1.7 copy.107
  134.8 11.4 %all-to-all-start.1 = ((bf16[32,128,128]{2,0,1:T(8,128)(2,1)}), bf16[32,128,128]{2,0,1:T(8,128)(2,1)S(1)}, u32[]{:S(2)}, u32[]{:S(2)}) async-start(bf16[32,128,128]{2,0,1:T(8,128)(2,1)} %copy.107), calls=%async_computation.1 | async-start | bytes 2097152 | tf_op jit(solution)/shard_map/all_to_all | solution.py:254
  147.5 1.9 collective-permute-start.2
  149.5 3.0 %collective-permute-start.3 = (f32[1,4096]{1,0:T(1,128)S(1)}, f32[1,4096]{1,0:T(1,128)S(1)}, u32[]{:S(2)}, u32[]{:S(2)}) collective-permute-start(f32[1,4096]{1,0:T(1,128)S(1)} %get-tuple-element.63), channel_id=1, source_target_pairs={{0,256},{128,384},{256,0},{384,128},{1,257},{129,385},{257,1},{385... | collective-permute-start | bytes 49160 | tf_op jit(solution)/shard_map/ppermute | solution.py:30
  152.5 4.0 %collective-permute-start.4 = (f32[1,4096]{1,0:T(1,128)S(1)}, f32[1,4096]{1,0:T(1,128)S(1)}, u32[]{:S(2)}, u32[]{:S(2)}) collective-permute-start(f32[1,4096]{1,0:T(1,128)S(1)} %get-tuple-element.62), channel_id=1, source_target_pairs={{0,384},{128,0},{256,128},{384,256},{1,385},{129,1},{257,129},{385... | collective-permute-start | bytes 49160 | tf_op jit(solution)/shard_map/ppermute | solution.py:30
  156.6 42.3 %all-to-all-done.1 = bf16[32,128,128]{2,0,1:T(8,128)(2,1)S(1)} async-done(((bf16[32,128,128]{2,0,1:T(8,128)(2,1)}), bf16[32,128,128]{2,0,1:T(8,128)(2,1)S(1)}, u32[]{:S(2)}, u32[]{:S(2)}) %all-to-all-start.1) | async-done | bytes 1048608 | tf_op jit(solution)/shard_map/all_to_all | solution.py:254
  200.1 2.6 %collective-permute-start.1 = (bf16[2048,6]{1,0:T(8,128)(2,1)S(1)}, bf16[2048,6]{1,0:T(8,128)(2,1)S(1)}, u32[]{:S(2)}, u32[]{:S(2)}) collective-permute-start(bf16[2048,6]{1,0:T(8,128)(2,1)S(1)} %pad_maximum_fusion.6), channel_id=1, source_target_pairs={{1,0},{2,1},{3,2},{4,3},{5,4},{6,5},{7,6},{8,7},{9,8},{10,9},{11,1... | collective-permute-start | bytes 73736 | tf_op jit(solution)/shard_map/ppermute | solution.py:18
  203.6 21.1 %collective-permute-done.1 = bf16[2048,6]{1,0:T(8,128)(2,1)S(1)} collective-permute-done((bf16[2048,6]{1,0:T(8,128)(2,1)S(1)}, bf16[2048,6]{1,0:T(8,128)(2,1)S(1)}, u32[]{:S(2)}, u32[]{:S(2)}) %collective-permute-start.1) | collective-permute-done | bytes 24608 | tf_op jit(solution)/shard_map/ppermute | solution.py:18
  225.1 5.1 %fusion.53 = (bf16[2048,128]{1,0:T(8,128)(2,1)}, bf16[2048,128]{1,0:T(8,128)(2,1)}, bf16[2048,128]{1,0:T(8,128)(2,1)}) fusion(f32[2048,128]{1,0:T(8,128)S(1)} %convert_element_type.214, f32[2048,2]{1,0:T(8,128)S(1)} %get-tuple-element.38, f32[2048]{0:T(1024)S(1)} %bitcast.140, f32[2048]{0:T(1024)S(1)} %bitcast.141, f32[2048]{0:T(1024)S(1)} %bitcast.139, ...), kind=kLoop, calls=%fused_computation.53 | loop fusion | flops 6291456 | bytes 4792320 | tf_op jit(solution)/shard_map/convert_element_type | solution.py:286
  (84 shorter events, 16.4 us)
Async XLA Ops:
  0.6 63.3 %copy-start = (bf16[1,16384]{1,0:T(2,128)(2,1)S(1)}, bf16[1,16384]{1,0:T(2,128)(2,1)}, u32[]{:S(2)}) copy-start(bf16[1,16384]{1,0:T(2,128)(2,1)} %param.10) | copy-start | bytes 98308
  0.6 3.0 %copy-start.4 = (bf16[2048,128]{1,0:T(8,128)(2,1)S(1)}, bf16[2048,128]{1,0:T(8,128)(2,1)}, u32[]{:S(2)}) copy-start(bf16[2048,128]{1,0:T(8,128)(2,1)} %v_ref.1) | copy-start | bytes 1572868
  2.0 11.6 %copy-start.12 = (f32[3,2048]{1,0:T(4,128)S(1)}, f32[3,2048]{1,0:T(4,128)}, u32[]{:S(2)}) copy-start(f32[3,2048]{1,0:T(4,128)} %param.11) | copy-start | bytes 73732
  4.5 16.9 %collective-permute-start = (bf16[2048,6]{1,0:T(8,128)(2,1)S(1)}, bf16[2048,6]{1,0:T(8,128)(2,1)S(1)}, u32[]{:S(2)}, u32[]{:S(2)}) collective-permute-start(bf16[2048,6]{1,0:T(8,128)(2,1)S(1)} %copy.85), channel_id=1, source_target_pairs={{0,1},{1,2},{2,3},{3,4},{4,5},{5,6},{6,7},{7,8},{8,9},{9,10},{10,1... | collective-permute-start | bytes 73736 | tf_op jit(solution)/shard_map/ppermute | solution.py:18
  28.0 85.1 %all-to-all-start = ((bf16[128,32,128]{2,1,0:T(8,128)(2,1)}), bf16[128,32,128]{2,1,0:T(8,128)(2,1)S(1)}, u32[]{:S(2)}, u32[]{:S(2)}) async-start(bf16[128,32,128]{2,1,0:T(8,128)(2,1)} %bitcast.134), calls=%async_computation | async-start | bytes 2097152 | tf_op jit(solution)/shard_map/all_to_all | solution.py:242
  121.3 1.6 copy-start.2
  125.5 1.1 copy-start.5
  125.5 1.1 copy-start.6
  129.7 0.9 copy-start.9
  129.7 1.0 copy-start.10
  129.7 1.0 copy-start.11
  134.8 64.1 %all-to-all-start.1 = ((bf16[32,128,128]{2,0,1:T(8,128)(2,1)}), bf16[32,128,128]{2,0,1:T(8,128)(2,1)S(1)}, u32[]{:S(2)}, u32[]{:S(2)}) async-start(bf16[32,128,128]{2,0,1:T(8,128)(2,1)} %copy.107), calls=%async_computation.1 | async-start | bytes 2097152 | tf_op jit(solution)/shard_map/all_to_all | solution.py:254
  146.3 52.8 %copy-start.3 = (bf16[2048,128]{1,0:T(8,128)(2,1)S(1)}, bf16[2048,128]{1,0:T(8,128)(2,1)}, u32[]{:S(2)}) copy-start(bf16[2048,128]{1,0:T(8,128)(2,1)} %g_ref.1) | copy-start | bytes 1572868
  147.2 52.1 %copy-start.7 = (bf16[2048,128]{1,0:T(8,128)(2,1)S(1)}, bf16[2048,128]{1,0:T(8,128)(2,1)}, u32[]{:S(2)}) copy-start(bf16[2048,128]{1,0:T(8,128)(2,1)} %get-tuple-element.12) | copy-start | bytes 1572868
  147.2 52.1 %copy-start.8 = (bf16[2048,128]{1,0:T(8,128)(2,1)S(1)}, bf16[2048,128]{1,0:T(8,128)(2,1)}, u32[]{:S(2)}) copy-start(bf16[2048,128]{1,0:T(8,128)(2,1)} %get-tuple-element.11) | copy-start | bytes 1572868
  147.5 55.1 %collective-permute-start.2 = (f32[1,4096]{1,0:T(1,128)S(1)}, f32[1,4096]{1,0:T(1,128)S(1)}, u32[]{:S(2)}, u32[]{:S(2)}) collective-permute-start(f32[1,4096]{1,0:T(1,128)S(1)} %get-tuple-element.61), channel_id=1, source_target_pairs={{0,128},{128,256},{256,384},{384,0},{1,129},{129,257},{257,385},{3... | collective-permute-start | bytes 49160 | tf_op jit(solution)/shard_map/ppermute | solution.py:30
  149.5 53.2 %collective-permute-start.3 = (f32[1,4096]{1,0:T(1,128)S(1)}, f32[1,4096]{1,0:T(1,128)S(1)}, u32[]{:S(2)}, u32[]{:S(2)}) collective-permute-start(f32[1,4096]{1,0:T(1,128)S(1)} %get-tuple-element.63), channel_id=1, source_target_pairs={{0,256},{128,384},{256,0},{384,128},{1,257},{129,385},{257,1},{385... | collective-permute-start | bytes 49160 | tf_op jit(solution)/shard_map/ppermute | solution.py:30
  152.5 50.1 %collective-permute-start.4 = (f32[1,4096]{1,0:T(1,128)S(1)}, f32[1,4096]{1,0:T(1,128)S(1)}, u32[]{:S(2)}, u32[]{:S(2)}) collective-permute-start(f32[1,4096]{1,0:T(1,128)S(1)} %get-tuple-element.62), channel_id=1, source_target_pairs={{0,384},{128,0},{256,128},{384,256},{1,385},{129,1},{257,129},{385... | collective-permute-start | bytes 49160 | tf_op jit(solution)/shard_map/ppermute | solution.py:30
  200.1 24.6 %collective-permute-start.1 = (bf16[2048,6]{1,0:T(8,128)(2,1)S(1)}, bf16[2048,6]{1,0:T(8,128)(2,1)S(1)}, u32[]{:S(2)}, u32[]{:S(2)}) collective-permute-start(bf16[2048,6]{1,0:T(8,128)(2,1)S(1)} %pad_maximum_fusion.6), channel_id=1, source_target_pairs={{1,0},{2,1},{3,2},{4,3},{5,4},{6,5},{7,6},{8,7},{9,8},{10,9},{11,1... | collective-permute-start | bytes 73736 | tf_op jit(solution)/shard_map/ppermute | solution.py:18
  225.1 5.2 %copy-start.1 = (bf16[1,16384]{1,0:T(2,128)(2,1)S(1)}, bf16[1,16384]{1,0:T(2,128)(2,1)}, u32[]{:S(2)}) copy-start(bf16[1,16384]{1,0:T(2,128)(2,1)} %param.10) | copy-start | bytes 98308

commit v9 on v5

--- a/solution.py
+++ b/solution.py
@@ -262,9 +262,6 @@
     grad_vconv = (grad_gated_tok.astype(jnp.float32) * key_conv.astype(jnp.float32)).astype(
         jnp.bfloat16
     )
-    grad_qconv, grad_kconv, grad_vconv = lax.optimization_barrier(
-        (grad_qconv, grad_kconv, grad_vconv)
-    )
     heads = jnp.concatenate([grad_qconv[:, :2], grad_kconv[:, :2], grad_vconv[:, :2]], axis=1)
     heads = shifted(heads, "ctx", -1)
     following = (heads[:, 0:2], heads[:, 2:4], heads[:, 4:6])

time: 227 us -> 228 us (level)
  no operation moved by 1% of the time
where the time goes in v9:
time: 228 us
  waiting for transfers between devices  110 us (48%)
  starting transfers between devices  68.1 us (30%)
  other arithmetic  17.7 us (8%)
  local copies, waits for them, and re-layouts  14.5 us (6%)
  matrix products  9.66 us (4%)
  Pallas kernels  5.78 us (3%)
    all_to_all x1, waiting for transfers between devices, per_device(): lax.all_to_all(returning, 'ctx', split_axis=1, concat_axis=0, tiled=True)  42.3 us
    all_to_all x1, waiting for transfers between devices, per_device(): lax.all_to_all(outgoing, 'ctx', split_axis=0, concat_axis=1, tiled=True)  40.3 us
    all_to_all x1, starting transfers between devices, per_device(): lax.all_to_all(outgoing, 'ctx', split_axis=0, concat_axis=1, tiled=True)  35.9 us
    ppermute x2, waiting for transfers between devices, shifted(): return lax.ppermute(array, axis, pairs)  27.8 us
    ppermute x2, starting transfers between devices, shifted(): return lax.ppermute(array, axis, pairs)  11.6 us
    all_to_all x1, starting transfers between devices, per_device(): lax.all_to_all(returning, 'ctx', split_axis=1, concat_axis=0, tiled=True)  11.6 us
    ppermute x3, starting transfers between devices, ring_scatter_sum(): total = total + lax.ppermute(piece, axis, pairs)  9 us
    pallas_call x1, Pallas kernels, front(): pl.pallas_call(functools.partial(front_kernel, chan_dev), grid=(all_chans...  5.78 us
  transfers between devices with their start and end apart: 7, of which 4 were waited for; matrix products, arithmetic and copies ran while one was open for 6% of the time, Pallas kernels for 0%

profile of v9, /device:TPU:25, one launch (start us, length us, event | category | flops | bytes accessed | tf_op | source)
XLA Modules:
  0.0 227.5 jit_solution(8782061965876610663)
XLA Ops:
  0.7 1.3 slice.160
  2.2 1.3 slice.161
  4.5 9.0 %collective-permute-start = (bf16[2048,6]{1,0:T(8,128)(2,1)S(1)}, bf16[2048,6]{1,0:T(8,128)(2,1)S(1)}, u32[]{:S(2)}, u32[]{:S(2)}) collective-permute-start(bf16[2048,6]{1,0:T(8,128)(2,1)S(1)} %copy.85), channel_id=1, source_target_pairs={{0,1},{1,2},{2,3},{3,4},{4,5},{5,6},{6,7},{7,8},{8,9},{9,10},{10,1... | collective-permute-start | bytes 73736 | tf_op jit(solution)/shard_map/ppermute | solution.py:18
  13.6 1.4 copy.86
  14.9 6.5 %collective-permute-done = bf16[2048,6]{1,0:T(8,128)(2,1)S(1)} collective-permute-done((bf16[2048,6]{1,0:T(8,128)(2,1)S(1)}, bf16[2048,6]{1,0:T(8,128)(2,1)S(1)}, u32[]{:S(2)}, u32[]{:S(2)}) %collective-permute-start) | collective-permute-done | bytes 24608 | tf_op jit(solution)/shard_map/ppermute | solution.py:18
  21.4 0.8 broadcast_select_fusion.halo_ref
  22.2 5.8 %shard_map.93 = (bf16[2048,128]{1,0:T(8,128)(2,1)}, bf16[2048,128]{1,0:T(8,128)(2,1)}, bf16[2048,128]{1,0:T(8,128)(2,1)}, bf16[4096,128]{1,0:T(8,128)(2,1)}) custom-call(bf16[2048,128]{1,0:T(8,128)(2,1)} %q_ref.1, bf16[2048,128]{1,0:T(8,128)(2,1)} %k_ref.1, bf16[2048,128]{1,0:T(8,128)(2,1)} %v_ref.1, bf16[2048,128]{1,0:T(8,128)(2,1)} %g_ref.1, ...), custom_call_target="tpu_custom_call" | custom-call | flops 7864320 | bytes 4718592 | tf_op jit(solution)/shard_map/pallas_call | solution.py:154
  28.0 35.9 %all-to-all-start = ((bf16[128,32,128]{2,1,0:T(8,128)(2,1)}), bf16[128,32,128]{2,1,0:T(8,128)(2,1)S(1)}, u32[]{:S(2)}, u32[]{:S(2)}) async-start(bf16[128,32,128]{2,1,0:T(8,128)(2,1)} %bitcast.123), calls=%async_computation | async-start | bytes 2097152 | tf_op jit(solution)/shard_map/all_to_all | solution.py:235
  65.2 1.2 fusion.123
  69.1 1.2 fusion.130
  70.3 1.3 fusion.125
  71.5 1.2 fusion.127
  72.8 40.3 %all-to-all-done = bf16[128,32,128]{2,1,0:T(8,128)(2,1)S(1)} async-done(((bf16[128,32,128]{2,1,0:T(8,128)(2,1)}), bf16[128,32,128]{2,1,0:T(8,128)(2,1)S(1)}, u32[]{:S(2)}, u32[]{:S(2)}) %all-to-all-start) | async-done | bytes 1048608 | tf_op jit(solution)/shard_map/all_to_all | solution.py:235
  114.1 1.0 copy.100
  115.1 1.0 copy.99
  118.0 1.0 fusion.69
  119.1 1.0 fusion.70
  120.7 1.0 fusion.25
  121.8 1.3 fusion.22
  123.9 1.0 fusion.15
  125.0 1.0 fusion.4
  127.0 1.1 fusion.43
  128.1 1.1 fusion.40
  129.4 1.7 copy.107
  131.1 11.6 %all-to-all-start.1 = ((bf16[32,128,128]{2,0,1:T(8,128)(2,1)}), bf16[32,128,128]{2,0,1:T(8,128)(2,1)S(1)}, u32[]{:S(2)}, u32[]{:S(2)}) async-start(bf16[32,128,128]{2,0,1:T(8,128)(2,1)} %copy.107), calls=%async_computation.1 | async-start | bytes 2097152 | tf_op jit(solution)/shard_map/all_to_all | solution.py:247
  144.0 1.9 collective-permute-start.2
  146.0 3.0 %collective-permute-start.3 = (f32[1,4096]{1,0:T(1,128)S(1)}, f32[1,4096]{1,0:T(1,128)S(1)}, u32[]{:S(2)}, u32[]{:S(2)}) collective-permute-start(f32[1,4096]{1,0:T(1,128)S(1)} %get-tuple-element.63), channel_id=1, source_target_pairs={{0,256},{128,384},{256,0},{384,128},{1,257},{129,385},{257,1},{385... | collective-permute-start | bytes 49160 | tf_op jit(solution)/shard_map/ppermute | solution.py:30
  149.0 4.0 %collective-permute-start.4 = (f32[1,4096]{1,0:T(1,128)S(1)}, f32[1,4096]{1,0:T(1,128)S(1)}, u32[]{:S(2)}, u32[]{:S(2)}) collective-permute-start(f32[1,4096]{1,0:T(1,128)S(1)} %get-tuple-element.62), channel_id=1, source_target_pairs={{0,384},{128,0},{256,128},{384,256},{1,385},{129,1},{257,129},{385... | collective-permute-start | bytes 49160 | tf_op jit(solution)/shard_map/ppermute | solution.py:30
  153.1 42.3 %all-to-all-done.1 = bf16[32,128,128]{2,0,1:T(8,128)(2,1)S(1)} async-done(((bf16[32,128,128]{2,0,1:T(8,128)(2,1)}), bf16[32,128,128]{2,0,1:T(8,128)(2,1)S(1)}, u32[]{:S(2)}, u32[]{:S(2)}) %all-to-all-start.1) | async-done | bytes 1048608 | tf_op jit(solution)/shard_map/all_to_all | solution.py:247
  197.4 2.6 %collective-permute-start.1 = (bf16[2048,6]{1,0:T(8,128)(2,1)S(1)}, bf16[2048,6]{1,0:T(8,128)(2,1)S(1)}, u32[]{:S(2)}, u32[]{:S(2)}) collective-permute-start(bf16[2048,6]{1,0:T(8,128)(2,1)S(1)} %pad_maximum_fusion.6), channel_id=1, source_target_pairs={{1,0},{2,1},{3,2},{4,3},{5,4},{6,5},{7,6},{8,7},{9,8},{10,9},{11,1... | collective-permute-start | bytes 73736 | tf_op jit(solution)/shard_map/ppermute | solution.py:18
  200.6 21.3 %collective-permute-done.1 = bf16[2048,6]{1,0:T(8,128)(2,1)S(1)} collective-permute-done((bf16[2048,6]{1,0:T(8,128)(2,1)S(1)}, bf16[2048,6]{1,0:T(8,128)(2,1)S(1)}, u32[]{:S(2)}, u32[]{:S(2)}) %collective-permute-start.1) | collective-permute-done | bytes 24608 | tf_op jit(solution)/shard_map/ppermute | solution.py:18
  222.4 5.1 %fusion.52 = (bf16[2048,128]{1,0:T(8,128)(2,1)}, bf16[2048,128]{1,0:T(8,128)(2,1)}, bf16[2048,128]{1,0:T(8,128)(2,1)}) fusion(f32[2048,128]{1,0:T(8,128)S(1)} %get-tuple-element.45, f32[2048,2]{1,0:T(8,128)S(1)} %get-tuple-element.42, f32[2048]{0:T(1024)S(1)} %bitcast.129, f32[2048]{0:T(1024)S(1)} %bitcast.130, f32[2048]{0:T(1024)S(1)} %bitcast.128, ...), kind=kLoop, calls=%fused_computation.50 | loop fusion | flops 6291456 | bytes 4792320 | tf_op jit(solution)/shard_map/convert_element_type | solution.py:276
  (96 shorter events, 15.0 us)
Async XLA Ops:
  0.6 63.3 %copy-start = (bf16[1,16384]{1,0:T(2,128)(2,1)S(1)}, bf16[1,16384]{1,0:T(2,128)(2,1)}, u32[]{:S(2)}) copy-start(bf16[1,16384]{1,0:T(2,128)(2,1)} %param.10) | copy-start | bytes 98308
  0.6 3.0 %copy-start.5 = (bf16[2048,128]{1,0:T(8,128)(2,1)S(1)}, bf16[2048,128]{1,0:T(8,128)(2,1)}, u32[]{:S(2)}) copy-start(bf16[2048,128]{1,0:T(8,128)(2,1)} %v_ref.1) | copy-start | bytes 1572868
  2.0 11.6 %copy-start.21 = (f32[3,2048]{1,0:T(4,128)S(1)}, f32[3,2048]{1,0:T(4,128)}, u32[]{:S(2)}) copy-start(f32[3,2048]{1,0:T(4,128)} %param.11) | copy-start | bytes 73732
  4.5 16.9 %collective-permute-start = (bf16[2048,6]{1,0:T(8,128)(2,1)S(1)}, bf16[2048,6]{1,0:T(8,128)(2,1)S(1)}, u32[]{:S(2)}, u32[]{:S(2)}) collective-permute-start(bf16[2048,6]{1,0:T(8,128)(2,1)S(1)} %copy.85), channel_id=1, source_target_pairs={{0,1},{1,2},{2,3},{3,4},{4,5},{5,6},{6,7},{7,8},{8,9},{9,10},{10,1... | collective-permute-start | bytes 73736 | tf_op jit(solution)/shard_map/ppermute | solution.py:18
  28.0 85.1 %all-to-all-start = ((bf16[128,32,128]{2,1,0:T(8,128)(2,1)}), bf16[128,32,128]{2,1,0:T(8,128)(2,1)S(1)}, u32[]{:S(2)}, u32[]{:S(2)}) async-start(bf16[128,32,128]{2,1,0:T(8,128)(2,1)} %bitcast.123), calls=%async_computation | async-start | bytes 2097152 | tf_op jit(solution)/shard_map/all_to_all | solution.py:235
  66.3 46.7 %copy-start.2 = (f32[128,256]{1,0:T(8,128)}, f32[128,256]{1,0:T(8,128)S(1)}, u32[]{:S(2)}) copy-start(f32[128,256]{1,0:T(8,128)S(1)} %get-tuple-element.73) | copy-start | bytes 393220
  116.7 1.0 copy-start.6
  116.7 1.2 copy-start.7
  116.9 1.0 copy-start.3
  116.9 1.1 copy-start.10
  119.1 1.0 copy-start.8
  119.1 1.0 copy-start.9
  121.8 1.3 copy-start.11
  121.8 1.3 copy-start.12
  126.0 0.9 copy-start.15
  126.0 1.0 copy-start.17
  126.0 1.0 copy-start.19
  129.4 13.4 %copy-start.16 = (f32[256,128]{0,1:T(8,128)S(1)}, f32[256,128]{0,1:T(8,128)}, u32[]{:S(2)}) copy-start(f32[256,128]{0,1:T(8,128)} %fusion.130) | copy-start | bytes 393220
  129.4 13.4 %copy-start.18 = (f32[256,128]{0,1:T(8,128)S(1)}, f32[256,128]{0,1:T(8,128)}, u32[]{:S(2)}) copy-start(f32[256,128]{0,1:T(8,128)} %get-tuple-element.80) | copy-start | bytes 393220
  129.4 13.4 %copy-start.20 = (f32[256,128]{0,1:T(8,128)S(1)}, f32[256,128]{0,1:T(8,128)}, u32[]{:S(2)}) copy-start(f32[256,128]{0,1:T(8,128)} %get-tuple-element.81) | copy-start | bytes 393220
  131.1 11.7 %copy-start.22 = (f32[3,2048]{1,0:T(4,128)S(1)}, f32[3,2048]{1,0:T(4,128)}, u32[]{:S(2)}) copy-start(f32[3,2048]{1,0:T(4,128)} %param.11) | copy-start | bytes 73732
  131.1 64.3 %all-to-all-start.1 = ((bf16[32,128,128]{2,0,1:T(8,128)(2,1)}), bf16[32,128,128]{2,0,1:T(8,128)(2,1)S(1)}, u32[]{:S(2)}, u32[]{:S(2)}) async-start(bf16[32,128,128]{2,0,1:T(8,128)(2,1)} %copy.107), calls=%async_computation.1 | async-start | bytes 2097152 | tf_op jit(solution)/shard_map/all_to_all | solution.py:247
  142.9 52.7 %copy-start.4 = (bf16[2048,128]{1,0:T(8,128)(2,1)S(1)}, bf16[2048,128]{1,0:T(8,128)(2,1)}, u32[]{:S(2)}) copy-start(bf16[2048,128]{1,0:T(8,128)(2,1)} %g_ref.1) | copy-start | bytes 1572868
  144.0 55.9 %collective-permute-start.2 = (f32[1,4096]{1,0:T(1,128)S(1)}, f32[1,4096]{1,0:T(1,128)S(1)}, u32[]{:S(2)}, u32[]{:S(2)}) collective-permute-start(f32[1,4096]{1,0:T(1,128)S(1)} %get-tuple-element.61), channel_id=1, source_target_pairs={{0,128},{128,256},{256,384},{384,0},{1,129},{129,257},{257,385},{3... | collective-permute-start | bytes 49160 | tf_op jit(solution)/shard_map/ppermute | solution.py:30
  146.0 54.0 %collective-permute-start.3 = (f32[1,4096]{1,0:T(1,128)S(1)}, f32[1,4096]{1,0:T(1,128)S(1)}, u32[]{:S(2)}, u32[]{:S(2)}) collective-permute-start(f32[1,4096]{1,0:T(1,128)S(1)} %get-tuple-element.63), channel_id=1, source_target_pairs={{0,256},{128,384},{256,0},{384,128},{1,257},{129,385},{257,1},{385... | collective-permute-start | bytes 49160 | tf_op jit(solution)/shard_map/ppermute | solution.py:30
  149.0 51.0 %collective-permute-start.4 = (f32[1,4096]{1,0:T(1,128)S(1)}, f32[1,4096]{1,0:T(1,128)S(1)}, u32[]{:S(2)}, u32[]{:S(2)}) collective-permute-start(f32[1,4096]{1,0:T(1,128)S(1)} %get-tuple-element.62), channel_id=1, source_target_pairs={{0,384},{128,0},{256,128},{384,256},{1,385},{129,1},{257,129},{385... | collective-permute-start | bytes 49160 | tf_op jit(solution)/shard_map/ppermute | solution.py:30
  195.4 1.0 copy-start.13
  195.4 1.2 copy-start.14
  197.4 24.6 %collective-permute-start.1 = (bf16[2048,6]{1,0:T(8,128)(2,1)S(1)}, bf16[2048,6]{1,0:T(8,128)(2,1)S(1)}, u32[]{:S(2)}, u32[]{:S(2)}) collective-permute-start(bf16[2048,6]{1,0:T(8,128)(2,1)S(1)} %pad_maximum_fusion.6), channel_id=1, source_target_pairs={{1,0},{2,1},{3,2},{4,3},{5,4},{6,5},{7,6},{8,7},{9,8},{10,9},{11,1... | collective-permute-start | bytes 73736 | tf_op jit(solution)/shard_map/ppermute | solution.py:18
  222.4 5.2 %copy-start.1 = (bf16[1,16384]{1,0:T(2,128)(2,1)S(1)}, bf16[1,16384]{1,0:T(2,128)(2,1)}, u32[]{:S(2)}) copy-start(bf16[1,16384]{1,0:T(2,128)(2,1)} %param.10) | copy-start | bytes 98308

commit v10 on v5

--- a/solution.py
+++ b/solution.py
@@ -116,10 +116,10 @@
 BLOCK_ROWS = 1024
 
 
-def front_kernel(chan_dev, q_ref, k_ref, v_ref, g_ref, halo_ref, taps_ref, qc_ref, kc_ref, vc_ref, out_ref):
+def front_kernel(chan_dev, keep_ref, q_ref, k_ref, v_ref, g_ref, halo_ref, taps_ref, qc_ref, kc_ref, vc_ref, out_ref):
     rows, cols = q_ref.shape
     lane = lax.broadcasted_iota(jnp.int32, (rows, cols), 1)
-    halo = halo_ref[...].astype(jnp.float32)
+    halo = halo_ref[...].astype(jnp.float32) * keep_ref[0, 0]
     taps = taps_ref[...]
     first, second, third = taps[:, 0:1], taps[:, 1:2], taps[:, 2:3]
 
@@ -147,21 +147,22 @@
         ]
 
 
-def front(query_proj, key_proj, value_proj, grad_out, halo, taps_cols, chan_dev):
+def front(query_proj, key_proj, value_proj, grad_out, halo, taps_cols, chan_dev, keep):
     all_chans, tok_cols = query_proj.shape
     block = min(BLOCK_ROWS, all_chans)
     tile = pl.BlockSpec((block, tok_cols), lambda i: (i, 0))
     return pl.pallas_call(
         functools.partial(front_kernel, chan_dev),
         grid=(all_chans // block,),
-        in_specs=[tile, tile, tile, tile, pl.BlockSpec((block, 6), lambda i: (i, 0)),
+        in_specs=[pl.BlockSpec(memory_space=pltpu.SMEM), tile, tile, tile, tile,
+                  pl.BlockSpec((block, 6), lambda i: (i, 0)),
                   pl.BlockSpec((block, 3), lambda i: (i, 0))],
         out_specs=[tile, tile, tile, pl.BlockSpec((2 * block, tok_cols), lambda i: (i, 0))],
         out_shape=[jax.ShapeDtypeStruct((all_chans, tok_cols), jnp.bfloat16)] * 3
         + [jax.ShapeDtypeStruct((2 * all_chans, tok_cols), jnp.bfloat16)],
         cost_estimate=pl.CostEstimate(flops=30 * all_chans * tok_cols, transcendentals=0,
                                       bytes_accessed=18 * all_chans * tok_cols),
-    )(query_proj, key_proj, value_proj, grad_out, halo, taps_cols)
+    )(keep.reshape(1, 1), query_proj, key_proj, value_proj, grad_out, halo, taps_cols)
 
 
 def taps_forward(current, earlier, short_taps):
@@ -201,9 +202,8 @@
     inner = tables[4].shape[1]
     tails = jnp.concatenate([query_proj[:, -2:], key_proj[:, -2:], value_proj[:, -2:]], axis=1)
     tails = shifted(tails, "ctx", 1)
-    halo = jnp.where(keep_prev > 0, tails, jnp.zeros_like(tails))
     query_conv, key_conv, value_conv, outgoing = front(
-        query_proj, key_proj, value_proj, grad_out, halo, short_taps.T, chan_dev
+        query_proj, key_proj, value_proj, grad_out, tails, short_taps.T, chan_dev, keep_prev
     )
     filter_spec = forward_spectrum(filters.astype(jnp.float32), None, tables)
     filter_real = filter_spec[:, None, :, :inner]

time: 227 us -> 228 us (level)
  no operation moved by 1% of the time
where the time goes in v10:
time: 228 us; the launch traced here: 227 us
  waiting for transfers between devices  110 us (48%)
  starting transfers between devices  68.1 us (30%)
  other arithmetic  17.1 us (8%)
  local copies, waits for them, and re-layouts  15.1 us (7%)
  matrix products  9.67 us (4%)
  Pallas kernels  6.39 us (3%)
    all_to_all x1, waiting for transfers between devices, per_device(): lax.all_to_all(returning, 'ctx', split_axis=1, concat_axis=0, tiled=True)  41.7 us
    all_to_all x1, waiting for transfers between devices, per_device(): lax.all_to_all(outgoing, 'ctx', split_axis=0, concat_axis=1, tiled=True)  40.3 us
    all_to_all x1, starting transfers between devices, per_device(): lax.all_to_all(outgoing, 'ctx', split_axis=0, concat_axis=1, tiled=True)  35.9 us
    ppermute x2, waiting for transfers between devices, shifted(): return lax.ppermute(array, axis, pairs)  27.5 us
    ppermute x2, starting transfers between devices, shifted(): return lax.ppermute(array, axis, pairs)  11.6 us
    all_to_all x1, starting transfers between devices, per_device(): lax.all_to_all(returning, 'ctx', split_axis=1, concat_axis=0, tiled=True)  11.5 us
    ppermute x3, starting transfers between devices, ring_scatter_sum(): total = total + lax.ppermute(piece, axis, pairs)  9 us
    pallas_call x1, Pallas kernels, front(): pl.pallas_call(functools.partial(front_kernel, chan_dev), grid=(all_chans...  6.39 us
  transfers between devices with their start and end apart: 7, of which 4 were waited for; matrix products, arithmetic and copies ran while one was open for 6% of the time, Pallas kernels for 0%

profile of v10, /device:TPU:25, one launch (start us, length us, event | category | flops | bytes accessed | tf_op | source)
XLA Modules:
  0.0 227.2 jit_solution(11613908094295051976)
XLA Ops:
  0.7 1.3 slice.160
  2.2 1.3 slice.161
  4.5 9.0 %collective-permute-start = (bf16[2048,6]{1,0:T(8,128)(2,1)S(1)}, bf16[2048,6]{1,0:T(8,128)(2,1)S(1)}, u32[]{:S(2)}, u32[]{:S(2)}) collective-permute-start(bf16[2048,6]{1,0:T(8,128)(2,1)S(1)} %copy.85), channel_id=1, source_target_pairs={{0,1},{1,2},{2,3},{3,4},{4,5},{5,6},{6,7},{7,8},{8,9},{9,10},{10,1... | collective-permute-start | bytes 73736 | tf_op jit(solution)/shard_map/ppermute | solution.py:18
  13.5 1.4 copy.86
  14.9 6.5 %collective-permute-done.halo_ref = bf16[2048,6]{1,0:T(8,128)(2,1)S(1)} collective-permute-done((bf16[2048,6]{1,0:T(8,128)(2,1)S(1)}, bf16[2048,6]{1,0:T(8,128)(2,1)S(1)}, u32[]{:S(2)}, u32[]{:S(2)}) %collective-permute-start) | collective-permute-done | bytes 24608 | tf_op jit(solution)/shard_map/ppermute | solution.py:18
  22.2 6.4 %shard_map.93 = (bf16[2048,128]{1,0:T(8,128)(2,1)}, bf16[2048,128]{1,0:T(8,128)(2,1)}, bf16[2048,128]{1,0:T(8,128)(2,1)}, bf16[4096,128]{1,0:T(8,128)(2,1)}) custom-call(f32[1,1]{1,0:T(1,128)} %bitcast.2.keep_ref, bf16[2048,128]{1,0:T(8,128)(2,1)} %q_ref.1, bf16[2048,128]{1,0:T(8,128)(2,1)} %k_ref.1, bf16[2048,128]{1,0:T(8,128)(2,1)} %v_ref.1, ...), custom_call_target="tpu_custom_call" | custom-call | flops 7864320 | bytes 4718592 | tf_op jit(solution)/shard_map/pallas_call | solution.py:154
  28.6 35.9 %all-to-all-start = ((bf16[128,32,128]{2,1,0:T(8,128)(2,1)}), bf16[128,32,128]{2,1,0:T(8,128)(2,1)S(1)}, u32[]{:S(2)}, u32[]{:S(2)}) async-start(bf16[128,32,128]{2,1,0:T(8,128)(2,1)} %bitcast.121), calls=%async_computation | async-start | bytes 2097152 | tf_op jit(solution)/shard_map/all_to_all | solution.py:235
  65.7 1.2 fusion.123
  69.7 1.1 fusion.130
  70.8 1.3 fusion.125
  72.1 1.2 fusion.127
  73.3 40.3 %all-to-all-done = bf16[128,32,128]{2,1,0:T(8,128)(2,1)S(1)} async-done(((bf16[128,32,128]{2,1,0:T(8,128)(2,1)}), bf16[128,32,128]{2,1,0:T(8,128)(2,1)S(1)}, u32[]{:S(2)}, u32[]{:S(2)}) %all-to-all-start) | async-done | bytes 1048608 | tf_op jit(solution)/shard_map/all_to_all | solution.py:235
  114.6 1.0 copy.100
  115.6 1.0 copy.99
  118.6 1.0 fusion.69
  119.7 1.0 fusion.70
  121.3 1.0 fusion.25
  122.4 1.3 fusion.22
  123.7 0.8 add_reduce_fusion
  124.5 1.0 fusion.15
  125.5 1.0 fusion.4
  127.6 1.1 fusion.43
  128.7 1.1 fusion.40
  130.0 1.7 copy.107
  131.7 11.5 %all-to-all-start.1 = ((bf16[32,128,128]{2,0,1:T(8,128)(2,1)}), bf16[32,128,128]{2,0,1:T(8,128)(2,1)S(1)}, u32[]{:S(2)}, u32[]{:S(2)}) async-start(bf16[32,128,128]{2,0,1:T(8,128)(2,1)} %copy.107), calls=%async_computation.1 | async-start | bytes 2097152 | tf_op jit(solution)/shard_map/all_to_all | solution.py:247
  145.2 1.9 collective-permute-start.2
  147.1 3.1 %collective-permute-start.3 = (f32[1,4096]{1,0:T(1,128)S(1)}, f32[1,4096]{1,0:T(1,128)S(1)}, u32[]{:S(2)}, u32[]{:S(2)}) collective-permute-start(f32[1,4096]{1,0:T(1,128)S(1)} %get-tuple-element.63), channel_id=1, source_target_pairs={{0,256},{128,384},{256,0},{384,128},{1,257},{129,385},{257,1},{385... | collective-permute-start | bytes 49160 | tf_op jit(solution)/shard_map/ppermute | solution.py:30
  150.2 4.0 %collective-permute-start.4 = (f32[1,4096]{1,0:T(1,128)S(1)}, f32[1,4096]{1,0:T(1,128)S(1)}, u32[]{:S(2)}, u32[]{:S(2)}) collective-permute-start(f32[1,4096]{1,0:T(1,128)S(1)} %get-tuple-element.62), channel_id=1, source_target_pairs={{0,384},{128,0},{256,128},{384,256},{1,385},{129,1},{257,129},{385... | collective-permute-start | bytes 49160 | tf_op jit(solution)/shard_map/ppermute | solution.py:30
  154.2 41.7 %all-to-all-done.1 = bf16[32,128,128]{2,0,1:T(8,128)(2,1)S(1)} async-done(((bf16[32,128,128]{2,0,1:T(8,128)(2,1)}), bf16[32,128,128]{2,0,1:T(8,128)(2,1)S(1)}, u32[]{:S(2)}, u32[]{:S(2)}) %all-to-all-start.1) | async-done | bytes 1048608 | tf_op jit(solution)/shard_map/all_to_all | solution.py:247
  197.1 2.6 %collective-permute-start.1 = (bf16[2048,6]{1,0:T(8,128)(2,1)S(1)}, bf16[2048,6]{1,0:T(8,128)(2,1)S(1)}, u32[]{:S(2)}, u32[]{:S(2)}) collective-permute-start(bf16[2048,6]{1,0:T(8,128)(2,1)S(1)} %pad_maximum_fusion.6), channel_id=1, source_target_pairs={{1,0},{2,1},{3,2},{4,3},{5,4},{6,5},{7,6},{8,7},{9,8},{10,9},{11,1... | collective-permute-start | bytes 73736 | tf_op jit(solution)/shard_map/ppermute | solution.py:18
  200.6 21.1 %collective-permute-done.1 = bf16[2048,6]{1,0:T(8,128)(2,1)S(1)} collective-permute-done((bf16[2048,6]{1,0:T(8,128)(2,1)S(1)}, bf16[2048,6]{1,0:T(8,128)(2,1)S(1)}, u32[]{:S(2)}, u32[]{:S(2)}) %collective-permute-start.1) | collective-permute-done | bytes 24608 | tf_op jit(solution)/shard_map/ppermute | solution.py:18
  222.1 5.1 %fusion.52 = (bf16[2048,128]{1,0:T(8,128)(2,1)}, bf16[2048,128]{1,0:T(8,128)(2,1)}, bf16[2048,128]{1,0:T(8,128)(2,1)}) fusion(f32[2048,128]{1,0:T(8,128)S(1)} %convert_element_type.220, f32[2048,2]{1,0:T(8,128)S(1)} %get-tuple-element.42, f32[2048]{0:T(1024)S(1)} %bitcast.127, f32[2048]{0:T(1024)S(1)} %bitcast.128, f32[2048]{0:T(1024)S(1)} %bitcast.126, ...), kind=kLoop, calls=%fused_computation.50 | loop fusion | flops 6291456 | bytes 4792320 | tf_op jit(solution)/shard_map/convert_element_type | solution.py:279
  (102 shorter events, 14.9 us)
Async XLA Ops:
  0.6 63.9 %copy-start = (bf16[1,16384]{1,0:T(2,128)(2,1)S(1)}, bf16[1,16384]{1,0:T(2,128)(2,1)}, u32[]{:S(2)}) copy-start(bf16[1,16384]{1,0:T(2,128)(2,1)} %param.10) | copy-start | bytes 98308
  0.6 3.0 %copy-start.5 = (bf16[2048,128]{1,0:T(8,128)(2,1)S(1)}, bf16[2048,128]{1,0:T(8,128)(2,1)}, u32[]{:S(2)}) copy-start(bf16[2048,128]{1,0:T(8,128)(2,1)} %v_ref.1) | copy-start | bytes 1572868
  2.0 11.6 %copy-start.22 = (f32[3,2048]{1,0:T(4,128)S(1)}, f32[3,2048]{1,0:T(4,128)}, u32[]{:S(2)}) copy-start(f32[3,2048]{1,0:T(4,128)} %param.11) | copy-start | bytes 73732
  4.5 16.9 %collective-permute-start = (bf16[2048,6]{1,0:T(8,128)(2,1)S(1)}, bf16[2048,6]{1,0:T(8,128)(2,1)S(1)}, u32[]{:S(2)}, u32[]{:S(2)}) collective-permute-start(bf16[2048,6]{1,0:T(8,128)(2,1)S(1)} %copy.85), channel_id=1, source_target_pairs={{0,1},{1,2},{2,3},{3,4},{4,5},{5,6},{6,7},{7,8},{8,9},{9,10},{10,1... | collective-permute-start | bytes 73736 | tf_op jit(solution)/shard_map/ppermute | solution.py:18
  21.4 0.8 copy-start.21
  28.6 85.1 %all-to-all-start = ((bf16[128,32,128]{2,1,0:T(8,128)(2,1)}), bf16[128,32,128]{2,1,0:T(8,128)(2,1)S(1)}, u32[]{:S(2)}, u32[]{:S(2)}) async-start(bf16[128,32,128]{2,1,0:T(8,128)(2,1)} %bitcast.121), calls=%async_computation | async-start | bytes 2097152 | tf_op jit(solution)/shard_map/all_to_all | solution.py:235
  66.9 46.7 %copy-start.2 = (f32[128,256]{1,0:T(8,128)}, f32[128,256]{1,0:T(8,128)S(1)}, u32[]{:S(2)}) copy-start(f32[128,256]{1,0:T(8,128)S(1)} %get-tuple-element.73) | copy-start | bytes 393220
  117.3 1.0 copy-start.6
  117.3 1.2 copy-start.7
  117.5 1.0 copy-start.3
  117.5 1.1 copy-start.10
  119.6 1.0 copy-start.8
  119.7 1.0 copy-start.9
  122.4 1.3 copy-start.11
  122.4 1.3 copy-start.12
  126.6 0.9 copy-start.15
  126.6 1.0 copy-start.17
  126.6 1.0 copy-start.19
  130.0 13.3 %copy-start.16 = (f32[256,128]{0,1:T(8,128)S(1)}, f32[256,128]{0,1:T(8,128)}, u32[]{:S(2)}) copy-start(f32[256,128]{0,1:T(8,128)} %fusion.130) | copy-start | bytes 393220
  130.0 13.3 %copy-start.18 = (f32[256,128]{0,1:T(8,128)S(1)}, f32[256,128]{0,1:T(8,128)}, u32[]{:S(2)}) copy-start(f32[256,128]{0,1:T(8,128)} %get-tuple-element.80) | copy-start | bytes 393220
  130.0 13.3 %copy-start.20 = (f32[256,128]{0,1:T(8,128)S(1)}, f32[256,128]{0,1:T(8,128)}, u32[]{:S(2)}) copy-start(f32[256,128]{0,1:T(8,128)} %get-tuple-element.81) | copy-start | bytes 393220
  131.7 11.7 %copy-start.23 = (f32[3,2048]{1,0:T(4,128)S(1)}, f32[3,2048]{1,0:T(4,128)}, u32[]{:S(2)}) copy-start(f32[3,2048]{1,0:T(4,128)} %param.11) | copy-start | bytes 73732
  131.7 64.2 %all-to-all-start.1 = ((bf16[32,128,128]{2,0,1:T(8,128)(2,1)}), bf16[32,128,128]{2,0,1:T(8,128)(2,1)S(1)}, u32[]{:S(2)}, u32[]{:S(2)}) async-start(bf16[32,128,128]{2,0,1:T(8,128)(2,1)} %copy.107), calls=%async_computation.1 | async-start | bytes 2097152 | tf_op jit(solution)/shard_map/all_to_all | solution.py:247
  143.4 52.7 %copy-start.4 = (bf16[2048,128]{1,0:T(8,128)(2,1)S(1)}, bf16[2048,128]{1,0:T(8,128)(2,1)}, u32[]{:S(2)}) copy-start(bf16[2048,128]{1,0:T(8,128)(2,1)} %g_ref.1) | copy-start | bytes 1572868
  144.9 51.4 %copy-start.13 = (bf16[2048,128]{1,0:T(8,128)(2,1)S(1)}, bf16[2048,128]{1,0:T(8,128)(2,1)}, u32[]{:S(2)}) copy-start(bf16[2048,128]{1,0:T(8,128)(2,1)} %get-tuple-element.12) | copy-start | bytes 1572868
  144.9 51.4 %copy-start.14 = (bf16[2048,128]{1,0:T(8,128)(2,1)S(1)}, bf16[2048,128]{1,0:T(8,128)(2,1)}, u32[]{:S(2)}) copy-start(bf16[2048,128]{1,0:T(8,128)(2,1)} %get-tuple-element.11) | copy-start | bytes 1572868
  145.2 54.5 %collective-permute-start.2 = (f32[1,4096]{1,0:T(1,128)S(1)}, f32[1,4096]{1,0:T(1,128)S(1)}, u32[]{:S(2)}, u32[]{:S(2)}) collective-permute-start(f32[1,4096]{1,0:T(1,128)S(1)} %get-tuple-element.61), channel_id=1, source_target_pairs={{0,128},{128,256},{256,384},{384,0},{1,129},{129,257},{257,385},{3... | collective-permute-start | bytes 49160 | tf_op jit(solution)/shard_map/ppermute | solution.py:30
  147.1 52.6 %collective-permute-start.3 = (f32[1,4096]{1,0:T(1,128)S(1)}, f32[1,4096]{1,0:T(1,128)S(1)}, u32[]{:S(2)}, u32[]{:S(2)}) collective-permute-start(f32[1,4096]{1,0:T(1,128)S(1)} %get-tuple-element.63), channel_id=1, source_target_pairs={{0,256},{128,384},{256,0},{384,128},{1,257},{129,385},{257,1},{385... | collective-permute-start | bytes 49160 | tf_op jit(solution)/shard_map/ppermute | solution.py:30
  150.2 49.5 %collective-permute-start.4 = (f32[1,4096]{1,0:T(1,128)S(1)}, f32[1,4096]{1,0:T(1,128)S(1)}, u32[]{:S(2)}, u32[]{:S(2)}) collective-permute-start(f32[1,4096]{1,0:T(1,128)S(1)} %get-tuple-element.62), channel_id=1, source_target_pairs={{0,384},{128,0},{256,128},{384,256},{1,385},{129,1},{257,129},{385... | collective-permute-start | bytes 49160 | tf_op jit(solution)/shard_map/ppermute | solution.py:30
  197.1 24.6 %collective-permute-start.1 = (bf16[2048,6]{1,0:T(8,128)(2,1)S(1)}, bf16[2048,6]{1,0:T(8,128)(2,1)S(1)}, u32[]{:S(2)}, u32[]{:S(2)}) collective-permute-start(bf16[2048,6]{1,0:T(8,128)(2,1)S(1)} %pad_maximum_fusion.6), channel_id=1, source_target_pairs={{1,0},{2,1},{3,2},{4,3},{5,4},{6,5},{7,6},{8,7},{9,8},{10,9},{11,1... | collective-permute-start | bytes 73736 | tf_op jit(solution)/shard_map/ppermute | solution.py:18
  200.6 21.5 %copy-start.24 = (f32[1,2048]{1,0:T(1,128)S(1)}, f32[1,2048]{1,0:T(1,128)}, u32[]{:S(2)}) copy-start(f32[1,2048]{1,0:T(1,128)} %get-tuple-element.66) | copy-start | bytes 24580
  222.1 5.2 %copy-start.1 = (bf16[1,16384]{1,0:T(2,128)(2,1)S(1)}, bf16[1,16384]{1,0:T(2,128)(2,1)}, u32[]{:S(2)}) copy-start(bf16[1,16384]{1,0:T(2,128)(2,1)} %param.10) | copy-start | bytes 98308
